TPU v7x, 512 devices: a whole 4x8x8 slice. The times are simulated.
512 devices in a mesh: gx: 8 (over y), gy: 16 (over z_hi, x, core), gz: 4 (over z_lo).
Axes of the slice: x: 4, y: 8, z: 8 (z_hi: 2, z_lo: 4; z = z_hi * 4 + z_lo), core: 2. Of those that a mesh axis runs over, the one named last changes fastest.
Arguments:
- features: bfloat16 [8, 64, 128, 256], P('gx', 'gy', 'gz'), may hold values from -6 to 6
- neighbour_code: int32 [8, 64, 128, 64], P('gx', 'gy', 'gz'), may hold values from 0 to 107, as said below
- distance: float32 [8, 64, 128, 64], P('gx', 'gy', 'gz'), may hold values from 0.8 to 4.8
- w_message: bfloat16 [2, 2048, 256], replicated, may hold values from -0.125 to 0.125
- w_update: bfloat16 [2, 256, 256], replicated, may hold values from -0.375 to 0.375
- norm_gain: float32 [2, 256], replicated, may hold values from 0.1 to 1.9
- w_env: bfloat16 [256, 128], replicated, may hold values from -0.375 to 0.375
- w_out: bfloat16 [3, 256], replicated, may hold values from -0.375 to 0.375
- w_first: bfloat16 [128, 128, 1024], P(('gx', 'gy')), may hold values from -0.5 to 0.5
- w_head: bfloat16 [128, 3, 1024], P(('gx', 'gy')), may hold values from -0.75 to 0.75
- flag_ids: int32 [8, 16, 4, 32], P('gx', 'gy', 'gz'), may hold values from 0 to 127, as said below
- flag_owner: int32 [8, 16, 4, 32, 1], P('gx', 'gy', 'gz'), may hold values from 0 to 127; in each aligned block of 32 rows (0 to 31, 32 to 63, ..., all dimensions but the last counted through in order) at most 2 rows name the same one
- flag_count: int32 [8, 16, 4], P('gx', 'gy', 'gz'), may hold values from 24 to 32, as said below
Outputs:
- forces: float32 [3, 8, 64, 128], P(None, 'gx', 'gy', 'gz')
Inputs may be any that keep to these rules, and one draw needn't show every extreme that they name: `neighbour_code`: an atom's 64 codes are distinct and never name the atom itself (code 13 * 4 + its position along the thickness mod 4). `flag_ids`: the 32 indices of one device are distinct. `flag_owner`: of the 32 rows of one device, live or not, at most 2 name the same specialist, and some device has 2 rows naming one. Rows 0 to flag_count - 1 of a device are live; some device has all 32 live.
All inputs are finite; a program needn't handle non-finite values.
Results may differ from a plain program's by a relative error of at most 0.0085.
Values may be sent and summed in bfloat16 or wider, within the bound.
No kernel may reach another device: no remote copies, remote signals or barrier semaphores. Data moves between devices by JAX's collectives and lax.ppermute only.
A program may use at most 64 MiB of HBM per device.

v0:
```python
import math

import jax
import jax.numpy as jnp
from jax import lax
from jax.sharding import PartitionSpec as P

M = 4
NRB = 8
L = 2


CUTOFF_RADIUS = 5.0
WIDTH_GAMMA = 2.0


def with_halo(cells, sides, width, closed):
    for axis, dim in sides:
        count = lax.axis_size(axis)
        ends = count if closed else count - 1
        head = lax.slice_in_dim(cells, 0, width, axis=dim)
        tail = lax.slice_in_dim(cells, cells.shape[dim] - width, cells.shape[dim], axis=dim)
        cells = jnp.concatenate(
            [
                lax.ppermute(tail, axis, [(i, (i + 1) % count) for i in range(ends)]),
                cells,
                lax.ppermute(head, axis, [((i + 1) % count, i) for i in range(ends)]),
            ],
            axis=dim,
        )
    return cells


def radial(distance):
    cutoff = 0.5 * (jnp.cos(jnp.pi * distance / CUTOFF_RADIUS) + 1.0)
    centres = 0.8 + jnp.arange(NRB).astype(distance.dtype) * (4.0 / (NRB - 1))
    radial_basis = jnp.exp(-WIDTH_GAMMA * (distance[..., None] - centres) ** 2) * cutoff[..., None]
    return (radial_basis.astype(jnp.bfloat16), cutoff)


def neighbour_rows(codes, coord_x, coord_y, coord_z, span_y, span_z):
    offset = codes // M
    within = codes % M
    step_x = offset // 9 - 1
    step_y = offset // 3 % 3 - 1
    step_z = offset % 3 - 1
    return (
        ((coord_x + 1 + step_x) * span_y + (coord_y + 1 + step_y)) * span_z
        + (coord_z // M + 1 + step_z) * M
        + within
    )


def update(state, summed, w_message, w_update, gain):
    message = jnp.dot(summed, w_message, preferred_element_type=jnp.float32)
    active = jax.nn.silu(message).astype(jnp.bfloat16)
    residual = state.astype(jnp.float32) + jnp.dot(
        active, w_update, preferred_element_type=jnp.float32
    )
    inv_rms = lax.rsqrt(jnp.mean(residual * residual, axis=-1, keepdims=True) + 1e-06)
    return (residual * inv_rms * gain).astype(jnp.bfloat16)


def ghosts(values):
    deeper = with_halo(values, (("gz", 2),), M, False)
    return with_halo(deeper, (("gx", 0), ("gy", 1)), 1, True)


def cheap_layer(state, row_index, radial_basis, w_message, w_update, gain):
    feature_width = state.shape[-1]
    flat_rows = ghosts(state).reshape(-1, feature_width)
    atom_count = row_index.shape[0]
    block_size = math.gcd(atom_count, 128)

    def one_block(offset):
        nearby = flat_rows[row_index]
        summed = jnp.einsum(
            "ask,asf->akf", radial_basis, nearby, preferred_element_type=jnp.float32
        )
        return summed.reshape(block_size, -1).astype(jnp.bfloat16)

    starts = jnp.arange(atom_count // block_size, dtype=jnp.int32) * block_size
    summed = lax.map(one_block, starts).reshape(atom_count, -1)
    return update(
        state.reshape(atom_count, feature_width), summed, w_message, w_update, gain
    ).reshape(state.shape)


def specialist(received, live_mark, w_first, w_head):
    sources, item_count = (received.shape[0], received.shape[1])
    env_total = sources * item_count
    block_size = math.gcd(env_total, 16)
    environs = received.reshape(env_total, received.shape[2], received.shape[3])
    flat_live = live_mark.reshape(env_total).astype(jnp.float32) > 0.5

    def run_block(env_piece):
        hidden = jax.nn.silu(
            jnp.einsum("bse,eh->bsh", env_piece, w_first, preferred_element_type=jnp.float32)
        ).astype(jnp.bfloat16)
        pooled = (jnp.sum(hidden, axis=1, dtype=jnp.float32) / hidden.shape[1]).astype(jnp.bfloat16)
        return jnp.einsum("bh,ch->bc", pooled, w_head, preferred_element_type=jnp.float32)

    order = jnp.argsort(jnp.where(flat_live, 0, 1).astype(jnp.int32), stable=True)
    live_total = jnp.sum(flat_live.astype(jnp.int32))
    ordered = environs[order]
    block_count = (live_total + block_size - 1) // block_size

    def step_block(index, gathered):
        offset = index * block_size
        piece = lax.dynamic_slice_in_dim(ordered, offset, block_size, 0)
        return lax.dynamic_update_slice_in_dim(gathered, run_block(piece), offset, 0)

    sorted_results = lax.fori_loop(
        0, block_count, step_block, jnp.zeros((env_total, 3), jnp.float32)
    )
    results = jnp.zeros((env_total, 3), jnp.float32).at[order].set(sorted_results)
    results = results * flat_live[:, None].astype(jnp.float32)
    return results.reshape(sources, item_count, 3)


def per_device(
    features,
    neighbour_code,
    distance,
    w_message,
    w_update,
    norm_gain,
    w_env,
    w_out,
    w_first,
    w_head,
    flag_ids,
    flag_owner,
    flag_count,
):
    cells_x, cells_y, depth, feature_width = features.shape
    atom_count = cells_x * cells_y * depth
    position = jnp.arange(atom_count, dtype=jnp.int32)
    coord_x = position // (cells_y * depth)
    coord_y = position // depth % cells_y
    coord_z = position % depth
    codes = neighbour_code.reshape(atom_count, -1)
    row_index = neighbour_rows(
        codes, coord_x[:, None], coord_y[:, None], coord_z[:, None], cells_y + 2, depth + 2 * M
    )
    radial_basis, cutoff = radial(distance.reshape(atom_count, -1))
    state = features
    for layer_index in range(L):
        state = cheap_layer(
            state,
            row_index,
            radial_basis,
            w_message[layer_index],
            w_update[layer_index],
            norm_gain[layer_index],
        )
    flat_state = state.reshape(atom_count, feature_width)
    projected = jnp.dot(flat_state, w_env, preferred_element_type=jnp.float32).astype(jnp.bfloat16)
    env_width = projected.shape[-1]
    proj_rows = ghosts(projected.reshape(cells_x, cells_y, depth, env_width)).reshape(-1, env_width)
    base_force = jnp.einsum("af,cf->ca", flat_state, w_out, preferred_element_type=jnp.float32)
    local_ids = flag_ids.reshape(-1)
    owner = flag_owner.reshape(-1)
    flag_total = local_ids.shape[0]
    live_rows = jnp.arange(flag_total, dtype=jnp.int32) < flag_count.reshape(())
    nearby = proj_rows[row_index[local_ids]]
    environ = (cutoff[local_ids][..., None] * nearby.astype(jnp.float32)).astype(jnp.bfloat16)
    owner_total = lax.axis_size("gx") * lax.axis_size("gy")
    capacity = max(2, 2 * flag_total // owner_total)
    onehot = (owner[:, None] == jnp.arange(owner_total, dtype=jnp.int32)[None, :]).astype(jnp.int32)
    before = jnp.cumsum(onehot, axis=0) - onehot
    slot_index = jnp.sum(before * onehot, axis=1)
    target = jnp.where(live_rows, owner * capacity + slot_index, owner_total * capacity)
    outgoing = jnp.zeros((owner_total * capacity, environ.shape[1], env_width), jnp.bfloat16)
    outgoing = outgoing.at[target].set(environ, mode="drop")
    slot_live = (
        jnp.zeros((owner_total * capacity,), jnp.bfloat16)
        .at[target]
        .set(jnp.ones((flag_total,), jnp.bfloat16), mode="drop")
    )
    local_first = w_first[0]
    local_head = w_head[0]
    results = specialist(
        lax.all_to_all(
            outgoing.reshape(owner_total, capacity, environ.shape[1], env_width),
            ("gx", "gy"),
            split_axis=0,
            concat_axis=0,
            tiled=True,
        ),
        lax.all_to_all(
            slot_live.reshape(owner_total, capacity),
            ("gx", "gy"),
            split_axis=0,
            concat_axis=0,
            tiled=True,
        ),
        local_first,
        local_head,
    )
    returned = lax.all_to_all(results, ("gx", "gy"), split_axis=0, concat_axis=0, tiled=True)
    returned = returned.reshape(owner_total * capacity, 3)
    correction = returned[jnp.minimum(target, owner_total * capacity - 1)] * live_rows[
        :, None
    ].astype(jnp.float32)
    forces = base_force.at[:, local_ids].add(correction.T)
    return forces.reshape(3, cells_x, cells_y, depth)


def solution(mesh):
    placed = (
        P("gx", "gy", "gz", None),
        P("gx", "gy", "gz", None),
        P("gx", "gy", "gz", None),
        P(),
        P(),
        P(),
        P(),
        P(),
        P(("gx", "gy"), None, None),
        P(("gx", "gy"), None, None),
        P("gx", "gy", "gz", None),
        P("gx", "gy", "gz", None, None),
        P("gx", "gy", "gz"),
    )
    return jax.shard_map(
        per_device, mesh=mesh, in_specs=placed, out_specs=P(None, "gx", "gy", "gz"), check_vma=False
    )
```

profile of v0, /device:TPU:1, one launch (start us, length us, event | category | flops | bytes accessed | tf_op | source)
XLA Modules:
  0.0 395.6 jit_solution(14932897799061744893)
XLA Ops:
  0.8 4.8 %collective-permute-start = (bf16[1,4,4,256]{3,2,1,0:T(4,128)(2,1)S(1)}, bf16[1,4,4,256]{3,2,1,0:T(4,128)(2,1)S(1)}, u32[]{:S(2)}, u32[]{:S(2)}) collective-permute-start(bf16[1,4,4,256]{3,2,1,0:T(4,128)(2,1)S(1)} %get-tuple-element.113), channel_id=1, source_target_pairs={{0,1},{1,2},{2,3},{4,5},{5,6},{6,7},{8,9},{9,10},{10,11},{12,13},{... | collective-permute-start | bytes 24584 | tf_op jit(solution)/shard_map/ppermute | solution.py:25
  13.1 5.1 %collective-permute-start.3 = (bf16[1,4,40,256]{3,2,1,0:T(8,128)(2,1)S(1)}, bf16[1,4,40,256]{3,2,1,0:T(8,128)(2,1)S(1)}, u32[]{:S(2)}, u32[]{:S(2)}) collective-permute-start(bf16[1,4,40,256]{3,2,1,0:T(8,128)(2,1)S(1)} %pad_maximum_fusion.3), channel_id=1, source_target_pairs={{64,0},{128,64},{192,128},{256,192},{320,256},{384,320},{448,384},... | collective-permute-start | bytes 245768 | tf_op jit(solution)/shard_map/ppermute | solution.py:27
  20.8 3.8 collective-permute-done.2
  25.3 5.4 %collective-permute-start.4 = (bf16[3,1,40,256]{3,2,1,0:T(8,128)(2,1)S(1)}, bf16[3,1,40,256]{3,2,1,0:T(8,128)(2,1)S(1)}, u32[]{:S(2)}, u32[]{:S(2)}) collective-permute-start(bf16[3,1,40,256]{3,2,1,0:T(8,128)(2,1)S(1)} %get-tuple-element.107), channel_id=1, source_target_pairs={{0,4},{4,8},{8,12},{12,16},{16,20},{20,24},{24,28},{28,32},{32,36}... | collective-permute-start | bytes 184328 | tf_op jit(solution)/shard_map/ppermute | solution.py:25
  32.7 3.9 collective-permute-done.5
  37.5 33.0 %gather_fusion = bf16[8192,256]{1,0:T(8,128)(2,1)} fusion(bf16[720,256]{1,0:T(8,128)(2,1)S(1)} %bitcast.136, s32[8192]{0:T(1024)S(1)} %broadcast_clamp_fusion), kind=kCustom, calls=%fused_computation | custom fusion | bytes 8421376 | tf_op jit(solution)/shard_map/while/body/eval_jaxpr/gather | solution.py:76
  70.5 3.0 convolution_convert_fusion.1
  75.5 4.6 %collective-permute-start.6 = (bf16[1,4,4,256]{3,2,1,0:T(4,128)(2,1)S(1)}, bf16[1,4,4,256]{3,2,1,0:T(4,128)(2,1)S(1)}, u32[]{:S(2)}, u32[]{:S(2)}) collective-permute-start(bf16[1,4,4,256]{3,2,1,0:T(4,128)(2,1)S(1)} %get-tuple-element.111), channel_id=1, source_target_pairs={{0,1},{1,2},{2,3},{4,5},{5,6},{6,7},{8,9},{9,10},{10,11},{12,13},{... | collective-permute-start | bytes 24584 | tf_op jit(solution)/shard_map/ppermute | solution.py:25
  83.0 19.6 %all-to-all-start = ((bf16[128,1,2]{2,1,0:T(2,128)(2,1)}), bf16[128,1,2]{2,1,0:T(2,128)(2,1)S(1)}, u32[]{:S(2)}, u32[]{:S(2)}) async-start(bf16[128,1,2]{2,1,0:T(2,128)(2,1)} %all_to_all.16), calls=%async_computation | async-start | bytes 131072 | tf_op jit(solution)/shard_map/all_to_all | solution.py:191
  102.7 5.1 %collective-permute-start.9 = (bf16[1,4,40,256]{3,2,1,0:T(8,128)(2,1)S(1)}, bf16[1,4,40,256]{3,2,1,0:T(8,128)(2,1)S(1)}, u32[]{:S(2)}, u32[]{:S(2)}) collective-permute-start(bf16[1,4,40,256]{3,2,1,0:T(8,128)(2,1)S(1)} %pad_maximum_fusion.4), channel_id=1, source_target_pairs={{64,0},{128,64},{192,128},{256,192},{320,256},{384,320},{448,384},... | collective-permute-start | bytes 245768 | tf_op jit(solution)/shard_map/ppermute | solution.py:27
  110.0 4.5 %collective-permute-done.8 = bf16[1,4,40,256]{3,2,1,0:T(8,128)(2,1)S(1)} collective-permute-done((bf16[1,4,40,256]{3,2,1,0:T(8,128)(2,1)S(1)}, bf16[1,4,40,256]{3,2,1,0:T(8,128)(2,1)S(1)}, u32[]{:S(2)}, u32[]{:S(2)}) %collective-permute-start.8) | collective-permute-done | bytes 81952 | tf_op jit(solution)/shard_map/ppermute | solution.py:25
  114.6 4.5 %collective-permute-start.10 = (bf16[3,1,40,256]{3,2,1,0:T(8,128)(2,1)S(1)}, bf16[3,1,40,256]{3,2,1,0:T(8,128)(2,1)S(1)}, u32[]{:S(2)}, u32[]{:S(2)}) collective-permute-start(bf16[3,1,40,256]{3,2,1,0:T(8,128)(2,1)S(1)} %get-tuple-element.105), channel_id=1, source_target_pairs={{0,4},{4,8},{8,12},{12,16},{16,20},{20,24},{24,28},{28,32},{32,36}... | collective-permute-start | bytes 184328 | tf_op jit(solution)/shard_map/ppermute | solution.py:25
  121.1 3.9 collective-permute-done.11
  125.0 33.0 %gather_fusion.1 = bf16[8192,256]{1,0:T(8,128)(2,1)} fusion(bf16[720,256]{1,0:T(8,128)(2,1)S(1)} %bitcast.135, s32[8192]{0:T(1024)S(1)} %broadcast_clamp_fusion), kind=kCustom, calls=%fused_computation.1 | custom fusion | bytes 8421376 | tf_op jit(solution)/shard_map/while/body/eval_jaxpr/gather | solution.py:76
  158.0 2.9 convolution_convert_fusion
  163.1 4.0 %collective-permute-start.12 = (bf16[1,4,4,128]{3,2,1,0:T(4,128)(2,1)S(1)}, bf16[1,4,4,128]{3,2,1,0:T(4,128)(2,1)S(1)}, u32[]{:S(2)}, u32[]{:S(2)}) collective-permute-start(bf16[1,4,4,128]{3,2,1,0:T(4,128)(2,1)S(1)} %get-tuple-element.115), channel_id=1, source_target_pairs={{0,1},{1,2},{2,3},{4,5},{5,6},{6,7},{8,9},{9,10},{10,11},{12,13},{... | collective-permute-start | bytes 12296 | tf_op jit(solution)/shard_map/ppermute | solution.py:25
  168.9 2.5 collective-permute-done.13
  173.4 3.4 collective-permute-start.14
  176.8 2.5 collective-permute-done.14
  179.3 4.3 %collective-permute-start.16 = (bf16[3,1,40,128]{3,2,1,0:T(8,128)(2,1)S(1)}, bf16[3,1,40,128]{3,2,1,0:T(8,128)(2,1)S(1)}, u32[]{:S(2)}, u32[]{:S(2)}) collective-permute-start(bf16[3,1,40,128]{3,2,1,0:T(8,128)(2,1)S(1)} %get-tuple-element.109), channel_id=1, source_target_pairs={{0,4},{4,8},{8,12},{12,16},{16,20},{20,24},{24,28},{28,32},{32,36}... | collective-permute-start | bytes 92168 | tf_op jit(solution)/shard_map/ppermute | solution.py:25
  183.6 6.9 %collective-permute-start.17 = (bf16[3,1,40,128]{3,2,1,0:T(8,128)(2,1)S(1)}, bf16[3,1,40,128]{3,2,1,0:T(8,128)(2,1)S(1)}, u32[]{:S(2)}, u32[]{:S(2)}) collective-permute-start(bf16[3,1,40,128]{3,2,1,0:T(8,128)(2,1)S(1)} %get-tuple-element.110), channel_id=1, source_target_pairs={{4,0},{8,4},{12,8},{16,12},{20,16},{24,20},{28,24},{32,28},{36,32}... | collective-permute-start | bytes 92168 | tf_op jit(solution)/shard_map/ppermute | solution.py:27
  191.4 6.2 %gather_fusion.4 = bf16[2048,128]{1,0:T(8,128)(2,1)S(1)} fusion(bf16[720,128]{1,0:T(8,128)(2,1)S(1)} %bitcast.137, s32[2048]{0:T(1024)S(1)} %broadcast_clamp_fusion.1), kind=kCustom, calls=%fused_computation.4 | custom fusion | bytes 1056768 | tf_op jit(solution)/shard_map/gather | solution.py:166
  197.9 3.0 broadcast_in_dim.61
  200.9 4.3 %scatter_fusion = bf16[256,64,128]{2,1,0:T(8,128)(2,1)} fusion(bf16[256,64,128]{2,1,0:T(8,128)(2,1)} %broadcast_in_dim.61, s32[32]{0:T(128)S(1)} %fusion.71, bf16[32,64,128]{2,1,0:T(8,128)(2,1)S(1)} %fusion.6), kind=kCustom, calls=%fused_computation.8 | custom fusion | bytes 1572992 | tf_op jit(solution)/shard_map/scatter | solution.py:175
  205.2 21.6 %all-to-all-start.1 = ((bf16[128,2,64,128]{3,2,1,0:T(8,128)(2,1)}), bf16[128,2,64,128]{3,2,1,0:T(8,128)(2,1)}, u32[]{:S(2)}, u32[]{:S(2)}) async-start(bf16[128,2,64,128]{3,2,1,0:T(8,128)(2,1)} %bitcast.138), calls=%async_computation.1 | async-start | bytes 8388608 | tf_op jit(solution)/shard_map/all_to_all | solution.py:184
  229.0 3.2 sort.17
  232.1 93.8 %all-to-all-done.1 = bf16[128,2,64,128]{3,2,1,0:T(8,128)(2,1)} async-done(((bf16[128,2,64,128]{3,2,1,0:T(8,128)(2,1)}), bf16[128,2,64,128]{3,2,1,0:T(8,128)(2,1)}, u32[]{:S(2)}, u32[]{:S(2)}) %all-to-all-start.1) | async-done | bytes 4194336 | tf_op jit(solution)/shard_map/all_to_all | solution.py:184
  325.9 5.3 %gather_fusion.5 = bf16[256,64,128]{2,1,0:T(8,128)(2,1)} fusion(bf16[256,64,128]{2,1,0:T(8,128)(2,1)} %bitcast.29, s32[1024]{0:T(1024)S(1)} %pad_clamp_fusion.1), kind=kCustom, calls=%fused_computation.5 | custom fusion | bytes 8389632 | tf_op jit(solution)/shard_map/gather | solution.py:105
  331.2 5.1 %while.2 = (s32[]{:T(128)}, f32[256,3]{0,1:T(4,128)S(1)}, s32[]{:T(128)}, bf16[256,64,128]{2,1,0:T(8,128)(2,1)}, bf16[128,1024]{1,0:T(8,128)(2,1)S(1)}, /*index=...) while((s32[]{:T(128)}, f32[256,3]{0,1:T(4,128)S(1)}, s32[]{:T(128)}, ...), condition=%wide.region_10.11_spmd, body=%wide.region_8.10_spmd.sunk | while | flops 275890176 | bytes 662235 | solution.py:113
  333.7 2.3 convert_reduce_fusion.4
  338.6 39.6 %all-to-all-start.2 = ((f32[128,2,3]{2,1,0:T(2,128)}), f32[128,2,3]{2,1,0:T(2,128)S(1)}, u32[]{:S(2)}, u32[]{:S(2)}) async-start(f32[128,2,3]{2,1,0:T(2,128)} %bitcast.32), calls=%async_computation.2 | async-start | bytes 262144 | tf_op jit(solution)/shard_map/all_to_all | solution.py:201
  378.5 15.6 %all-to-all-done.2 = f32[128,2,3]{2,1,0:T(2,128)S(1)} async-done(((f32[128,2,3]{2,1,0:T(2,128)}), f32[128,2,3]{2,1,0:T(2,128)S(1)}, u32[]{:S(2)}, u32[]{:S(2)}) %all-to-all-start.2) | async-done | bytes 3104 | tf_op jit(solution)/shard_map/all_to_all | solution.py:201
  (108 shorter events, 38.3 us)
Async XLA Ops:
  0.0 162.8 %copy-start = (bf16[256,128]{1,0:T(8,128)(2,1)S(1)}, bf16[256,128]{1,0:T(8,128)(2,1)}, u32[]{:S(2)}) copy-start(bf16[256,128]{1,0:T(8,128)(2,1)} %param.21) | copy-start | bytes 196612
  0.8 11.4 %collective-permute-start = (bf16[1,4,4,256]{3,2,1,0:T(4,128)(2,1)S(1)}, bf16[1,4,4,256]{3,2,1,0:T(4,128)(2,1)S(1)}, u32[]{:S(2)}, u32[]{:S(2)}) collective-permute-start(bf16[1,4,4,256]{3,2,1,0:T(4,128)(2,1)S(1)} %get-tuple-element.113), channel_id=1, source_target_pairs={{0,1},{1,2},{2,3},{4,5},{5,6},{6,7},{8,9},{9,10},{10,11},{12,13},{... | collective-permute-start | bytes 24584 | tf_op jit(solution)/shard_map/ppermute | solution.py:25
  5.6 6.6 %collective-permute-start.1 = (bf16[1,4,4,256]{3,2,1,0:T(4,128)(2,1)S(1)}, bf16[1,4,4,256]{3,2,1,0:T(4,128)(2,1)S(1)}, u32[]{:S(2)}, u32[]{:S(2)}) collective-permute-start(bf16[1,4,4,256]{3,2,1,0:T(4,128)(2,1)S(1)} %get-tuple-element.114), channel_id=1, source_target_pairs={{1,0},{2,1},{3,2},{5,4},{6,5},{7,6},{9,8},{10,9},{11,10},{13,12},{... | collective-permute-start | bytes 24584 | tf_op jit(solution)/shard_map/ppermute | solution.py:27
  13.1 7.7 %collective-permute-start.3 = (bf16[1,4,40,256]{3,2,1,0:T(8,128)(2,1)S(1)}, bf16[1,4,40,256]{3,2,1,0:T(8,128)(2,1)S(1)}, u32[]{:S(2)}, u32[]{:S(2)}) collective-permute-start(bf16[1,4,40,256]{3,2,1,0:T(8,128)(2,1)S(1)} %pad_maximum_fusion.3), channel_id=1, source_target_pairs={{64,0},{128,64},{192,128},{256,192},{320,256},{384,320},{448,384},... | collective-permute-start | bytes 245768 | tf_op jit(solution)/shard_map/ppermute | solution.py:27
  18.2 6.4 %collective-permute-start.2 = (bf16[1,4,40,256]{3,2,1,0:T(8,128)(2,1)S(1)}, bf16[1,4,40,256]{3,2,1,0:T(8,128)(2,1)S(1)}, u32[]{:S(2)}, u32[]{:S(2)}) collective-permute-start(bf16[1,4,40,256]{3,2,1,0:T(8,128)(2,1)S(1)} %pad_maximum_fusion.3), channel_id=1, source_target_pairs={{0,64},{64,128},{128,192},{192,256},{256,320},{320,384},{384,448},... | collective-permute-start | bytes 245768 | tf_op jit(solution)/shard_map/ppermute | solution.py:25
  25.3 7.3 %collective-permute-start.4 = (bf16[3,1,40,256]{3,2,1,0:T(8,128)(2,1)S(1)}, bf16[3,1,40,256]{3,2,1,0:T(8,128)(2,1)S(1)}, u32[]{:S(2)}, u32[]{:S(2)}) collective-permute-start(bf16[3,1,40,256]{3,2,1,0:T(8,128)(2,1)S(1)} %get-tuple-element.107), channel_id=1, source_target_pairs={{0,4},{4,8},{8,12},{12,16},{16,20},{20,24},{24,28},{28,32},{32,36}... | collective-permute-start | bytes 184328 | tf_op jit(solution)/shard_map/ppermute | solution.py:25
  30.7 5.8 %collective-permute-start.5 = (bf16[3,1,40,256]{3,2,1,0:T(8,128)(2,1)S(1)}, bf16[3,1,40,256]{3,2,1,0:T(8,128)(2,1)S(1)}, u32[]{:S(2)}, u32[]{:S(2)}) collective-permute-start(bf16[3,1,40,256]{3,2,1,0:T(8,128)(2,1)S(1)} %get-tuple-element.108), channel_id=1, source_target_pairs={{4,0},{8,4},{12,8},{16,12},{20,16},{24,20},{28,24},{32,28},{36,32}... | collective-permute-start | bytes 184328 | tf_op jit(solution)/shard_map/ppermute | solution.py:27
  37.5 33.0 %copy-start.2 = (f32[1,4,32,64]{3,2,1,0:T(8,128)S(1)}, f32[1,4,32,64]{3,2,1,0:T(8,128)}, u32[]{:S(2)}) copy-start(f32[1,4,32,64]{3,2,1,0:T(8,128)} %param.17) | copy-start | bytes 98308
  70.4 3.1 copy-start.1
  70.4 3.1 copy-start.6
  70.5 39.3 %copy-start.3 = (s32[1,4,32,64]{3,2,1,0:T(8,128)S(1)}, s32[1,4,32,64]{3,2,1,0:T(8,128)}, u32[]{:S(2)}) copy-start(s32[1,4,32,64]{3,2,1,0:T(8,128)} %param.16) | copy-start | bytes 98308
  70.5 50.6 %copy-start.8 = (s32[1,1,1,32]{3,2,1,0:T(1,128)S(1)}, s32[1,1,1,32]{3,2,1,0:T(1,128)}, u32[]{:S(2)}) copy-start(s32[1,1,1,32]{3,2,1,0:T(1,128)} %param.25) | copy-start | bytes 388
  75.5 27.1 %collective-permute-start.6 = (bf16[1,4,4,256]{3,2,1,0:T(4,128)(2,1)S(1)}, bf16[1,4,4,256]{3,2,1,0:T(4,128)(2,1)S(1)}, u32[]{:S(2)}, u32[]{:S(2)}) collective-permute-start(bf16[1,4,4,256]{3,2,1,0:T(4,128)(2,1)S(1)} %get-tuple-element.111), channel_id=1, source_target_pairs={{0,1},{1,2},{2,3},{4,5},{5,6},{6,7},{8,9},{9,10},{10,11},{12,13},{... | collective-permute-start | bytes 24584 | tf_op jit(solution)/shard_map/ppermute | solution.py:25
  80.2 22.5 %collective-permute-start.7 = (bf16[1,4,4,256]{3,2,1,0:T(4,128)(2,1)S(1)}, bf16[1,4,4,256]{3,2,1,0:T(4,128)(2,1)S(1)}, u32[]{:S(2)}, u32[]{:S(2)}) collective-permute-start(bf16[1,4,4,256]{3,2,1,0:T(4,128)(2,1)S(1)} %get-tuple-element.112), channel_id=1, source_target_pairs={{1,0},{2,1},{3,2},{5,4},{6,5},{7,6},{9,8},{10,9},{11,10},{13,12},{... | collective-permute-start | bytes 24584 | tf_op jit(solution)/shard_map/ppermute | solution.py:27
  83.0 122.2 %all-to-all-start = ((bf16[128,1,2]{2,1,0:T(2,128)(2,1)}), bf16[128,1,2]{2,1,0:T(2,128)(2,1)S(1)}, u32[]{:S(2)}, u32[]{:S(2)}) async-start(bf16[128,1,2]{2,1,0:T(2,128)(2,1)} %all_to_all.16), calls=%async_computation | async-start | bytes 131072 | tf_op jit(solution)/shard_map/all_to_all | solution.py:191
  102.7 7.3 %collective-permute-start.9 = (bf16[1,4,40,256]{3,2,1,0:T(8,128)(2,1)S(1)}, bf16[1,4,40,256]{3,2,1,0:T(8,128)(2,1)S(1)}, u32[]{:S(2)}, u32[]{:S(2)}) collective-permute-start(bf16[1,4,40,256]{3,2,1,0:T(8,128)(2,1)S(1)} %pad_maximum_fusion.4), channel_id=1, source_target_pairs={{64,0},{128,64},{192,128},{256,192},{320,256},{384,320},{448,384},... | collective-permute-start | bytes 245768 | tf_op jit(solution)/shard_map/ppermute | solution.py:27
  107.9 6.7 %collective-permute-start.8 = (bf16[1,4,40,256]{3,2,1,0:T(8,128)(2,1)S(1)}, bf16[1,4,40,256]{3,2,1,0:T(8,128)(2,1)S(1)}, u32[]{:S(2)}, u32[]{:S(2)}) collective-permute-start(bf16[1,4,40,256]{3,2,1,0:T(8,128)(2,1)S(1)} %pad_maximum_fusion.4), channel_id=1, source_target_pairs={{0,64},{64,128},{128,192},{192,256},{256,320},{320,384},{384,448},... | collective-permute-start | bytes 245768 | tf_op jit(solution)/shard_map/ppermute | solution.py:25
  114.6 6.5 %collective-permute-start.10 = (bf16[3,1,40,256]{3,2,1,0:T(8,128)(2,1)S(1)}, bf16[3,1,40,256]{3,2,1,0:T(8,128)(2,1)S(1)}, u32[]{:S(2)}, u32[]{:S(2)}) collective-permute-start(bf16[3,1,40,256]{3,2,1,0:T(8,128)(2,1)S(1)} %get-tuple-element.105), channel_id=1, source_target_pairs={{0,4},{4,8},{8,12},{12,16},{16,20},{20,24},{24,28},{28,32},{32,36}... | collective-permute-start | bytes 184328 | tf_op jit(solution)/shard_map/ppermute | solution.py:25
  119.1 5.8 %collective-permute-start.11 = (bf16[3,1,40,256]{3,2,1,0:T(8,128)(2,1)S(1)}, bf16[3,1,40,256]{3,2,1,0:T(8,128)(2,1)S(1)}, u32[]{:S(2)}, u32[]{:S(2)}) collective-permute-start(bf16[3,1,40,256]{3,2,1,0:T(8,128)(2,1)S(1)} %get-tuple-element.106), channel_id=1, source_target_pairs={{4,0},{8,4},{12,8},{16,12},{20,16},{24,20},{28,24},{32,28},{36,32}... | collective-permute-start | bytes 184328 | tf_op jit(solution)/shard_map/ppermute | solution.py:27
  163.1 5.9 %collective-permute-start.12 = (bf16[1,4,4,128]{3,2,1,0:T(4,128)(2,1)S(1)}, bf16[1,4,4,128]{3,2,1,0:T(4,128)(2,1)S(1)}, u32[]{:S(2)}, u32[]{:S(2)}) collective-permute-start(bf16[1,4,4,128]{3,2,1,0:T(4,128)(2,1)S(1)} %get-tuple-element.115), channel_id=1, source_target_pairs={{0,1},{1,2},{2,3},{4,5},{5,6},{6,7},{8,9},{9,10},{10,11},{12,13},{... | collective-permute-start | bytes 12296 | tf_op jit(solution)/shard_map/ppermute | solution.py:25
  167.1 4.4 %collective-permute-start.13 = (bf16[1,4,4,128]{3,2,1,0:T(4,128)(2,1)S(1)}, bf16[1,4,4,128]{3,2,1,0:T(4,128)(2,1)S(1)}, u32[]{:S(2)}, u32[]{:S(2)}) collective-permute-start(bf16[1,4,4,128]{3,2,1,0:T(4,128)(2,1)S(1)} %get-tuple-element.116), channel_id=1, source_target_pairs={{1,0},{2,1},{3,2},{5,4},{6,5},{7,6},{9,8},{10,9},{11,10},{13,12},{... | collective-permute-start | bytes 12296 | tf_op jit(solution)/shard_map/ppermute | solution.py:27
  171.4 5.4 %collective-permute-start.15 = (bf16[1,4,40,128]{3,2,1,0:T(8,128)(2,1)S(1)}, bf16[1,4,40,128]{3,2,1,0:T(8,128)(2,1)S(1)}, u32[]{:S(2)}, u32[]{:S(2)}) collective-permute-start(bf16[1,4,40,128]{3,2,1,0:T(8,128)(2,1)S(1)} %pad_maximum_fusion.15), channel_id=1, source_target_pairs={{64,0},{128,64},{192,128},{256,192},{320,256},{384,320},{448,384},... | collective-permute-start | bytes 122888 | tf_op jit(solution)/shard_map/ppermute | solution.py:27
  173.4 6.0 %collective-permute-start.14 = (bf16[1,4,40,128]{3,2,1,0:T(8,128)(2,1)S(1)}, bf16[1,4,40,128]{3,2,1,0:T(8,128)(2,1)S(1)}, u32[]{:S(2)}, u32[]{:S(2)}) collective-permute-start(bf16[1,4,40,128]{3,2,1,0:T(8,128)(2,1)S(1)} %pad_maximum_fusion.15), channel_id=1, source_target_pairs={{0,64},{64,128},{128,192},{192,256},{256,320},{320,384},{384,448},... | collective-permute-start | bytes 122888 | tf_op jit(solution)/shard_map/ppermute | solution.py:25
  179.3 11.7 %collective-permute-start.16 = (bf16[3,1,40,128]{3,2,1,0:T(8,128)(2,1)S(1)}, bf16[3,1,40,128]{3,2,1,0:T(8,128)(2,1)S(1)}, u32[]{:S(2)}, u32[]{:S(2)}) collective-permute-start(bf16[3,1,40,128]{3,2,1,0:T(8,128)(2,1)S(1)} %get-tuple-element.109), channel_id=1, source_target_pairs={{0,4},{4,8},{8,12},{12,16},{16,20},{20,24},{24,28},{28,32},{32,36}... | collective-permute-start | bytes 92168 | tf_op jit(solution)/shard_map/ppermute | solution.py:25
  183.6 7.7 %collective-permute-start.17 = (bf16[3,1,40,128]{3,2,1,0:T(8,128)(2,1)S(1)}, bf16[3,1,40,128]{3,2,1,0:T(8,128)(2,1)S(1)}, u32[]{:S(2)}, u32[]{:S(2)}) collective-permute-start(bf16[3,1,40,128]{3,2,1,0:T(8,128)(2,1)S(1)} %get-tuple-element.110), channel_id=1, source_target_pairs={{4,0},{8,4},{12,8},{16,12},{20,16},{24,20},{28,24},{32,28},{36,32}... | collective-permute-start | bytes 92168 | tf_op jit(solution)/shard_map/ppermute | solution.py:27
  205.2 120.7 %all-to-all-start.1 = ((bf16[128,2,64,128]{3,2,1,0:T(8,128)(2,1)}), bf16[128,2,64,128]{3,2,1,0:T(8,128)(2,1)}, u32[]{:S(2)}, u32[]{:S(2)}) async-start(bf16[128,2,64,128]{3,2,1,0:T(8,128)(2,1)} %bitcast.138), calls=%async_computation.1 | async-start | bytes 8388608 | tf_op jit(solution)/shard_map/all_to_all | solution.py:184
  325.9 5.3 %copy-start.4 = (bf16[1,3,1024]{2,1,0:T(4,128)(2,1)S(1)}, bf16[1,3,1024]{2,1,0:T(4,128)(2,1)}, u32[]{:S(2)}) copy-start(bf16[1,3,1024]{2,1,0:T(4,128)(2,1)} %param.24) | copy-start | bytes 18436
  325.9 5.3 %copy-start.7 = (bf16[1,128,1024]{2,1,0:T(8,128)(2,1)S(1)}, bf16[1,128,1024]{2,1,0:T(8,128)(2,1)}, u32[]{:S(2)}) copy-start(bf16[1,128,1024]{2,1,0:T(8,128)(2,1)} %param.23) | copy-start | bytes 786436
  331.2 47.0 %copy-start.5 = (bf16[3,256]{1,0:T(4,128)(2,1)S(1)}, bf16[3,256]{1,0:T(4,128)(2,1)}, u32[]{:S(2)}) copy-start(bf16[3,256]{1,0:T(4,128)(2,1)} %param.22) | copy-start | bytes 4612
  338.6 55.5 %all-to-all-start.2 = ((f32[128,2,3]{2,1,0:T(2,128)}), f32[128,2,3]{2,1,0:T(2,128)S(1)}, u32[]{:S(2)}, u32[]{:S(2)}) async-start(f32[128,2,3]{2,1,0:T(2,128)} %bitcast.32), calls=%async_computation.2 | async-start | bytes 262144 | tf_op jit(solution)/shard_map/all_to_all | solution.py:201
where the time goes:
time: 397 us; the launch traced here: 396 us
  starting transfers between devices  142 us (36%)
  waiting for transfers between devices  131 us (33%)
  local copies, waits for them, and re-layouts  93 us (23%)
  matrix products  14.7 us (4%)
  other arithmetic  13 us (3%)
    all_to_all x1, waiting for transfers between devices, per_device(): lax.all_to_all(outgoing.reshape(owner_total, capacity, environ.shape[1],...  93.8 us
    gather x2, local copies, waits for them, and re-layouts, one_block(): nearby = flat_rows[row_index]  65.9 us
    all_to_all x1, starting transfers between devices, per_device(): lax.all_to_all(results, ('gx', 'gy'), split_axis=0, concat_axis=0, tiled=...  39.6 us
    ppermute x9, starting transfers between devices, with_halo(): lax.ppermute(tail, axis, [(i, (i + 1) % count) for i in range(ends)])  34.8 us
    ppermute x9, starting transfers between devices, with_halo(): lax.ppermute(head, axis, [((i + 1) % count, i) for i in range(ends)])  26.7 us
    all_to_all x1, starting transfers between devices, per_device(): lax.all_to_all(outgoing.reshape(owner_total, capacity, environ.shape[1],...  21.6 us
    all_to_all x1, starting transfers between devices, per_device(): lax.all_to_all(slot_live.reshape(owner_total, capacity), ('gx', 'gy'), sp...  19.6 us
    all_to_all x1, waiting for transfers between devices, per_device(): lax.all_to_all(results, ('gx', 'gy'), split_axis=0, concat_axis=0, tiled=...  15.6 us
  transfers between devices with their start and end apart: 21, of which 9 were waited for; matrix products, arithmetic and copies ran while one was open for 16% of the time, Pallas kernels for 0%

commit v1 on v0

--- a/solution.py
+++ b/solution.py
@@ -66,32 +66,46 @@
     return with_halo(deeper, (("gx", 0), ("gy", 1)), 1, True)
 
 
-def cheap_layer(state, row_index, radial_basis, w_message, w_update, gain):
-    feature_width = state.shape[-1]
-    flat_rows = ghosts(state).reshape(-1, feature_width)
-    atom_count = row_index.shape[0]
-    block_size = math.gcd(atom_count, 128)
-
-    def one_block(offset):
-        nearby = flat_rows[row_index]
-        summed = jnp.einsum(
-            "ask,asf->akf", radial_basis, nearby, preferred_element_type=jnp.float32
-        )
-        return summed.reshape(block_size, -1).astype(jnp.bfloat16)
-
-    starts = jnp.arange(atom_count // block_size, dtype=jnp.int32) * block_size
-    summed = lax.map(one_block, starts).reshape(atom_count, -1)
+def candidates(padded, cells_x, cells_y, cells_z):
+    feature_width = padded.shape[-1]
+    pieces = []
+    for step_x in range(3):
+        for step_y in range(3):
+            for step_z in range(3):
+                piece = padded[
+                    step_x : step_x + cells_x,
+                    step_y : step_y + cells_y,
+                    step_z * M : step_z * M + cells_z * M,
+                ]
+                pieces.append(piece.reshape(cells_x, cells_y, cells_z, M, feature_width))
+    stacked = jnp.stack(pieces, axis=3)
+    return stacked.reshape(cells_x * cells_y * cells_z, 27 * M, feature_width)
+
+
+def cheap_layer(state, weights, w_message, w_update, gain):
+    cells_x, cells_y, depth, feature_width = state.shape
+    cells_z = depth // M
+    cell_count = cells_x * cells_y * cells_z
+    atom_count = cell_count * M
+    nearby = candidates(ghosts(state), cells_x, cells_y, cells_z)
+    summed = jnp.einsum(
+        "bmkc,bcf->bmkf",
+        weights.reshape(cell_count, M, NRB, 27 * M),
+        nearby,
+        preferred_element_type=jnp.float32,
+    )
+    summed = summed.reshape(atom_count, NRB * feature_width).astype(jnp.bfloat16)
     return update(
         state.reshape(atom_count, feature_width), summed, w_message, w_update, gain
     ).reshape(state.shape)
 
 
-def specialist(received, live_mark, w_first, w_head):
+def specialist(received, w_first, w_head):
     sources, item_count = (received.shape[0], received.shape[1])
     env_total = sources * item_count
     block_size = math.gcd(env_total, 16)
     environs = received.reshape(env_total, received.shape[2], received.shape[3])
-    flat_live = live_mark.reshape(env_total).astype(jnp.float32) > 0.5
+    flat_live = jnp.any(environs != 0, axis=(1, 2))
 
     def run_block(env_piece):
         hidden = jax.nn.silu(
@@ -134,22 +148,20 @@
     flag_count,
 ):
     cells_x, cells_y, depth, feature_width = features.shape
+    cells_z = depth // M
     atom_count = cells_x * cells_y * depth
-    position = jnp.arange(atom_count, dtype=jnp.int32)
-    coord_x = position // (cells_y * depth)
-    coord_y = position // depth % cells_y
-    coord_z = position % depth
     codes = neighbour_code.reshape(atom_count, -1)
-    row_index = neighbour_rows(
-        codes, coord_x[:, None], coord_y[:, None], coord_z[:, None], cells_y + 2, depth + 2 * M
-    )
     radial_basis, cutoff = radial(distance.reshape(atom_count, -1))
+    code_range = jnp.arange(27 * M, dtype=jnp.int32)
+    onehot = (codes[:, :, None] == code_range[None, None, :]).astype(jnp.bfloat16)
+    weights = jnp.einsum(
+        "ask,asc->akc", radial_basis, onehot, preferred_element_type=jnp.float32
+    ).astype(jnp.bfloat16)
     state = features
     for layer_index in range(L):
         state = cheap_layer(
             state,
-            row_index,
-            radial_basis,
+            weights,
             w_message[layer_index],
             w_update[layer_index],
             norm_gain[layer_index],
@@ -157,39 +169,39 @@
     flat_state = state.reshape(atom_count, feature_width)
     projected = jnp.dot(flat_state, w_env, preferred_element_type=jnp.float32).astype(jnp.bfloat16)
     env_width = projected.shape[-1]
-    proj_rows = ghosts(projected.reshape(cells_x, cells_y, depth, env_width)).reshape(-1, env_width)
+    proj_near = candidates(
+        ghosts(projected.reshape(cells_x, cells_y, depth, env_width)), cells_x, cells_y, cells_z
+    )
     base_force = jnp.einsum("af,cf->ca", flat_state, w_out, preferred_element_type=jnp.float32)
     local_ids = flag_ids.reshape(-1)
     owner = flag_owner.reshape(-1)
     flag_total = local_ids.shape[0]
     live_rows = jnp.arange(flag_total, dtype=jnp.int32) < flag_count.reshape(())
-    nearby = proj_rows[row_index[local_ids]]
-    environ = (cutoff[local_ids][..., None] * nearby.astype(jnp.float32)).astype(jnp.bfloat16)
+    picked = jnp.einsum(
+        "rsc,rce->rse",
+        onehot[local_ids],
+        proj_near[local_ids // M],
+        preferred_element_type=jnp.float32,
+    )
+    environ = (cutoff[local_ids][..., None] * picked).astype(jnp.bfloat16)
+    slots = environ.shape[1]
     owner_total = lax.axis_size("gx") * lax.axis_size("gy")
     capacity = max(2, 2 * flag_total // owner_total)
-    onehot = (owner[:, None] == jnp.arange(owner_total, dtype=jnp.int32)[None, :]).astype(jnp.int32)
-    before = jnp.cumsum(onehot, axis=0) - onehot
-    slot_index = jnp.sum(before * onehot, axis=1)
+    same = (owner[:, None] == jnp.arange(owner_total, dtype=jnp.int32)[None, :]).astype(jnp.int32)
+    before = jnp.cumsum(same, axis=0) - same
+    slot_index = jnp.sum(before * same, axis=1)
     target = jnp.where(live_rows, owner * capacity + slot_index, owner_total * capacity)
-    outgoing = jnp.zeros((owner_total * capacity, environ.shape[1], env_width), jnp.bfloat16)
-    outgoing = outgoing.at[target].set(environ, mode="drop")
-    slot_live = (
-        jnp.zeros((owner_total * capacity,), jnp.bfloat16)
-        .at[target]
-        .set(jnp.ones((flag_total,), jnp.bfloat16), mode="drop")
-    )
+    placing = (
+        jnp.arange(owner_total * capacity, dtype=jnp.int32)[:, None] == target[None, :]
+    ).astype(jnp.bfloat16)
+    outgoing = jnp.dot(
+        placing, environ.reshape(flag_total, slots * env_width), preferred_element_type=jnp.float32
+    ).astype(jnp.bfloat16)
     local_first = w_first[0]
     local_head = w_head[0]
     results = specialist(
         lax.all_to_all(
-            outgoing.reshape(owner_total, capacity, environ.shape[1], env_width),
-            ("gx", "gy"),
-            split_axis=0,
-            concat_axis=0,
-            tiled=True,
-        ),
-        lax.all_to_all(
-            slot_live.reshape(owner_total, capacity),
+            outgoing.reshape(owner_total, capacity, slots, env_width),
             ("gx", "gy"),
             split_axis=0,
             concat_axis=0,

time: 397 us -> 329 us (0.83)
  local copies, waits for them, and re-layouts: 93 us -> 23.7 us
  starting transfers between devices: 142 us -> 127 us
  waiting for transfers between devices: 131 us -> 139 us
  other arithmetic: 13 us -> 19.3 us
    gather x5 -> x3, local copies, waits for them, and re-layouts: 73.3 us -> 1.9 us  [the longest x1 0.73 us: per_device(): proj_near[local_ids // M]]
    all_to_all x2 -> x1, starting transfers between devices: 41.2 us -> 14.5 us  [per_device(): lax.all_to_all(outgoing.reshape(owner_total, capacity, slots, env_width),...]
    ppermute x9, starting transfers between devices: 26.7 us -> 45 us  [with_halo(): lax.ppermute(head, axis, [((i + 1) % count, i) for i in range(ends)])]
    ppermute x9, waiting for transfers between devices: 10.8 us -> 19.7 us  [with_halo(): lax.ppermute(tail, axis, [(i, (i + 1) % count) for i in range(ends)])]
    ppermute x9, starting transfers between devices: 34.8 us -> 27.5 us  [with_halo(): lax.ppermute(tail, axis, [(i, (i + 1) % count) for i in range(ends)])]
    reduce_or x0 -> x1, other arithmetic: none -> 6.81 us  [specialist(): flat_live = jnp.any(environs != 0, axis=(1, 2))]
    unnamed x20 -> x98, local copies, waits for them, and re-layouts: 0.28 us -> 6.06 us
    ppermute x9, waiting for transfers between devices: 10.5 us -> 4.87 us  [with_halo(): lax.ppermute(head, axis, [((i + 1) % count, i) for i in range(ends)])]
  transfers between devices with their start and end apart: 21 -> 20, of which waited for: 9 -> 10; matrix products, arithmetic and copies ran while one was open for 16% -> 4% of each run, Pallas kernels for 0% -> 0%
where the time goes in v1:
time: 329 us; the launch traced here: 327 us
  waiting for transfers between devices  139 us (42%)
  starting transfers between devices  127 us (39%)
  local copies, waits for them, and re-layouts  23.7 us (7%)
  other arithmetic  19.3 us (6%)
  matrix products  15.5 us (5%)
    all_to_all x1, waiting for transfers between devices, per_device(): lax.all_to_all(outgoing.reshape(owner_total, capacity, slots, env_width),...  98.7 us
    ppermute x9, starting transfers between devices, with_halo(): lax.ppermute(head, axis, [((i + 1) % count, i) for i in range(ends)])  45 us
    all_to_all x1, starting transfers between devices, per_device(): lax.all_to_all(results, ('gx', 'gy'), split_axis=0, concat_axis=0, tiled=...  40.3 us
    ppermute x9, starting transfers between devices, with_halo(): lax.ppermute(tail, axis, [(i, (i + 1) % count) for i in range(ends)])  27.5 us
    ppermute x9, waiting for transfers between devices, with_halo(): lax.ppermute(tail, axis, [(i, (i + 1) % count) for i in range(ends)])  19.7 us
    all_to_all x1, waiting for transfers between devices, per_device(): lax.all_to_all(results, ('gx', 'gy'), split_axis=0, concat_axis=0, tiled=...  15.6 us
    all_to_all x1, starting transfers between devices, per_device(): lax.all_to_all(outgoing.reshape(owner_total, capacity, slots, env_width),...  14.5 us
    reduce_or x1, other arithmetic, specialist(): flat_live = jnp.any(environs != 0, axis=(1, 2))  6.81 us
  transfers between devices with their start and end apart: 20, of which 10 were waited for; matrix products, arithmetic and copies ran while one was open for 4% of the time, Pallas kernels for 0%

profile of v1, /device:TPU:1, one launch (start us, length us, event | category | flops | bytes accessed | tf_op | source)
XLA Modules:
  0.0 327.3 jit_solution(13885803270458152055)
XLA Ops:
  0.8 4.8 %collective-permute-start = (bf16[1,4,4,256]{3,2,1,0:T(4,128)(2,1)S(1)}, bf16[1,4,4,256]{3,2,1,0:T(4,128)(2,1)S(1)}, u32[]{:S(2)}, u32[]{:S(2)}) collective-permute-start(bf16[1,4,4,256]{3,2,1,0:T(4,128)(2,1)S(1)} %get-tuple-element.161), channel_id=1, source_target_pairs={{0,1},{1,2},{2,3},{4,5},{5,6},{6,7},{8,9},{9,10},{10,11},{12,13},{... | collective-permute-start | bytes 24584 | tf_op jit(solution)/shard_map/ppermute | solution.py:25
  10.2 4.0 %iota_compare_fusion = pred[128,64,108]{2,1,0:T(8,128)(4,1)S(1)} fusion(s32[128,64]{1,0:T(8,128)} %bitcast.299), kind=kLoop, calls=%fused_computation.18 | loop fusion | flops 884736 | bytes 917504 | tf_op jit(solution)/shard_map/eq | solution.py:156
  14.2 2.8 convolution_convert_fusion.1
  18.0 5.1 %collective-permute-start.3 = (bf16[1,4,40,256]{3,2,1,0:T(8,128)(2,1)S(1)}, bf16[1,4,40,256]{3,2,1,0:T(8,128)(2,1)S(1)}, u32[]{:S(2)}, u32[]{:S(2)}) collective-permute-start(bf16[1,4,40,256]{3,2,1,0:T(8,128)(2,1)S(1)} %pad_maximum_fusion.4), channel_id=1, source_target_pairs={{64,0},{128,64},{192,128},{256,192},{320,256},{384,320},{448,384},... | collective-permute-start | bytes 245768 | tf_op jit(solution)/shard_map/ppermute | solution.py:27
  23.1 1.9 collective-permute-start.2
  25.2 4.3 %collective-permute-done.2 = bf16[1,4,40,256]{3,2,1,0:T(8,128)(2,1)S(1)} collective-permute-done((bf16[1,4,40,256]{3,2,1,0:T(8,128)(2,1)S(1)}, bf16[1,4,40,256]{3,2,1,0:T(8,128)(2,1)S(1)}, u32[]{:S(2)}, u32[]{:S(2)}) %collective-permute-start.2) | collective-permute-done | bytes 81952 | tf_op jit(solution)/shard_map/ppermute | solution.py:25
  29.6 4.3 %collective-permute-start.5 = (bf16[3,1,40,256]{3,2,1,0:T(8,128)(2,1)S(1)}, bf16[3,1,40,256]{3,2,1,0:T(8,128)(2,1)S(1)}, u32[]{:S(2)}, u32[]{:S(2)}) collective-permute-start(bf16[3,1,40,256]{3,2,1,0:T(8,128)(2,1)S(1)} %get-tuple-element.119), channel_id=1, source_target_pairs={{4,0},{8,4},{12,8},{16,12},{20,16},{24,20},{28,24},{32,28},{36,32}... | collective-permute-start | bytes 184328 | tf_op jit(solution)/shard_map/ppermute | solution.py:27
  33.9 3.0 collective-permute-start.4
  37.3 7.2 %collective-permute-done.4 = bf16[3,1,40,256]{3,2,1,0:T(8,128)(2,1)S(1)} collective-permute-done((bf16[3,1,40,256]{3,2,1,0:T(8,128)(2,1)S(1)}, bf16[3,1,40,256]{3,2,1,0:T(8,128)(2,1)S(1)}, u32[]{:S(2)}, u32[]{:S(2)}) %collective-permute-start.4) | collective-permute-done | bytes 61472 | tf_op jit(solution)/shard_map/ppermute | solution.py:25
  51.4 4.0 %collective-permute-start.6 = (bf16[1,4,4,256]{3,1,2,0:T(4,128)(2,1)S(1)}, bf16[1,4,4,256]{3,1,2,0:T(4,128)(2,1)S(1)}, u32[]{:S(2)}, u32[]{:S(2)}) collective-permute-start(bf16[1,4,4,256]{3,1,2,0:T(4,128)(2,1)S(1)} %get-tuple-element.158), channel_id=1, source_target_pairs={{0,1},{1,2},{2,3},{4,5},{5,6},{6,7},{8,9},{9,10},{10,11},{12,13},{... | collective-permute-start | bytes 24584 | tf_op jit(solution)/shard_map/ppermute | solution.py:25
  56.8 3.0 collective-permute-done.7
  59.8 2.0 collective-permute-start.9
  61.8 3.3 %collective-permute-start.8 = (bf16[1,4,40,256]{3,1,2,0:T(4,128)(2,1)S(1)}, bf16[1,4,40,256]{3,1,2,0:T(4,128)(2,1)S(1)}, u32[]{:S(2)}, u32[]{:S(2)}) collective-permute-start(bf16[1,4,40,256]{3,1,2,0:T(4,128)(2,1)S(1)} %constant_dynamic-update-slice_fusion.27), channel_id=1, source_target_pairs={{0,64},{64,128},{128,192},{192,256},{256,320},{320,384},{384,448},... | collective-permute-start | bytes 245768 | tf_op jit(solution)/shard_map/ppermute | solution.py:25
  65.2 3.0 collective-permute-done.8
  68.6 13.7 %collective-permute-start.11 = (bf16[3,1,40,256]{3,1,2,0:T(2,128)(2,1)S(1)}, bf16[3,1,40,256]{3,1,2,0:T(2,128)(2,1)S(1)}, u32[]{:S(2)}, u32[]{:S(2)}) collective-permute-start(bf16[3,1,40,256]{3,1,2,0:T(2,128)(2,1)S(1)} %get-tuple-element.115), channel_id=1, source_target_pairs={{4,0},{8,4},{12,8},{16,12},{20,16},{24,20},{28,24},{32,28},{36,32}... | collective-permute-start | bytes 184328 | tf_op jit(solution)/shard_map/ppermute | solution.py:27
  82.3 2.1 collective-permute-start.10
  92.4 3.1 collective-permute-start.12
  99.9 1.9 collective-permute-start.15
  101.8 3.4 %collective-permute-start.14 = (bf16[1,4,40,128]{3,2,1,0:T(8,128)(2,1)S(1)}, bf16[1,4,40,128]{3,2,1,0:T(8,128)(2,1)S(1)}, u32[]{:S(2)}, u32[]{:S(2)}) collective-permute-start(bf16[1,4,40,128]{3,2,1,0:T(8,128)(2,1)S(1)} %pad_maximum_fusion.14), channel_id=1, source_target_pairs={{0,64},{64,128},{128,192},{192,256},{256,320},{320,384},{384,448},... | collective-permute-start | bytes 122888 | tf_op jit(solution)/shard_map/ppermute | solution.py:25
  105.2 2.5 collective-permute-done.14
  107.8 14.2 %collective-permute-start.17 = (bf16[3,1,40,128]{3,2,1,0:T(8,128)(2,1)S(1)}, bf16[3,1,40,128]{3,2,1,0:T(8,128)(2,1)S(1)}, u32[]{:S(2)}, u32[]{:S(2)}) collective-permute-start(bf16[3,1,40,128]{3,2,1,0:T(8,128)(2,1)S(1)} %get-tuple-element.141), channel_id=1, source_target_pairs={{4,0},{8,4},{12,8},{16,12},{20,16},{24,20},{28,24},{32,28},{36,32}... | collective-permute-start | bytes 92168 | tf_op jit(solution)/shard_map/ppermute | solution.py:27
  128.9 3.1 copy.203
  132.0 14.5 %all-to-all-start = ((bf16[128,2,64,128]{3,2,1,0:T(8,128)(2,1)}), bf16[128,2,64,128]{3,2,1,0:T(8,128)(2,1)}, u32[]{:S(2)}, u32[]{:S(2)}) async-start(bf16[128,2,64,128]{3,2,1,0:T(8,128)(2,1)} %bitcast.197), calls=%async_computation | async-start | bytes 8388608 | tf_op jit(solution)/shard_map/all_to_all | solution.py:203
  146.5 98.7 %all-to-all-done = bf16[128,2,64,128]{3,2,1,0:T(8,128)(2,1)} async-done(((bf16[128,2,64,128]{3,2,1,0:T(8,128)(2,1)}), bf16[128,2,64,128]{3,2,1,0:T(8,128)(2,1)}, u32[]{:S(2)}, u32[]{:S(2)}) %all-to-all-start) | async-done | bytes 4194336 | tf_op jit(solution)/shard_map/all_to_all | solution.py:203
  245.2 6.8 %compare_reduce_fusion = pred[128,2]{1,0:T(8,128)(4,1)S(1)} fusion(bf16[128,2,64,128]{3,2,1,0:T(8,128)(2,1)} %all-to-all-done), kind=kLoop, calls=%fused_computation.17 | loop fusion | flops 4194048 | bytes 4194560 | tf_op jit(solution)/shard_map/reduce_or | solution.py:108
  253.7 3.2 sort.17
  256.9 5.3 %gather_fusion.3 = bf16[256,64,128]{2,1,0:T(8,128)(2,1)} fusion(bf16[256,64,128]{2,1,0:T(8,128)(2,1)} %bitcast.104, s32[1024]{0:T(1024)S(1)} %pad_clamp_fusion.1), kind=kCustom, calls=%fused_computation.3 | custom fusion | bytes 8389632 | tf_op jit(solution)/shard_map/gather | solution.py:119
  262.2 5.1 %while.10 = (s32[]{:T(128)}, f32[256,3]{0,1:T(4,128)S(1)}, s32[]{:T(128)}, bf16[256,64,128]{2,1,0:T(8,128)(2,1)}, bf16[128,1024]{1,0:T(8,128)(2,1)S(1)}, /*index...) while((s32[]{:T(128)}, f32[256,3]{0,1:T(4,128)S(1)}, s32[]{:T(128)}, ...), condition=%wide.region_9.10_spmd, body=%wide.region_7.9_spmd.sunk | while | flops 275890176 | bytes 662235 | solution.py:127
  262.2 2.3 convert_reduce_fusion.3
  264.7 2.3 convert_reduce_fusion.3
  269.5 40.3 %all-to-all-start.1 = ((f32[128,2,3]{2,1,0:T(2,128)}), f32[128,2,3]{2,1,0:T(2,128)S(1)}, u32[]{:S(2)}, u32[]{:S(2)}) async-start(f32[128,2,3]{2,1,0:T(2,128)} %bitcast.107), calls=%async_computation.1 | async-start | bytes 262144 | tf_op jit(solution)/shard_map/all_to_all | solution.py:213
  310.2 15.6 %all-to-all-done.1 = f32[128,2,3]{2,1,0:T(2,128)S(1)} async-done(((f32[128,2,3]{2,1,0:T(2,128)}), f32[128,2,3]{2,1,0:T(2,128)S(1)}, u32[]{:S(2)}, u32[]{:S(2)}) %all-to-all-start.1) | async-done | bytes 3104 | tf_op jit(solution)/shard_map/all_to_all | solution.py:213
  (222 shorter events, 39.1 us)
Async XLA Ops:
  0.0 92.2 %copy-start = (bf16[256,128]{1,0:T(8,128)(2,1)S(1)}, bf16[256,128]{1,0:T(8,128)(2,1)}, u32[]{:S(2)}) copy-start(bf16[256,128]{1,0:T(8,128)(2,1)} %param.21) | copy-start | bytes 196612
  0.0 17.3 %copy-start.1 = (bf16[1,4,32,256]{3,2,1,0:T(8,128)(2,1)S(1)}, bf16[1,4,32,256]{3,2,1,0:T(8,128)(2,1)}, u32[]{:S(2)}) copy-start(bf16[1,4,32,256]{3,2,1,0:T(8,128)(2,1)} %param.15) | copy-start | bytes 196612
  0.0 17.1 %copy-start.3 = (s32[1,1,1,32,1]{3,4,2,1,0:T(1,128)S(1)}, s32[1,1,1,32,1]{3,4,2,1,0:T(1,128)}, u32[]{:S(2)}) copy-start(s32[1,1,1,32,1]{3,4,2,1,0:T(1,128)} %param.26) | copy-start | bytes 388
  0.8 17.2 %collective-permute-start = (bf16[1,4,4,256]{3,2,1,0:T(4,128)(2,1)S(1)}, bf16[1,4,4,256]{3,2,1,0:T(4,128)(2,1)S(1)}, u32[]{:S(2)}, u32[]{:S(2)}) collective-permute-start(bf16[1,4,4,256]{3,2,1,0:T(4,128)(2,1)S(1)} %get-tuple-element.161), channel_id=1, source_target_pairs={{0,1},{1,2},{2,3},{4,5},{5,6},{6,7},{8,9},{9,10},{10,11},{12,13},{... | collective-permute-start | bytes 24584 | tf_op jit(solution)/shard_map/ppermute | solution.py:25
  5.6 12.4 %collective-permute-start.1 = (bf16[1,4,4,256]{3,2,1,0:T(4,128)(2,1)S(1)}, bf16[1,4,4,256]{3,2,1,0:T(4,128)(2,1)S(1)}, u32[]{:S(2)}, u32[]{:S(2)}) collective-permute-start(bf16[1,4,4,256]{3,2,1,0:T(4,128)(2,1)S(1)} %get-tuple-element.162), channel_id=1, source_target_pairs={{1,0},{2,1},{3,2},{5,4},{6,5},{7,6},{9,8},{10,9},{11,10},{13,12},{... | collective-permute-start | bytes 24584 | tf_op jit(solution)/shard_map/ppermute | solution.py:27
  18.0 7.2 %collective-permute-start.3 = (bf16[1,4,40,256]{3,2,1,0:T(8,128)(2,1)S(1)}, bf16[1,4,40,256]{3,2,1,0:T(8,128)(2,1)S(1)}, u32[]{:S(2)}, u32[]{:S(2)}) collective-permute-start(bf16[1,4,40,256]{3,2,1,0:T(8,128)(2,1)S(1)} %pad_maximum_fusion.4), channel_id=1, source_target_pairs={{64,0},{128,64},{192,128},{256,192},{320,256},{384,320},{448,384},... | collective-permute-start | bytes 245768 | tf_op jit(solution)/shard_map/ppermute | solution.py:27
  23.1 6.4 %collective-permute-start.2 = (bf16[1,4,40,256]{3,2,1,0:T(8,128)(2,1)S(1)}, bf16[1,4,40,256]{3,2,1,0:T(8,128)(2,1)S(1)}, u32[]{:S(2)}, u32[]{:S(2)}) collective-permute-start(bf16[1,4,40,256]{3,2,1,0:T(8,128)(2,1)S(1)} %pad_maximum_fusion.4), channel_id=1, source_target_pairs={{0,64},{64,128},{128,192},{192,256},{256,320},{320,384},{384,448},... | collective-permute-start | bytes 245768 | tf_op jit(solution)/shard_map/ppermute | solution.py:25
  29.6 7.8 %collective-permute-start.5 = (bf16[3,1,40,256]{3,2,1,0:T(8,128)(2,1)S(1)}, bf16[3,1,40,256]{3,2,1,0:T(8,128)(2,1)S(1)}, u32[]{:S(2)}, u32[]{:S(2)}) collective-permute-start(bf16[3,1,40,256]{3,2,1,0:T(8,128)(2,1)S(1)} %get-tuple-element.119), channel_id=1, source_target_pairs={{4,0},{8,4},{12,8},{16,12},{20,16},{24,20},{28,24},{32,28},{36,32}... | collective-permute-start | bytes 184328 | tf_op jit(solution)/shard_map/ppermute | solution.py:27
  33.9 10.7 %collective-permute-start.4 = (bf16[3,1,40,256]{3,2,1,0:T(8,128)(2,1)S(1)}, bf16[3,1,40,256]{3,2,1,0:T(8,128)(2,1)S(1)}, u32[]{:S(2)}, u32[]{:S(2)}) collective-permute-start(bf16[3,1,40,256]{3,2,1,0:T(8,128)(2,1)S(1)} %get-tuple-element.120), channel_id=1, source_target_pairs={{0,4},{4,8},{8,12},{12,16},{16,20},{20,24},{24,28},{28,32},{32,36}... | collective-permute-start | bytes 184328 | tf_op jit(solution)/shard_map/ppermute | solution.py:25
  48.1 1.3 copy-start.5
  51.4 5.3 %collective-permute-start.6 = (bf16[1,4,4,256]{3,1,2,0:T(4,128)(2,1)S(1)}, bf16[1,4,4,256]{3,1,2,0:T(4,128)(2,1)S(1)}, u32[]{:S(2)}, u32[]{:S(2)}) collective-permute-start(bf16[1,4,4,256]{3,1,2,0:T(4,128)(2,1)S(1)} %get-tuple-element.158), channel_id=1, source_target_pairs={{0,1},{1,2},{2,3},{4,5},{5,6},{6,7},{8,9},{9,10},{10,11},{12,13},{... | collective-permute-start | bytes 24584 | tf_op jit(solution)/shard_map/ppermute | solution.py:25
  55.4 4.4 %collective-permute-start.7 = (bf16[1,4,4,256]{3,1,2,0:T(4,128)(2,1)S(1)}, bf16[1,4,4,256]{3,1,2,0:T(4,128)(2,1)S(1)}, u32[]{:S(2)}, u32[]{:S(2)}) collective-permute-start(bf16[1,4,4,256]{3,1,2,0:T(4,128)(2,1)S(1)} %get-tuple-element.157), channel_id=1, source_target_pairs={{1,0},{2,1},{3,2},{5,4},{6,5},{7,6},{9,8},{10,9},{11,10},{13,12},{... | collective-permute-start | bytes 24584 | tf_op jit(solution)/shard_map/ppermute | solution.py:27
  59.8 5.4 %collective-permute-start.9 = (bf16[1,4,40,256]{3,1,2,0:T(4,128)(2,1)S(1)}, bf16[1,4,40,256]{3,1,2,0:T(4,128)(2,1)S(1)}, u32[]{:S(2)}, u32[]{:S(2)}) collective-permute-start(bf16[1,4,40,256]{3,1,2,0:T(4,128)(2,1)S(1)} %constant_dynamic-update-slice_fusion.27), channel_id=1, source_target_pairs={{64,0},{128,64},{192,128},{256,192},{320,256},{384,320},{448,384},... | collective-permute-start | bytes 245768 | tf_op jit(solution)/shard_map/ppermute | solution.py:27
  61.8 6.4 %collective-permute-start.8 = (bf16[1,4,40,256]{3,1,2,0:T(4,128)(2,1)S(1)}, bf16[1,4,40,256]{3,1,2,0:T(4,128)(2,1)S(1)}, u32[]{:S(2)}, u32[]{:S(2)}) collective-permute-start(bf16[1,4,40,256]{3,1,2,0:T(4,128)(2,1)S(1)} %constant_dynamic-update-slice_fusion.27), channel_id=1, source_target_pairs={{0,64},{64,128},{128,192},{192,256},{256,320},{320,384},{384,448},... | collective-permute-start | bytes 245768 | tf_op jit(solution)/shard_map/ppermute | solution.py:25
  68.6 15.9 %collective-permute-start.11 = (bf16[3,1,40,256]{3,1,2,0:T(2,128)(2,1)S(1)}, bf16[3,1,40,256]{3,1,2,0:T(2,128)(2,1)S(1)}, u32[]{:S(2)}, u32[]{:S(2)}) collective-permute-start(bf16[3,1,40,256]{3,1,2,0:T(2,128)(2,1)S(1)} %get-tuple-element.115), channel_id=1, source_target_pairs={{4,0},{8,4},{12,8},{16,12},{20,16},{24,20},{28,24},{32,28},{36,32}... | collective-permute-start | bytes 184328 | tf_op jit(solution)/shard_map/ppermute | solution.py:27
  82.3 3.8 %collective-permute-start.10 = (bf16[3,1,40,256]{3,1,2,0:T(2,128)(2,1)S(1)}, bf16[3,1,40,256]{3,1,2,0:T(2,128)(2,1)S(1)}, u32[]{:S(2)}, u32[]{:S(2)}) collective-permute-start(bf16[3,1,40,256]{3,1,2,0:T(2,128)(2,1)S(1)} %get-tuple-element.116), channel_id=1, source_target_pairs={{0,4},{4,8},{8,12},{12,16},{16,20},{20,24},{24,28},{28,32},{32,36}... | collective-permute-start | bytes 184328 | tf_op jit(solution)/shard_map/ppermute | solution.py:25
  92.4 5.6 %collective-permute-start.12 = (bf16[1,4,4,128]{3,2,1,0:T(4,128)(2,1)S(1)}, bf16[1,4,4,128]{3,2,1,0:T(4,128)(2,1)S(1)}, u32[]{:S(2)}, u32[]{:S(2)}) collective-permute-start(bf16[1,4,4,128]{3,2,1,0:T(4,128)(2,1)S(1)} %get-tuple-element.171), channel_id=1, source_target_pairs={{0,1},{1,2},{2,3},{4,5},{5,6},{6,7},{8,9},{9,10},{10,11},{12,13},{... | collective-permute-start | bytes 12296 | tf_op jit(solution)/shard_map/ppermute | solution.py:25
  95.5 4.4 %collective-permute-start.13 = (bf16[1,4,4,128]{3,2,1,0:T(4,128)(2,1)S(1)}, bf16[1,4,4,128]{3,2,1,0:T(4,128)(2,1)S(1)}, u32[]{:S(2)}, u32[]{:S(2)}) collective-permute-start(bf16[1,4,4,128]{3,2,1,0:T(4,128)(2,1)S(1)} %get-tuple-element.172), channel_id=1, source_target_pairs={{1,0},{2,1},{3,2},{5,4},{6,5},{7,6},{9,8},{10,9},{11,10},{13,12},{... | collective-permute-start | bytes 12296 | tf_op jit(solution)/shard_map/ppermute | solution.py:27
  99.9 5.3 %collective-permute-start.15 = (bf16[1,4,40,128]{3,2,1,0:T(8,128)(2,1)S(1)}, bf16[1,4,40,128]{3,2,1,0:T(8,128)(2,1)S(1)}, u32[]{:S(2)}, u32[]{:S(2)}) collective-permute-start(bf16[1,4,40,128]{3,2,1,0:T(8,128)(2,1)S(1)} %pad_maximum_fusion.14), channel_id=1, source_target_pairs={{64,0},{128,64},{192,128},{256,192},{320,256},{384,320},{448,384},... | collective-permute-start | bytes 122888 | tf_op jit(solution)/shard_map/ppermute | solution.py:27
  101.8 6.0 %collective-permute-start.14 = (bf16[1,4,40,128]{3,2,1,0:T(8,128)(2,1)S(1)}, bf16[1,4,40,128]{3,2,1,0:T(8,128)(2,1)S(1)}, u32[]{:S(2)}, u32[]{:S(2)}) collective-permute-start(bf16[1,4,40,128]{3,2,1,0:T(8,128)(2,1)S(1)} %pad_maximum_fusion.14), channel_id=1, source_target_pairs={{0,64},{64,128},{128,192},{192,256},{256,320},{320,384},{384,448},... | collective-permute-start | bytes 122888 | tf_op jit(solution)/shard_map/ppermute | solution.py:25
  107.8 16.2 %collective-permute-start.17 = (bf16[3,1,40,128]{3,2,1,0:T(8,128)(2,1)S(1)}, bf16[3,1,40,128]{3,2,1,0:T(8,128)(2,1)S(1)}, u32[]{:S(2)}, u32[]{:S(2)}) collective-permute-start(bf16[3,1,40,128]{3,2,1,0:T(8,128)(2,1)S(1)} %get-tuple-element.141), channel_id=1, source_target_pairs={{4,0},{8,4},{12,8},{16,12},{20,16},{24,20},{28,24},{32,28},{36,32}... | collective-permute-start | bytes 92168 | tf_op jit(solution)/shard_map/ppermute | solution.py:27
  122.0 3.1 collective-permute-start.16
  132.0 113.2 %all-to-all-start = ((bf16[128,2,64,128]{3,2,1,0:T(8,128)(2,1)}), bf16[128,2,64,128]{3,2,1,0:T(8,128)(2,1)}, u32[]{:S(2)}, u32[]{:S(2)}) async-start(bf16[128,2,64,128]{3,2,1,0:T(8,128)(2,1)} %bitcast.197), calls=%async_computation | async-start | bytes 8388608 | tf_op jit(solution)/shard_map/all_to_all | solution.py:203
  256.9 5.3 %copy-start.2 = (bf16[1,3,1024]{2,1,0:T(4,128)(2,1)S(1)}, bf16[1,3,1024]{2,1,0:T(4,128)(2,1)}, u32[]{:S(2)}) copy-start(bf16[1,3,1024]{2,1,0:T(4,128)(2,1)} %param.24) | copy-start | bytes 18436
  256.9 5.3 %copy-start.6 = (bf16[1,128,1024]{2,1,0:T(8,128)(2,1)S(1)}, bf16[1,128,1024]{2,1,0:T(8,128)(2,1)}, u32[]{:S(2)}) copy-start(bf16[1,128,1024]{2,1,0:T(8,128)(2,1)} %param.23) | copy-start | bytes 786436
  262.2 47.7 %copy-start.4 = (bf16[3,256]{1,0:T(4,128)(2,1)S(1)}, bf16[3,256]{1,0:T(4,128)(2,1)}, u32[]{:S(2)}) copy-start(bf16[3,256]{1,0:T(4,128)(2,1)} %param.22) | copy-start | bytes 4612
  269.5 56.2 %all-to-all-start.1 = ((f32[128,2,3]{2,1,0:T(2,128)}), f32[128,2,3]{2,1,0:T(2,128)S(1)}, u32[]{:S(2)}, u32[]{:S(2)}) async-start(f32[128,2,3]{2,1,0:T(2,128)} %bitcast.107), calls=%async_computation.1 | async-start | bytes 262144 | tf_op jit(solution)/shard_map/all_to_all | solution.py:213

commit v2 on v1

--- a/solution.py
+++ b/solution.py
@@ -4,6 +4,7 @@
 import jax.numpy as jnp
 from jax import lax
 from jax.sharding import PartitionSpec as P
+from jax.experimental import pallas as pl
 
 M = 4
 NRB = 8
@@ -100,36 +101,48 @@
     ).reshape(state.shape)
 
 
+def specialist_kernel(env_ref, first_ref, head_ref, out_ref):
+    piece = 8
+    slots = env_ref.shape[0] // out_ref.shape[0]
+    span = piece * slots
+    column = lax.broadcasted_iota(jnp.int32, (piece, span), 1)
+    row = lax.broadcasted_iota(jnp.int32, (piece, span), 0)
+    pool = ((column >= row * slots) & (column < (row + 1) * slots)).astype(jnp.bfloat16)
+
+    def body(index, carry):
+        begin = pl.multiple_of(index * span, span)
+        message = jnp.dot(
+            env_ref[pl.ds(begin, span), :], first_ref[...], preferred_element_type=jnp.float32
+        )
+        hidden = (message * (0.5 * jnp.tanh(0.5 * message) + 0.5)).astype(jnp.bfloat16)
+        pooled = jnp.dot(pool, hidden, preferred_element_type=jnp.float32)
+        pooled = (pooled * (1.0 / slots)).astype(jnp.bfloat16)
+        out_ref[pl.ds(pl.multiple_of(index * piece, piece), piece), :] = jnp.dot(
+            pooled, head_ref[...], preferred_element_type=jnp.float32
+        )
+        return carry
+
+    lax.fori_loop(0, out_ref.shape[0] // piece, body, 0)
+
+
 def specialist(received, w_first, w_head):
-    sources, item_count = (received.shape[0], received.shape[1])
+    sources, item_count, slots, env_width = received.shape
     env_total = sources * item_count
-    block_size = math.gcd(env_total, 16)
-    environs = received.reshape(env_total, received.shape[2], received.shape[3])
-    flat_live = jnp.any(environs != 0, axis=(1, 2))
-
-    def run_block(env_piece):
-        hidden = jax.nn.silu(
-            jnp.einsum("bse,eh->bsh", env_piece, w_first, preferred_element_type=jnp.float32)
-        ).astype(jnp.bfloat16)
-        pooled = (jnp.sum(hidden, axis=1, dtype=jnp.float32) / hidden.shape[1]).astype(jnp.bfloat16)
-        return jnp.einsum("bh,ch->bc", pooled, w_head, preferred_element_type=jnp.float32)
-
-    order = jnp.argsort(jnp.where(flat_live, 0, 1).astype(jnp.int32), stable=True)
-    live_total = jnp.sum(flat_live.astype(jnp.int32))
-    ordered = environs[order]
-    block_count = (live_total + block_size - 1) // block_size
-
-    def step_block(index, gathered):
-        offset = index * block_size
-        piece = lax.dynamic_slice_in_dim(ordered, offset, block_size, 0)
-        return lax.dynamic_update_slice_in_dim(gathered, run_block(piece), offset, 0)
-
-    sorted_results = lax.fori_loop(
-        0, block_count, step_block, jnp.zeros((env_total, 3), jnp.float32)
-    )
-    results = jnp.zeros((env_total, 3), jnp.float32).at[order].set(sorted_results)
-    results = results * flat_live[:, None].astype(jnp.float32)
-    return results.reshape(sources, item_count, 3)
+    hidden_width = w_first.shape[-1]
+    block = math.gcd(env_total, 32)
+    head = jnp.zeros((hidden_width, 128), jnp.bfloat16).at[:, : w_head.shape[0]].set(w_head.T)
+    results = pl.pallas_call(
+        specialist_kernel,
+        grid=(env_total // block,),
+        in_specs=[
+            pl.BlockSpec((block * slots, env_width), lambda i: (i, 0)),
+            pl.BlockSpec((env_width, hidden_width), lambda i: (0, 0)),
+            pl.BlockSpec((hidden_width, 128), lambda i: (0, 0)),
+        ],
+        out_specs=pl.BlockSpec((block, 128), lambda i: (i, 0)),
+        out_shape=jax.ShapeDtypeStruct((env_total, 128), jnp.float32),
+    )(received.reshape(env_total * slots, env_width), w_first, head)
+    return results[:, : w_head.shape[0]].reshape(sources, item_count, w_head.shape[0])
 
 
 def per_device(

time: 329 us -> 299 us (0.909)
  starting transfers between devices: 127 us -> 96.2 us
  Pallas kernels: 0 us -> 26.9 us
  other arithmetic: 19.3 us -> 9.98 us
  local copies, waits for them, and re-layouts: 23.7 us -> 16.7 us
  matrix products: 15.5 us -> 10.8 us
  waiting for transfers between devices: 139 us -> 135 us
    all_to_all x1, starting transfers between devices: 40.3 us -> 9.68 us  [per_device(): lax.all_to_all(results, ('gx', 'gy'), split_axis=0, concat_axis=0, tiled=...]
    pallas_call x0 -> x1, Pallas kernels: none -> 26.9 us  [specialist(): pl.pallas_call(specialist_kernel, grid=(env_total // block,), in_specs=[p...]
    reduce_or x1 -> x0, other arithmetic: 6.81 us -> none  [specialist(): flat_live = jnp.any(environs != 0, axis=(1, 2))]
    gather x1 -> x0, local copies, waits for them, and re-layouts: 5.27 us -> none  [specialist(): ordered = environs[order]]
    dot_general x4 -> x0, matrix products: 4.77 us -> none  [the longest x2 4.53 us: run_block(): jnp.einsum('bse,eh->bsh', env_piece, w_first, preferred_element_type=jnp....]
  transfers between devices with their start and end apart: 20 -> 20, of which waited for: 10 -> 9; matrix products, arithmetic and copies ran while one was open for 4% -> 5% of each run, Pallas kernels for 0% -> 0%
where the time goes in v2:
time: 299 us; the launch traced here: 297 us
  waiting for transfers between devices  135 us (45%)
  starting transfers between devices  96.2 us (32%)
  Pallas kernels  26.9 us (9%)
  local copies, waits for them, and re-layouts  16.7 us (6%)
  matrix products  10.8 us (4%)
  other arithmetic  9.98 us (3%)
    all_to_all x1, waiting for transfers between devices, per_device(): lax.all_to_all(outgoing.reshape(owner_total, capacity, slots, env_width),...  96.9 us
    ppermute x9, starting transfers between devices, with_halo(): lax.ppermute(head, axis, [((i + 1) % count, i) for i in range(ends)])  44.9 us
    ppermute x9, starting transfers between devices, with_halo(): lax.ppermute(tail, axis, [(i, (i + 1) % count) for i in range(ends)])  27.1 us
    pallas_call x1, Pallas kernels, specialist(): pl.pallas_call(specialist_kernel, grid=(env_total // block,), in_specs=[p...  26.9 us
    ppermute x9, waiting for transfers between devices, with_halo(): lax.ppermute(tail, axis, [(i, (i + 1) % count) for i in range(ends)])  19.5 us
    all_to_all x1, waiting for transfers between devices, per_device(): lax.all_to_all(results, ('gx', 'gy'), split_axis=0, concat_axis=0, tiled=...  15.6 us
    all_to_all x1, starting transfers between devices, per_device(): lax.all_to_all(outgoing.reshape(owner_total, capacity, slots, env_width),...  14.6 us
    all_to_all x1, starting transfers between devices, per_device(): lax.all_to_all(results, ('gx', 'gy'), split_axis=0, concat_axis=0, tiled=...  9.68 us
  transfers between devices with their start and end apart: 20, of which 9 were waited for; matrix products, arithmetic and copies ran while one was open for 5% of the time, Pallas kernels for 0%

profile of v2, /device:TPU:1, one launch (start us, length us, event | category | flops | bytes accessed | tf_op | source)
XLA Modules:
  0.0 297.4 jit_solution(12987406348396198540)
XLA Ops:
  0.8 1.3 collective-permute-start.1
  2.1 5.4 %collective-permute-start = (bf16[1,4,4,256]{3,2,1,0:T(4,128)(2,1)S(1)}, bf16[1,4,4,256]{3,2,1,0:T(4,128)(2,1)S(1)}, u32[]{:S(2)}, u32[]{:S(2)}) collective-permute-start(bf16[1,4,4,256]{3,2,1,0:T(4,128)(2,1)S(1)} %get-tuple-element.101), channel_id=1, source_target_pairs={{0,1},{1,2},{2,3},{4,5},{5,6},{6,7},{8,9},{9,10},{10,11},{12,13},{... | collective-permute-start | bytes 24584 | tf_op jit(solution)/shard_map/ppermute | solution.py:26
  10.1 4.0 %iota_compare_fusion = pred[128,64,108]{2,1,0:T(8,128)(4,1)S(1)} fusion(s32[128,64]{1,0:T(8,128)} %bitcast.295), kind=kLoop, calls=%fused_computation.6 | loop fusion | flops 884736 | bytes 917504 | tf_op jit(solution)/shard_map/eq | solution.py:169
  14.9 2.8 convolution_convert_fusion.1
  18.7 5.1 %collective-permute-start.3 = (bf16[1,4,40,256]{3,2,1,0:T(8,128)(2,1)S(1)}, bf16[1,4,40,256]{3,2,1,0:T(8,128)(2,1)S(1)}, u32[]{:S(2)}, u32[]{:S(2)}) collective-permute-start(bf16[1,4,40,256]{3,2,1,0:T(8,128)(2,1)S(1)} %pad_maximum_fusion.4), channel_id=1, source_target_pairs={{64,0},{128,64},{192,128},{256,192},{320,256},{384,320},{448,384},... | collective-permute-start | bytes 245768 | tf_op jit(solution)/shard_map/ppermute | solution.py:28
  23.8 1.9 collective-permute-start.2
  25.9 4.3 %collective-permute-done.2 = bf16[1,4,40,256]{3,2,1,0:T(8,128)(2,1)S(1)} collective-permute-done((bf16[1,4,40,256]{3,2,1,0:T(8,128)(2,1)S(1)}, bf16[1,4,40,256]{3,2,1,0:T(8,128)(2,1)S(1)}, u32[]{:S(2)}, u32[]{:S(2)}) %collective-permute-start.2) | collective-permute-done | bytes 81952 | tf_op jit(solution)/shard_map/ppermute | solution.py:26
  30.2 5.8 %collective-permute-start.5 = (bf16[3,1,40,256]{3,2,1,0:T(8,128)(2,1)S(1)}, bf16[3,1,40,256]{3,2,1,0:T(8,128)(2,1)S(1)}, u32[]{:S(2)}, u32[]{:S(2)}) collective-permute-start(bf16[3,1,40,256]{3,2,1,0:T(8,128)(2,1)S(1)} %get-tuple-element.59), channel_id=1, source_target_pairs={{4,0},{8,4},{12,8},{16,12},{20,16},{24,20},{28,24},{32,28},{36,32}... | collective-permute-start | bytes 184328 | tf_op jit(solution)/shard_map/ppermute | solution.py:28
  36.0 1.9 collective-permute-start.4
  38.4 7.0 %collective-permute-done.4 = bf16[3,1,40,256]{3,2,1,0:T(8,128)(2,1)S(1)} collective-permute-done((bf16[3,1,40,256]{3,2,1,0:T(8,128)(2,1)S(1)}, bf16[3,1,40,256]{3,2,1,0:T(8,128)(2,1)S(1)}, u32[]{:S(2)}, u32[]{:S(2)}) %collective-permute-start.4) | collective-permute-done | bytes 61472 | tf_op jit(solution)/shard_map/ppermute | solution.py:26
  50.3 1.8 multiply_reduce_fusion.1
  52.3 3.1 %collective-permute-start.6 = (bf16[1,4,4,256]{3,1,2,0:T(4,128)(2,1)S(1)}, bf16[1,4,4,256]{3,1,2,0:T(4,128)(2,1)S(1)}, u32[]{:S(2)}, u32[]{:S(2)}) collective-permute-start(bf16[1,4,4,256]{3,1,2,0:T(4,128)(2,1)S(1)} %get-tuple-element.98), channel_id=1, source_target_pairs={{0,1},{1,2},{2,3},{4,5},{5,6},{6,7},{8,9},{9,10},{10,11},{12,13},{... | collective-permute-start | bytes 24584 | tf_op jit(solution)/shard_map/ppermute | solution.py:26
  56.8 3.0 %collective-permute-done.7 = bf16[1,4,4,256]{3,1,2,0:T(4,128)(2,1)S(1)} collective-permute-done((bf16[1,4,4,256]{3,1,2,0:T(4,128)(2,1)S(1)}, bf16[1,4,4,256]{3,1,2,0:T(4,128)(2,1)S(1)}, u32[]{:S(2)}, u32[]{:S(2)}) %collective-permute-start.7) | collective-permute-done | bytes 8224 | tf_op jit(solution)/shard_map/ppermute | solution.py:28
  59.8 2.0 collective-permute-start.9
  61.8 3.3 %collective-permute-start.8 = (bf16[1,4,40,256]{3,1,2,0:T(4,128)(2,1)S(1)}, bf16[1,4,40,256]{3,1,2,0:T(4,128)(2,1)S(1)}, u32[]{:S(2)}, u32[]{:S(2)}) collective-permute-start(bf16[1,4,40,256]{3,1,2,0:T(4,128)(2,1)S(1)} %constant_dynamic-update-slice_fusion.27), channel_id=1, source_target_pairs={{0,64},{64,128},{128,192},{192,256},{256,320},{320,384},{384,448},... | collective-permute-start | bytes 245768 | tf_op jit(solution)/shard_map/ppermute | solution.py:26
  65.2 3.0 %collective-permute-done.8 = bf16[1,4,40,256]{3,1,2,0:T(4,128)(2,1)S(1)} collective-permute-done((bf16[1,4,40,256]{3,1,2,0:T(4,128)(2,1)S(1)}, bf16[1,4,40,256]{3,1,2,0:T(4,128)(2,1)S(1)}, u32[]{:S(2)}, u32[]{:S(2)}) %collective-permute-start.8) | collective-permute-done | bytes 81952 | tf_op jit(solution)/shard_map/ppermute | solution.py:26
  68.6 13.8 %collective-permute-start.11 = (bf16[3,1,40,256]{3,1,2,0:T(2,128)(2,1)S(1)}, bf16[3,1,40,256]{3,1,2,0:T(2,128)(2,1)S(1)}, u32[]{:S(2)}, u32[]{:S(2)}) collective-permute-start(bf16[3,1,40,256]{3,1,2,0:T(2,128)(2,1)S(1)} %get-tuple-element.55), channel_id=1, source_target_pairs={{4,0},{8,4},{12,8},{16,12},{20,16},{24,20},{28,24},{32,28},{36,32}... | collective-permute-start | bytes 184328 | tf_op jit(solution)/shard_map/ppermute | solution.py:28
  82.4 2.1 collective-permute-start.10
  84.6 1.5 collective-permute-done.10
  90.5 1.8 multiply_reduce_fusion
  93.8 4.0 %collective-permute-start.12 = (bf16[1,4,4,128]{3,2,1,0:T(4,128)(2,1)S(1)}, bf16[1,4,4,128]{3,2,1,0:T(4,128)(2,1)S(1)}, u32[]{:S(2)}, u32[]{:S(2)}) collective-permute-start(bf16[1,4,4,128]{3,2,1,0:T(4,128)(2,1)S(1)} %get-tuple-element.111), channel_id=1, source_target_pairs={{0,1},{1,2},{2,3},{4,5},{5,6},{6,7},{8,9},{9,10},{10,11},{12,13},{... | collective-permute-start | bytes 12296 | tf_op jit(solution)/shard_map/ppermute | solution.py:26
  99.1 1.9 collective-permute-start.15
  101.0 3.4 %collective-permute-start.14 = (bf16[1,4,40,128]{3,2,1,0:T(8,128)(2,1)S(1)}, bf16[1,4,40,128]{3,2,1,0:T(8,128)(2,1)S(1)}, u32[]{:S(2)}, u32[]{:S(2)}) collective-permute-start(bf16[1,4,40,128]{3,2,1,0:T(8,128)(2,1)S(1)} %pad_maximum_fusion.14), channel_id=1, source_target_pairs={{0,64},{64,128},{128,192},{192,256},{256,320},{320,384},{384,448},... | collective-permute-start | bytes 122888 | tf_op jit(solution)/shard_map/ppermute | solution.py:26
  104.4 2.5 collective-permute-done.14
  107.0 12.4 %collective-permute-start.17 = (bf16[3,1,40,128]{3,2,1,0:T(8,128)(2,1)S(1)}, bf16[3,1,40,128]{3,2,1,0:T(8,128)(2,1)S(1)}, u32[]{:S(2)}, u32[]{:S(2)}) collective-permute-start(bf16[3,1,40,128]{3,2,1,0:T(8,128)(2,1)S(1)} %get-tuple-element.81), channel_id=1, source_target_pairs={{4,0},{8,4},{12,8},{16,12},{20,16},{24,20},{28,24},{32,28},{36,32}... | collective-permute-start | bytes 92168 | tf_op jit(solution)/shard_map/ppermute | solution.py:28
  119.4 1.9 collective-permute-start.16
  126.3 3.2 %copy.104 = bf16[32,8,64,128]{3,2,1,0:T(8,128)(2,1)} copy(bf16[32,8,64,128]{3,1,2,0:T(8,128)(2,1)S(1)} %fusion) | data formatting | bytes 8388608
  129.5 14.6 %all-to-all-start = ((bf16[128,2,64,128]{3,2,1,0:T(8,128)(2,1)}), bf16[128,2,64,128]{3,2,1,0:T(8,128)(2,1)}, u32[]{:S(2)}, u32[]{:S(2)}) async-start(bf16[128,2,64,128]{3,2,1,0:T(8,128)(2,1)} %bitcast.192), calls=%async_computation | async-start | bytes 8388608 | tf_op jit(solution)/shard_map/all_to_all | solution.py:216
  146.4 96.9 %all-to-all-done = bf16[128,2,64,128]{3,2,1,0:T(8,128)(2,1)} async-done(((bf16[128,2,64,128]{3,2,1,0:T(8,128)(2,1)}), bf16[128,2,64,128]{3,2,1,0:T(8,128)(2,1)}, u32[]{:S(2)}, u32[]{:S(2)}) %all-to-all-start) | async-done | bytes 4194336 | tf_op jit(solution)/shard_map/all_to_all | solution.py:216
  243.3 26.9 %shard_map.127 = f32[256,128]{1,0:T(8,128)} custom-call(bf16[16384,128]{1,0:T(8,128)(2,1)} %bitcast.103.env_ref, bf16[128,1024]{1,0:T(8,128)(2,1)} %bitcast.214, bf16[1024,128]{1,0:T(8,128)(2,1)} %scatter.4.head_ref), custom_call_target="tpu_custom_call" | custom-call | tf_op jit(solution)/shard_map/pallas_call | solution.py:134
  270.3 9.7 %all-to-all-start.1 = ((f32[128,2,3]{2,1,0:T(2,128)}), f32[128,2,3]{2,1,0:T(2,128)S(1)}, u32[]{:S(2)}, u32[]{:S(2)}) async-start(f32[128,2,3]{2,1,0:T(2,128)} %bitcast.210), calls=%async_computation.1 | async-start | bytes 262144 | tf_op jit(solution)/shard_map/all_to_all | solution.py:226
  280.3 15.6 %all-to-all-done.1 = f32[128,2,3]{2,1,0:T(2,128)S(1)} async-done(((f32[128,2,3]{2,1,0:T(2,128)}), f32[128,2,3]{2,1,0:T(2,128)S(1)}, u32[]{:S(2)}, u32[]{:S(2)}) %all-to-all-start.1) | async-done | bytes 3104 | tf_op jit(solution)/shard_map/all_to_all | solution.py:226
  (202 shorter events, 27.5 us)
Async XLA Ops:
  0.0 92.3 %copy-start = (bf16[256,128]{1,0:T(8,128)(2,1)S(1)}, bf16[256,128]{1,0:T(8,128)(2,1)}, u32[]{:S(2)}) copy-start(bf16[256,128]{1,0:T(8,128)(2,1)} %param.21) | copy-start | bytes 196612
  0.0 17.9 %copy-start.1 = (bf16[1,4,32,256]{3,2,1,0:T(8,128)(2,1)S(1)}, bf16[1,4,32,256]{3,2,1,0:T(8,128)(2,1)}, u32[]{:S(2)}) copy-start(bf16[1,4,32,256]{3,2,1,0:T(8,128)(2,1)} %param.15) | copy-start | bytes 196612
  0.0 17.7 %copy-start.3 = (s32[1,1,1,32,1]{3,4,2,1,0:T(1,128)S(1)}, s32[1,1,1,32,1]{3,4,2,1,0:T(1,128)}, u32[]{:S(2)}) copy-start(s32[1,1,1,32,1]{3,4,2,1,0:T(1,128)} %param.26) | copy-start | bytes 388
  0.8 17.8 %collective-permute-start.1 = (bf16[1,4,4,256]{3,2,1,0:T(4,128)(2,1)S(1)}, bf16[1,4,4,256]{3,2,1,0:T(4,128)(2,1)S(1)}, u32[]{:S(2)}, u32[]{:S(2)}) collective-permute-start(bf16[1,4,4,256]{3,2,1,0:T(4,128)(2,1)S(1)} %get-tuple-element.102), channel_id=1, source_target_pairs={{1,0},{2,1},{3,2},{5,4},{6,5},{7,6},{9,8},{10,9},{11,10},{13,12},{... | collective-permute-start | bytes 24584 | tf_op jit(solution)/shard_map/ppermute | solution.py:28
  2.1 16.5 %collective-permute-start = (bf16[1,4,4,256]{3,2,1,0:T(4,128)(2,1)S(1)}, bf16[1,4,4,256]{3,2,1,0:T(4,128)(2,1)S(1)}, u32[]{:S(2)}, u32[]{:S(2)}) collective-permute-start(bf16[1,4,4,256]{3,2,1,0:T(4,128)(2,1)S(1)} %get-tuple-element.101), channel_id=1, source_target_pairs={{0,1},{1,2},{2,3},{4,5},{5,6},{6,7},{8,9},{9,10},{10,11},{12,13},{... | collective-permute-start | bytes 24584 | tf_op jit(solution)/shard_map/ppermute | solution.py:26
  18.7 7.2 %collective-permute-start.3 = (bf16[1,4,40,256]{3,2,1,0:T(8,128)(2,1)S(1)}, bf16[1,4,40,256]{3,2,1,0:T(8,128)(2,1)S(1)}, u32[]{:S(2)}, u32[]{:S(2)}) collective-permute-start(bf16[1,4,40,256]{3,2,1,0:T(8,128)(2,1)S(1)} %pad_maximum_fusion.4), channel_id=1, source_target_pairs={{64,0},{128,64},{192,128},{256,192},{320,256},{384,320},{448,384},... | collective-permute-start | bytes 245768 | tf_op jit(solution)/shard_map/ppermute | solution.py:28
  23.8 6.4 %collective-permute-start.2 = (bf16[1,4,40,256]{3,2,1,0:T(8,128)(2,1)S(1)}, bf16[1,4,40,256]{3,2,1,0:T(8,128)(2,1)S(1)}, u32[]{:S(2)}, u32[]{:S(2)}) collective-permute-start(bf16[1,4,40,256]{3,2,1,0:T(8,128)(2,1)S(1)} %pad_maximum_fusion.4), channel_id=1, source_target_pairs={{0,64},{64,128},{128,192},{192,256},{256,320},{320,384},{384,448},... | collective-permute-start | bytes 245768 | tf_op jit(solution)/shard_map/ppermute | solution.py:26
  30.2 8.2 %collective-permute-start.5 = (bf16[3,1,40,256]{3,2,1,0:T(8,128)(2,1)S(1)}, bf16[3,1,40,256]{3,2,1,0:T(8,128)(2,1)S(1)}, u32[]{:S(2)}, u32[]{:S(2)}) collective-permute-start(bf16[3,1,40,256]{3,2,1,0:T(8,128)(2,1)S(1)} %get-tuple-element.59), channel_id=1, source_target_pairs={{4,0},{8,4},{12,8},{16,12},{20,16},{24,20},{28,24},{32,28},{36,32}... | collective-permute-start | bytes 184328 | tf_op jit(solution)/shard_map/ppermute | solution.py:28
  36.0 9.4 %collective-permute-start.4 = (bf16[3,1,40,256]{3,2,1,0:T(8,128)(2,1)S(1)}, bf16[3,1,40,256]{3,2,1,0:T(8,128)(2,1)S(1)}, u32[]{:S(2)}, u32[]{:S(2)}) collective-permute-start(bf16[3,1,40,256]{3,2,1,0:T(8,128)(2,1)S(1)} %get-tuple-element.60), channel_id=1, source_target_pairs={{0,4},{4,8},{8,12},{12,16},{16,20},{20,24},{24,28},{28,32},{32,36}... | collective-permute-start | bytes 184328 | tf_op jit(solution)/shard_map/ppermute | solution.py:26
  49.0 1.3 copy-start.5
  52.3 4.4 %collective-permute-start.6 = (bf16[1,4,4,256]{3,1,2,0:T(4,128)(2,1)S(1)}, bf16[1,4,4,256]{3,1,2,0:T(4,128)(2,1)S(1)}, u32[]{:S(2)}, u32[]{:S(2)}) collective-permute-start(bf16[1,4,4,256]{3,1,2,0:T(4,128)(2,1)S(1)} %get-tuple-element.98), channel_id=1, source_target_pairs={{0,1},{1,2},{2,3},{4,5},{5,6},{6,7},{8,9},{9,10},{10,11},{12,13},{... | collective-permute-start | bytes 24584 | tf_op jit(solution)/shard_map/ppermute | solution.py:26
  55.4 4.4 %collective-permute-start.7 = (bf16[1,4,4,256]{3,1,2,0:T(4,128)(2,1)S(1)}, bf16[1,4,4,256]{3,1,2,0:T(4,128)(2,1)S(1)}, u32[]{:S(2)}, u32[]{:S(2)}) collective-permute-start(bf16[1,4,4,256]{3,1,2,0:T(4,128)(2,1)S(1)} %get-tuple-element.97), channel_id=1, source_target_pairs={{1,0},{2,1},{3,2},{5,4},{6,5},{7,6},{9,8},{10,9},{11,10},{13,12},{... | collective-permute-start | bytes 24584 | tf_op jit(solution)/shard_map/ppermute | solution.py:28
  59.8 5.4 %collective-permute-start.9 = (bf16[1,4,40,256]{3,1,2,0:T(4,128)(2,1)S(1)}, bf16[1,4,40,256]{3,1,2,0:T(4,128)(2,1)S(1)}, u32[]{:S(2)}, u32[]{:S(2)}) collective-permute-start(bf16[1,4,40,256]{3,1,2,0:T(4,128)(2,1)S(1)} %constant_dynamic-update-slice_fusion.27), channel_id=1, source_target_pairs={{64,0},{128,64},{192,128},{256,192},{320,256},{384,320},{448,384},... | collective-permute-start | bytes 245768 | tf_op jit(solution)/shard_map/ppermute | solution.py:28
  61.8 6.4 %collective-permute-start.8 = (bf16[1,4,40,256]{3,1,2,0:T(4,128)(2,1)S(1)}, bf16[1,4,40,256]{3,1,2,0:T(4,128)(2,1)S(1)}, u32[]{:S(2)}, u32[]{:S(2)}) collective-permute-start(bf16[1,4,40,256]{3,1,2,0:T(4,128)(2,1)S(1)} %constant_dynamic-update-slice_fusion.27), channel_id=1, source_target_pairs={{0,64},{64,128},{128,192},{192,256},{256,320},{320,384},{384,448},... | collective-permute-start | bytes 245768 | tf_op jit(solution)/shard_map/ppermute | solution.py:26
  68.6 16.0 %collective-permute-start.11 = (bf16[3,1,40,256]{3,1,2,0:T(2,128)(2,1)S(1)}, bf16[3,1,40,256]{3,1,2,0:T(2,128)(2,1)S(1)}, u32[]{:S(2)}, u32[]{:S(2)}) collective-permute-start(bf16[3,1,40,256]{3,1,2,0:T(2,128)(2,1)S(1)} %get-tuple-element.55), channel_id=1, source_target_pairs={{4,0},{8,4},{12,8},{16,12},{20,16},{24,20},{28,24},{32,28},{36,32}... | collective-permute-start | bytes 184328 | tf_op jit(solution)/shard_map/ppermute | solution.py:28
  82.4 3.8 %collective-permute-start.10 = (bf16[3,1,40,256]{3,1,2,0:T(2,128)(2,1)S(1)}, bf16[3,1,40,256]{3,1,2,0:T(2,128)(2,1)S(1)}, u32[]{:S(2)}, u32[]{:S(2)}) collective-permute-start(bf16[3,1,40,256]{3,1,2,0:T(2,128)(2,1)S(1)} %get-tuple-element.56), channel_id=1, source_target_pairs={{0,4},{4,8},{8,12},{12,16},{16,20},{20,24},{24,28},{28,32},{32,36}... | collective-permute-start | bytes 184328 | tf_op jit(solution)/shard_map/ppermute | solution.py:26
  92.5 6.5 %collective-permute-start.13 = (bf16[1,4,4,128]{3,2,1,0:T(4,128)(2,1)S(1)}, bf16[1,4,4,128]{3,2,1,0:T(4,128)(2,1)S(1)}, u32[]{:S(2)}, u32[]{:S(2)}) collective-permute-start(bf16[1,4,4,128]{3,2,1,0:T(4,128)(2,1)S(1)} %get-tuple-element.112), channel_id=1, source_target_pairs={{1,0},{2,1},{3,2},{5,4},{6,5},{7,6},{9,8},{10,9},{11,10},{13,12},{... | collective-permute-start | bytes 12296 | tf_op jit(solution)/shard_map/ppermute | solution.py:28
  93.8 5.2 %collective-permute-start.12 = (bf16[1,4,4,128]{3,2,1,0:T(4,128)(2,1)S(1)}, bf16[1,4,4,128]{3,2,1,0:T(4,128)(2,1)S(1)}, u32[]{:S(2)}, u32[]{:S(2)}) collective-permute-start(bf16[1,4,4,128]{3,2,1,0:T(4,128)(2,1)S(1)} %get-tuple-element.111), channel_id=1, source_target_pairs={{0,1},{1,2},{2,3},{4,5},{5,6},{6,7},{8,9},{9,10},{10,11},{12,13},{... | collective-permute-start | bytes 12296 | tf_op jit(solution)/shard_map/ppermute | solution.py:26
  99.1 5.3 %collective-permute-start.15 = (bf16[1,4,40,128]{3,2,1,0:T(8,128)(2,1)S(1)}, bf16[1,4,40,128]{3,2,1,0:T(8,128)(2,1)S(1)}, u32[]{:S(2)}, u32[]{:S(2)}) collective-permute-start(bf16[1,4,40,128]{3,2,1,0:T(8,128)(2,1)S(1)} %pad_maximum_fusion.14), channel_id=1, source_target_pairs={{64,0},{128,64},{192,128},{256,192},{320,256},{384,320},{448,384},... | collective-permute-start | bytes 122888 | tf_op jit(solution)/shard_map/ppermute | solution.py:28
  101.0 6.0 %collective-permute-start.14 = (bf16[1,4,40,128]{3,2,1,0:T(8,128)(2,1)S(1)}, bf16[1,4,40,128]{3,2,1,0:T(8,128)(2,1)S(1)}, u32[]{:S(2)}, u32[]{:S(2)}) collective-permute-start(bf16[1,4,40,128]{3,2,1,0:T(8,128)(2,1)S(1)} %pad_maximum_fusion.14), channel_id=1, source_target_pairs={{0,64},{64,128},{128,192},{192,256},{256,320},{320,384},{384,448},... | collective-permute-start | bytes 122888 | tf_op jit(solution)/shard_map/ppermute | solution.py:26
  107.0 14.4 %collective-permute-start.17 = (bf16[3,1,40,128]{3,2,1,0:T(8,128)(2,1)S(1)}, bf16[3,1,40,128]{3,2,1,0:T(8,128)(2,1)S(1)}, u32[]{:S(2)}, u32[]{:S(2)}) collective-permute-start(bf16[3,1,40,128]{3,2,1,0:T(8,128)(2,1)S(1)} %get-tuple-element.81), channel_id=1, source_target_pairs={{4,0},{8,4},{12,8},{16,12},{20,16},{24,20},{28,24},{32,28},{36,32}... | collective-permute-start | bytes 92168 | tf_op jit(solution)/shard_map/ppermute | solution.py:28
  119.4 3.1 %collective-permute-start.16 = (bf16[3,1,40,128]{3,2,1,0:T(8,128)(2,1)S(1)}, bf16[3,1,40,128]{3,2,1,0:T(8,128)(2,1)S(1)}, u32[]{:S(2)}, u32[]{:S(2)}) collective-permute-start(bf16[3,1,40,128]{3,2,1,0:T(8,128)(2,1)S(1)} %get-tuple-element.82), channel_id=1, source_target_pairs={{0,4},{4,8},{8,12},{12,16},{16,20},{20,24},{24,28},{28,32},{32,36}... | collective-permute-start | bytes 92168 | tf_op jit(solution)/shard_map/ppermute | solution.py:26
  129.5 14.6 %copy-start.2 = (bf16[1,3,1024]{2,1,0:T(4,128)(2,1)S(1)}, bf16[1,3,1024]{2,1,0:T(4,128)(2,1)}, u32[]{:S(2)}) copy-start(bf16[1,3,1024]{2,1,0:T(4,128)(2,1)} %param.24) | copy-start | bytes 18436
  129.5 113.9 %all-to-all-start = ((bf16[128,2,64,128]{3,2,1,0:T(8,128)(2,1)}), bf16[128,2,64,128]{3,2,1,0:T(8,128)(2,1)}, u32[]{:S(2)}, u32[]{:S(2)}) async-start(bf16[128,2,64,128]{3,2,1,0:T(8,128)(2,1)} %bitcast.192), calls=%async_computation | async-start | bytes 8388608 | tf_op jit(solution)/shard_map/all_to_all | solution.py:216
  243.3 36.6 %copy-start.4 = (bf16[3,256]{1,0:T(4,128)(2,1)S(1)}, bf16[3,256]{1,0:T(4,128)(2,1)}, u32[]{:S(2)}) copy-start(bf16[3,256]{1,0:T(4,128)(2,1)} %param.22) | copy-start | bytes 4612
  270.3 25.6 %all-to-all-start.1 = ((f32[128,2,3]{2,1,0:T(2,128)}), f32[128,2,3]{2,1,0:T(2,128)S(1)}, u32[]{:S(2)}, u32[]{:S(2)}) async-start(f32[128,2,3]{2,1,0:T(2,128)} %bitcast.210), calls=%async_computation.1 | async-start | bytes 262144 | tf_op jit(solution)/shard_map/all_to_all | solution.py:226

commit v3 on v2

--- a/solution.py
+++ b/solution.py
@@ -102,7 +102,7 @@
 
 
 def specialist_kernel(env_ref, first_ref, head_ref, out_ref):
-    piece = 8
+    piece = 64
     slots = env_ref.shape[0] // out_ref.shape[0]
     span = piece * slots
     column = lax.broadcasted_iota(jnp.int32, (piece, span), 1)
@@ -114,7 +114,7 @@
         message = jnp.dot(
             env_ref[pl.ds(begin, span), :], first_ref[...], preferred_element_type=jnp.float32
         )
-        hidden = (message * (0.5 * jnp.tanh(0.5 * message) + 0.5)).astype(jnp.bfloat16)
+        hidden = jax.nn.silu(message).astype(jnp.bfloat16)
         pooled = jnp.dot(pool, hidden, preferred_element_type=jnp.float32)
         pooled = (pooled * (1.0 / slots)).astype(jnp.bfloat16)
         out_ref[pl.ds(pl.multiple_of(index * piece, piece), piece), :] = jnp.dot(
@@ -129,7 +129,7 @@
     sources, item_count, slots, env_width = received.shape
     env_total = sources * item_count
     hidden_width = w_first.shape[-1]
-    block = math.gcd(env_total, 32)
+    block = math.gcd(env_total, 64)
     head = jnp.zeros((hidden_width, 128), jnp.bfloat16).at[:, : w_head.shape[0]].set(w_head.T)
     results = pl.pallas_call(
         specialist_kernel,

time: 299 us -> 290 us (0.970)
  Pallas kernels: 26.9 us -> 17.6 us
    pallas_call x1, Pallas kernels: 26.9 us -> 17.6 us  [specialist(): pl.pallas_call(specialist_kernel, grid=(env_total // block,), in_specs=[p...]
where the time goes in v3:
time: 290 us; the launch traced here: 288 us
  waiting for transfers between devices  135 us (47%)
  starting transfers between devices  96.2 us (33%)
  Pallas kernels  17.6 us (6%)
  local copies, waits for them, and re-layouts  16.7 us (6%)
  matrix products  10.8 us (4%)
  other arithmetic  9.98 us (3%)
    all_to_all x1, waiting for transfers between devices, per_device(): lax.all_to_all(outgoing.reshape(owner_total, capacity, slots, env_width),...  96.9 us
    ppermute x9, starting transfers between devices, with_halo(): lax.ppermute(head, axis, [((i + 1) % count, i) for i in range(ends)])  44.9 us
    ppermute x9, starting transfers between devices, with_halo(): lax.ppermute(tail, axis, [(i, (i + 1) % count) for i in range(ends)])  27.1 us
    ppermute x9, waiting for transfers between devices, with_halo(): lax.ppermute(tail, axis, [(i, (i + 1) % count) for i in range(ends)])  19.5 us
    pallas_call x1, Pallas kernels, specialist(): pl.pallas_call(specialist_kernel, grid=(env_total // block,), in_specs=[p...  17.6 us
    all_to_all x1, waiting for transfers between devices, per_device(): lax.all_to_all(results, ('gx', 'gy'), split_axis=0, concat_axis=0, tiled=...  15.6 us
    all_to_all x1, starting transfers between devices, per_device(): lax.all_to_all(outgoing.reshape(owner_total, capacity, slots, env_width),...  14.6 us
    all_to_all x1, starting transfers between devices, per_device(): lax.all_to_all(results, ('gx', 'gy'), split_axis=0, concat_axis=0, tiled=...  9.68 us
  transfers between devices with their start and end apart: 20, of which 9 were waited for; matrix products, arithmetic and copies ran while one was open for 5% of the time, Pallas kernels for 0%

profile of v3, /device:TPU:1, one launch (start us, length us, event | category | flops | bytes accessed | tf_op | source)
XLA Modules:
  0.0 288.2 jit_solution(14325073468720569912)
XLA Ops:
  0.8 1.3 collective-permute-start.1
  2.1 5.4 %collective-permute-start = (bf16[1,4,4,256]{3,2,1,0:T(4,128)(2,1)S(1)}, bf16[1,4,4,256]{3,2,1,0:T(4,128)(2,1)S(1)}, u32[]{:S(2)}, u32[]{:S(2)}) collective-permute-start(bf16[1,4,4,256]{3,2,1,0:T(4,128)(2,1)S(1)} %get-tuple-element.101), channel_id=1, source_target_pairs={{0,1},{1,2},{2,3},{4,5},{5,6},{6,7},{8,9},{9,10},{10,11},{12,13},{... | collective-permute-start | bytes 24584 | tf_op jit(solution)/shard_map/ppermute | solution.py:26
  10.1 4.0 %iota_compare_fusion = pred[128,64,108]{2,1,0:T(8,128)(4,1)S(1)} fusion(s32[128,64]{1,0:T(8,128)} %bitcast.295), kind=kLoop, calls=%fused_computation.6 | loop fusion | flops 884736 | bytes 917504 | tf_op jit(solution)/shard_map/eq | solution.py:169
  14.9 2.8 convolution_convert_fusion.1
  18.7 5.1 %collective-permute-start.3 = (bf16[1,4,40,256]{3,2,1,0:T(8,128)(2,1)S(1)}, bf16[1,4,40,256]{3,2,1,0:T(8,128)(2,1)S(1)}, u32[]{:S(2)}, u32[]{:S(2)}) collective-permute-start(bf16[1,4,40,256]{3,2,1,0:T(8,128)(2,1)S(1)} %pad_maximum_fusion.4), channel_id=1, source_target_pairs={{64,0},{128,64},{192,128},{256,192},{320,256},{384,320},{448,384},... | collective-permute-start | bytes 245768 | tf_op jit(solution)/shard_map/ppermute | solution.py:28
  23.8 1.9 collective-permute-start.2
  25.9 4.3 %collective-permute-done.2 = bf16[1,4,40,256]{3,2,1,0:T(8,128)(2,1)S(1)} collective-permute-done((bf16[1,4,40,256]{3,2,1,0:T(8,128)(2,1)S(1)}, bf16[1,4,40,256]{3,2,1,0:T(8,128)(2,1)S(1)}, u32[]{:S(2)}, u32[]{:S(2)}) %collective-permute-start.2) | collective-permute-done | bytes 81952 | tf_op jit(solution)/shard_map/ppermute | solution.py:26
  30.2 5.8 %collective-permute-start.5 = (bf16[3,1,40,256]{3,2,1,0:T(8,128)(2,1)S(1)}, bf16[3,1,40,256]{3,2,1,0:T(8,128)(2,1)S(1)}, u32[]{:S(2)}, u32[]{:S(2)}) collective-permute-start(bf16[3,1,40,256]{3,2,1,0:T(8,128)(2,1)S(1)} %get-tuple-element.59), channel_id=1, source_target_pairs={{4,0},{8,4},{12,8},{16,12},{20,16},{24,20},{28,24},{32,28},{36,32}... | collective-permute-start | bytes 184328 | tf_op jit(solution)/shard_map/ppermute | solution.py:28
  36.0 1.9 collective-permute-start.4
  38.4 7.0 %collective-permute-done.4 = bf16[3,1,40,256]{3,2,1,0:T(8,128)(2,1)S(1)} collective-permute-done((bf16[3,1,40,256]{3,2,1,0:T(8,128)(2,1)S(1)}, bf16[3,1,40,256]{3,2,1,0:T(8,128)(2,1)S(1)}, u32[]{:S(2)}, u32[]{:S(2)}) %collective-permute-start.4) | collective-permute-done | bytes 61472 | tf_op jit(solution)/shard_map/ppermute | solution.py:26
  50.3 1.8 multiply_reduce_fusion.1
  52.3 3.1 %collective-permute-start.6 = (bf16[1,4,4,256]{3,1,2,0:T(4,128)(2,1)S(1)}, bf16[1,4,4,256]{3,1,2,0:T(4,128)(2,1)S(1)}, u32[]{:S(2)}, u32[]{:S(2)}) collective-permute-start(bf16[1,4,4,256]{3,1,2,0:T(4,128)(2,1)S(1)} %get-tuple-element.98), channel_id=1, source_target_pairs={{0,1},{1,2},{2,3},{4,5},{5,6},{6,7},{8,9},{9,10},{10,11},{12,13},{... | collective-permute-start | bytes 24584 | tf_op jit(solution)/shard_map/ppermute | solution.py:26
  56.8 3.0 %collective-permute-done.7 = bf16[1,4,4,256]{3,1,2,0:T(4,128)(2,1)S(1)} collective-permute-done((bf16[1,4,4,256]{3,1,2,0:T(4,128)(2,1)S(1)}, bf16[1,4,4,256]{3,1,2,0:T(4,128)(2,1)S(1)}, u32[]{:S(2)}, u32[]{:S(2)}) %collective-permute-start.7) | collective-permute-done | bytes 8224 | tf_op jit(solution)/shard_map/ppermute | solution.py:28
  59.8 2.0 collective-permute-start.9
  61.8 3.3 %collective-permute-start.8 = (bf16[1,4,40,256]{3,1,2,0:T(4,128)(2,1)S(1)}, bf16[1,4,40,256]{3,1,2,0:T(4,128)(2,1)S(1)}, u32[]{:S(2)}, u32[]{:S(2)}) collective-permute-start(bf16[1,4,40,256]{3,1,2,0:T(4,128)(2,1)S(1)} %constant_dynamic-update-slice_fusion.27), channel_id=1, source_target_pairs={{0,64},{64,128},{128,192},{192,256},{256,320},{320,384},{384,448},... | collective-permute-start | bytes 245768 | tf_op jit(solution)/shard_map/ppermute | solution.py:26
  65.2 3.0 %collective-permute-done.8 = bf16[1,4,40,256]{3,1,2,0:T(4,128)(2,1)S(1)} collective-permute-done((bf16[1,4,40,256]{3,1,2,0:T(4,128)(2,1)S(1)}, bf16[1,4,40,256]{3,1,2,0:T(4,128)(2,1)S(1)}, u32[]{:S(2)}, u32[]{:S(2)}) %collective-permute-start.8) | collective-permute-done | bytes 81952 | tf_op jit(solution)/shard_map/ppermute | solution.py:26
  68.6 13.8 %collective-permute-start.11 = (bf16[3,1,40,256]{3,1,2,0:T(2,128)(2,1)S(1)}, bf16[3,1,40,256]{3,1,2,0:T(2,128)(2,1)S(1)}, u32[]{:S(2)}, u32[]{:S(2)}) collective-permute-start(bf16[3,1,40,256]{3,1,2,0:T(2,128)(2,1)S(1)} %get-tuple-element.55), channel_id=1, source_target_pairs={{4,0},{8,4},{12,8},{16,12},{20,16},{24,20},{28,24},{32,28},{36,32}... | collective-permute-start | bytes 184328 | tf_op jit(solution)/shard_map/ppermute | solution.py:28
  82.4 2.1 collective-permute-start.10
  84.6 1.5 collective-permute-done.10
  90.5 1.8 multiply_reduce_fusion
  93.8 4.0 %collective-permute-start.12 = (bf16[1,4,4,128]{3,2,1,0:T(4,128)(2,1)S(1)}, bf16[1,4,4,128]{3,2,1,0:T(4,128)(2,1)S(1)}, u32[]{:S(2)}, u32[]{:S(2)}) collective-permute-start(bf16[1,4,4,128]{3,2,1,0:T(4,128)(2,1)S(1)} %get-tuple-element.111), channel_id=1, source_target_pairs={{0,1},{1,2},{2,3},{4,5},{5,6},{6,7},{8,9},{9,10},{10,11},{12,13},{... | collective-permute-start | bytes 12296 | tf_op jit(solution)/shard_map/ppermute | solution.py:26
  99.1 1.9 collective-permute-start.15
  101.0 3.4 %collective-permute-start.14 = (bf16[1,4,40,128]{3,2,1,0:T(8,128)(2,1)S(1)}, bf16[1,4,40,128]{3,2,1,0:T(8,128)(2,1)S(1)}, u32[]{:S(2)}, u32[]{:S(2)}) collective-permute-start(bf16[1,4,40,128]{3,2,1,0:T(8,128)(2,1)S(1)} %pad_maximum_fusion.14), channel_id=1, source_target_pairs={{0,64},{64,128},{128,192},{192,256},{256,320},{320,384},{384,448},... | collective-permute-start | bytes 122888 | tf_op jit(solution)/shard_map/ppermute | solution.py:26
  104.4 2.5 collective-permute-done.14
  107.0 12.4 %collective-permute-start.17 = (bf16[3,1,40,128]{3,2,1,0:T(8,128)(2,1)S(1)}, bf16[3,1,40,128]{3,2,1,0:T(8,128)(2,1)S(1)}, u32[]{:S(2)}, u32[]{:S(2)}) collective-permute-start(bf16[3,1,40,128]{3,2,1,0:T(8,128)(2,1)S(1)} %get-tuple-element.81), channel_id=1, source_target_pairs={{4,0},{8,4},{12,8},{16,12},{20,16},{24,20},{28,24},{32,28},{36,32}... | collective-permute-start | bytes 92168 | tf_op jit(solution)/shard_map/ppermute | solution.py:28
  119.4 1.9 collective-permute-start.16
  126.3 3.2 %copy.104 = bf16[32,8,64,128]{3,2,1,0:T(8,128)(2,1)} copy(bf16[32,8,64,128]{3,1,2,0:T(8,128)(2,1)S(1)} %fusion) | data formatting | bytes 8388608
  129.5 14.6 %all-to-all-start = ((bf16[128,2,64,128]{3,2,1,0:T(8,128)(2,1)}), bf16[128,2,64,128]{3,2,1,0:T(8,128)(2,1)}, u32[]{:S(2)}, u32[]{:S(2)}) async-start(bf16[128,2,64,128]{3,2,1,0:T(8,128)(2,1)} %bitcast.192), calls=%async_computation | async-start | bytes 8388608 | tf_op jit(solution)/shard_map/all_to_all | solution.py:216
  146.4 96.9 %all-to-all-done = bf16[128,2,64,128]{3,2,1,0:T(8,128)(2,1)} async-done(((bf16[128,2,64,128]{3,2,1,0:T(8,128)(2,1)}), bf16[128,2,64,128]{3,2,1,0:T(8,128)(2,1)}, u32[]{:S(2)}, u32[]{:S(2)}) %all-to-all-start) | async-done | bytes 4194336 | tf_op jit(solution)/shard_map/all_to_all | solution.py:216
  243.3 17.6 %shard_map.127 = f32[256,128]{1,0:T(8,128)} custom-call(bf16[16384,128]{1,0:T(8,128)(2,1)} %bitcast.103.env_ref, bf16[128,1024]{1,0:T(8,128)(2,1)} %bitcast.214, bf16[1024,128]{1,0:T(8,128)(2,1)} %scatter.4.head_ref), custom_call_target="tpu_custom_call" | custom-call | tf_op jit(solution)/shard_map/pallas_call | solution.py:134
  261.0 9.7 %all-to-all-start.1 = ((f32[128,2,3]{2,1,0:T(2,128)}), f32[128,2,3]{2,1,0:T(2,128)S(1)}, u32[]{:S(2)}, u32[]{:S(2)}) async-start(f32[128,2,3]{2,1,0:T(2,128)} %bitcast.210), calls=%async_computation.1 | async-start | bytes 262144 | tf_op jit(solution)/shard_map/all_to_all | solution.py:226
  271.0 15.6 %all-to-all-done.1 = f32[128,2,3]{2,1,0:T(2,128)S(1)} async-done(((f32[128,2,3]{2,1,0:T(2,128)}), f32[128,2,3]{2,1,0:T(2,128)S(1)}, u32[]{:S(2)}, u32[]{:S(2)}) %all-to-all-start.1) | async-done | bytes 3104 | tf_op jit(solution)/shard_map/all_to_all | solution.py:226
  (202 shorter events, 27.5 us)
Async XLA Ops:
  0.0 92.3 %copy-start = (bf16[256,128]{1,0:T(8,128)(2,1)S(1)}, bf16[256,128]{1,0:T(8,128)(2,1)}, u32[]{:S(2)}) copy-start(bf16[256,128]{1,0:T(8,128)(2,1)} %param.21) | copy-start | bytes 196612
  0.0 17.9 %copy-start.1 = (bf16[1,4,32,256]{3,2,1,0:T(8,128)(2,1)S(1)}, bf16[1,4,32,256]{3,2,1,0:T(8,128)(2,1)}, u32[]{:S(2)}) copy-start(bf16[1,4,32,256]{3,2,1,0:T(8,128)(2,1)} %param.15) | copy-start | bytes 196612
  0.0 17.7 %copy-start.3 = (s32[1,1,1,32,1]{3,4,2,1,0:T(1,128)S(1)}, s32[1,1,1,32,1]{3,4,2,1,0:T(1,128)}, u32[]{:S(2)}) copy-start(s32[1,1,1,32,1]{3,4,2,1,0:T(1,128)} %param.26) | copy-start | bytes 388
  0.8 17.8 %collective-permute-start.1 = (bf16[1,4,4,256]{3,2,1,0:T(4,128)(2,1)S(1)}, bf16[1,4,4,256]{3,2,1,0:T(4,128)(2,1)S(1)}, u32[]{:S(2)}, u32[]{:S(2)}) collective-permute-start(bf16[1,4,4,256]{3,2,1,0:T(4,128)(2,1)S(1)} %get-tuple-element.102), channel_id=1, source_target_pairs={{1,0},{2,1},{3,2},{5,4},{6,5},{7,6},{9,8},{10,9},{11,10},{13,12},{... | collective-permute-start | bytes 24584 | tf_op jit(solution)/shard_map/ppermute | solution.py:28
  2.1 16.5 %collective-permute-start = (bf16[1,4,4,256]{3,2,1,0:T(4,128)(2,1)S(1)}, bf16[1,4,4,256]{3,2,1,0:T(4,128)(2,1)S(1)}, u32[]{:S(2)}, u32[]{:S(2)}) collective-permute-start(bf16[1,4,4,256]{3,2,1,0:T(4,128)(2,1)S(1)} %get-tuple-element.101), channel_id=1, source_target_pairs={{0,1},{1,2},{2,3},{4,5},{5,6},{6,7},{8,9},{9,10},{10,11},{12,13},{... | collective-permute-start | bytes 24584 | tf_op jit(solution)/shard_map/ppermute | solution.py:26
  18.7 7.2 %collective-permute-start.3 = (bf16[1,4,40,256]{3,2,1,0:T(8,128)(2,1)S(1)}, bf16[1,4,40,256]{3,2,1,0:T(8,128)(2,1)S(1)}, u32[]{:S(2)}, u32[]{:S(2)}) collective-permute-start(bf16[1,4,40,256]{3,2,1,0:T(8,128)(2,1)S(1)} %pad_maximum_fusion.4), channel_id=1, source_target_pairs={{64,0},{128,64},{192,128},{256,192},{320,256},{384,320},{448,384},... | collective-permute-start | bytes 245768 | tf_op jit(solution)/shard_map/ppermute | solution.py:28
  23.8 6.4 %collective-permute-start.2 = (bf16[1,4,40,256]{3,2,1,0:T(8,128)(2,1)S(1)}, bf16[1,4,40,256]{3,2,1,0:T(8,128)(2,1)S(1)}, u32[]{:S(2)}, u32[]{:S(2)}) collective-permute-start(bf16[1,4,40,256]{3,2,1,0:T(8,128)(2,1)S(1)} %pad_maximum_fusion.4), channel_id=1, source_target_pairs={{0,64},{64,128},{128,192},{192,256},{256,320},{320,384},{384,448},... | collective-permute-start | bytes 245768 | tf_op jit(solution)/shard_map/ppermute | solution.py:26
  30.2 8.2 %collective-permute-start.5 = (bf16[3,1,40,256]{3,2,1,0:T(8,128)(2,1)S(1)}, bf16[3,1,40,256]{3,2,1,0:T(8,128)(2,1)S(1)}, u32[]{:S(2)}, u32[]{:S(2)}) collective-permute-start(bf16[3,1,40,256]{3,2,1,0:T(8,128)(2,1)S(1)} %get-tuple-element.59), channel_id=1, source_target_pairs={{4,0},{8,4},{12,8},{16,12},{20,16},{24,20},{28,24},{32,28},{36,32}... | collective-permute-start | bytes 184328 | tf_op jit(solution)/shard_map/ppermute | solution.py:28
  36.0 9.4 %collective-permute-start.4 = (bf16[3,1,40,256]{3,2,1,0:T(8,128)(2,1)S(1)}, bf16[3,1,40,256]{3,2,1,0:T(8,128)(2,1)S(1)}, u32[]{:S(2)}, u32[]{:S(2)}) collective-permute-start(bf16[3,1,40,256]{3,2,1,0:T(8,128)(2,1)S(1)} %get-tuple-element.60), channel_id=1, source_target_pairs={{0,4},{4,8},{8,12},{12,16},{16,20},{20,24},{24,28},{28,32},{32,36}... | collective-permute-start | bytes 184328 | tf_op jit(solution)/shard_map/ppermute | solution.py:26
  49.0 1.3 copy-start.5
  52.3 4.4 %collective-permute-start.6 = (bf16[1,4,4,256]{3,1,2,0:T(4,128)(2,1)S(1)}, bf16[1,4,4,256]{3,1,2,0:T(4,128)(2,1)S(1)}, u32[]{:S(2)}, u32[]{:S(2)}) collective-permute-start(bf16[1,4,4,256]{3,1,2,0:T(4,128)(2,1)S(1)} %get-tuple-element.98), channel_id=1, source_target_pairs={{0,1},{1,2},{2,3},{4,5},{5,6},{6,7},{8,9},{9,10},{10,11},{12,13},{... | collective-permute-start | bytes 24584 | tf_op jit(solution)/shard_map/ppermute | solution.py:26
  55.4 4.4 %collective-permute-start.7 = (bf16[1,4,4,256]{3,1,2,0:T(4,128)(2,1)S(1)}, bf16[1,4,4,256]{3,1,2,0:T(4,128)(2,1)S(1)}, u32[]{:S(2)}, u32[]{:S(2)}) collective-permute-start(bf16[1,4,4,256]{3,1,2,0:T(4,128)(2,1)S(1)} %get-tuple-element.97), channel_id=1, source_target_pairs={{1,0},{2,1},{3,2},{5,4},{6,5},{7,6},{9,8},{10,9},{11,10},{13,12},{... | collective-permute-start | bytes 24584 | tf_op jit(solution)/shard_map/ppermute | solution.py:28
  59.8 5.4 %collective-permute-start.9 = (bf16[1,4,40,256]{3,1,2,0:T(4,128)(2,1)S(1)}, bf16[1,4,40,256]{3,1,2,0:T(4,128)(2,1)S(1)}, u32[]{:S(2)}, u32[]{:S(2)}) collective-permute-start(bf16[1,4,40,256]{3,1,2,0:T(4,128)(2,1)S(1)} %constant_dynamic-update-slice_fusion.27), channel_id=1, source_target_pairs={{64,0},{128,64},{192,128},{256,192},{320,256},{384,320},{448,384},... | collective-permute-start | bytes 245768 | tf_op jit(solution)/shard_map/ppermute | solution.py:28
  61.8 6.4 %collective-permute-start.8 = (bf16[1,4,40,256]{3,1,2,0:T(4,128)(2,1)S(1)}, bf16[1,4,40,256]{3,1,2,0:T(4,128)(2,1)S(1)}, u32[]{:S(2)}, u32[]{:S(2)}) collective-permute-start(bf16[1,4,40,256]{3,1,2,0:T(4,128)(2,1)S(1)} %constant_dynamic-update-slice_fusion.27), channel_id=1, source_target_pairs={{0,64},{64,128},{128,192},{192,256},{256,320},{320,384},{384,448},... | collective-permute-start | bytes 245768 | tf_op jit(solution)/shard_map/ppermute | solution.py:26
  68.6 16.0 %collective-permute-start.11 = (bf16[3,1,40,256]{3,1,2,0:T(2,128)(2,1)S(1)}, bf16[3,1,40,256]{3,1,2,0:T(2,128)(2,1)S(1)}, u32[]{:S(2)}, u32[]{:S(2)}) collective-permute-start(bf16[3,1,40,256]{3,1,2,0:T(2,128)(2,1)S(1)} %get-tuple-element.55), channel_id=1, source_target_pairs={{4,0},{8,4},{12,8},{16,12},{20,16},{24,20},{28,24},{32,28},{36,32}... | collective-permute-start | bytes 184328 | tf_op jit(solution)/shard_map/ppermute | solution.py:28
  82.4 3.8 %collective-permute-start.10 = (bf16[3,1,40,256]{3,1,2,0:T(2,128)(2,1)S(1)}, bf16[3,1,40,256]{3,1,2,0:T(2,128)(2,1)S(1)}, u32[]{:S(2)}, u32[]{:S(2)}) collective-permute-start(bf16[3,1,40,256]{3,1,2,0:T(2,128)(2,1)S(1)} %get-tuple-element.56), channel_id=1, source_target_pairs={{0,4},{4,8},{8,12},{12,16},{16,20},{20,24},{24,28},{28,32},{32,36}... | collective-permute-start | bytes 184328 | tf_op jit(solution)/shard_map/ppermute | solution.py:26
  92.5 6.5 %collective-permute-start.13 = (bf16[1,4,4,128]{3,2,1,0:T(4,128)(2,1)S(1)}, bf16[1,4,4,128]{3,2,1,0:T(4,128)(2,1)S(1)}, u32[]{:S(2)}, u32[]{:S(2)}) collective-permute-start(bf16[1,4,4,128]{3,2,1,0:T(4,128)(2,1)S(1)} %get-tuple-element.112), channel_id=1, source_target_pairs={{1,0},{2,1},{3,2},{5,4},{6,5},{7,6},{9,8},{10,9},{11,10},{13,12},{... | collective-permute-start | bytes 12296 | tf_op jit(solution)/shard_map/ppermute | solution.py:28
  93.8 5.2 %collective-permute-start.12 = (bf16[1,4,4,128]{3,2,1,0:T(4,128)(2,1)S(1)}, bf16[1,4,4,128]{3,2,1,0:T(4,128)(2,1)S(1)}, u32[]{:S(2)}, u32[]{:S(2)}) collective-permute-start(bf16[1,4,4,128]{3,2,1,0:T(4,128)(2,1)S(1)} %get-tuple-element.111), channel_id=1, source_target_pairs={{0,1},{1,2},{2,3},{4,5},{5,6},{6,7},{8,9},{9,10},{10,11},{12,13},{... | collective-permute-start | bytes 12296 | tf_op jit(solution)/shard_map/ppermute | solution.py:26
  99.1 5.3 %collective-permute-start.15 = (bf16[1,4,40,128]{3,2,1,0:T(8,128)(2,1)S(1)}, bf16[1,4,40,128]{3,2,1,0:T(8,128)(2,1)S(1)}, u32[]{:S(2)}, u32[]{:S(2)}) collective-permute-start(bf16[1,4,40,128]{3,2,1,0:T(8,128)(2,1)S(1)} %pad_maximum_fusion.14), channel_id=1, source_target_pairs={{64,0},{128,64},{192,128},{256,192},{320,256},{384,320},{448,384},... | collective-permute-start | bytes 122888 | tf_op jit(solution)/shard_map/ppermute | solution.py:28
  101.0 6.0 %collective-permute-start.14 = (bf16[1,4,40,128]{3,2,1,0:T(8,128)(2,1)S(1)}, bf16[1,4,40,128]{3,2,1,0:T(8,128)(2,1)S(1)}, u32[]{:S(2)}, u32[]{:S(2)}) collective-permute-start(bf16[1,4,40,128]{3,2,1,0:T(8,128)(2,1)S(1)} %pad_maximum_fusion.14), channel_id=1, source_target_pairs={{0,64},{64,128},{128,192},{192,256},{256,320},{320,384},{384,448},... | collective-permute-start | bytes 122888 | tf_op jit(solution)/shard_map/ppermute | solution.py:26
  107.0 14.4 %collective-permute-start.17 = (bf16[3,1,40,128]{3,2,1,0:T(8,128)(2,1)S(1)}, bf16[3,1,40,128]{3,2,1,0:T(8,128)(2,1)S(1)}, u32[]{:S(2)}, u32[]{:S(2)}) collective-permute-start(bf16[3,1,40,128]{3,2,1,0:T(8,128)(2,1)S(1)} %get-tuple-element.81), channel_id=1, source_target_pairs={{4,0},{8,4},{12,8},{16,12},{20,16},{24,20},{28,24},{32,28},{36,32}... | collective-permute-start | bytes 92168 | tf_op jit(solution)/shard_map/ppermute | solution.py:28
  119.4 3.1 %collective-permute-start.16 = (bf16[3,1,40,128]{3,2,1,0:T(8,128)(2,1)S(1)}, bf16[3,1,40,128]{3,2,1,0:T(8,128)(2,1)S(1)}, u32[]{:S(2)}, u32[]{:S(2)}) collective-permute-start(bf16[3,1,40,128]{3,2,1,0:T(8,128)(2,1)S(1)} %get-tuple-element.82), channel_id=1, source_target_pairs={{0,4},{4,8},{8,12},{12,16},{16,20},{20,24},{24,28},{28,32},{32,36}... | collective-permute-start | bytes 92168 | tf_op jit(solution)/shard_map/ppermute | solution.py:26
  129.5 14.6 %copy-start.2 = (bf16[1,3,1024]{2,1,0:T(4,128)(2,1)S(1)}, bf16[1,3,1024]{2,1,0:T(4,128)(2,1)}, u32[]{:S(2)}) copy-start(bf16[1,3,1024]{2,1,0:T(4,128)(2,1)} %param.24) | copy-start | bytes 18436
  129.5 113.9 %all-to-all-start = ((bf16[128,2,64,128]{3,2,1,0:T(8,128)(2,1)}), bf16[128,2,64,128]{3,2,1,0:T(8,128)(2,1)}, u32[]{:S(2)}, u32[]{:S(2)}) async-start(bf16[128,2,64,128]{3,2,1,0:T(8,128)(2,1)} %bitcast.192), calls=%async_computation | async-start | bytes 8388608 | tf_op jit(solution)/shard_map/all_to_all | solution.py:216
  243.3 27.3 %copy-start.4 = (bf16[3,256]{1,0:T(4,128)(2,1)S(1)}, bf16[3,256]{1,0:T(4,128)(2,1)}, u32[]{:S(2)}) copy-start(bf16[3,256]{1,0:T(4,128)(2,1)} %param.22) | copy-start | bytes 4612
  261.0 25.6 %all-to-all-start.1 = ((f32[128,2,3]{2,1,0:T(2,128)}), f32[128,2,3]{2,1,0:T(2,128)S(1)}, u32[]{:S(2)}, u32[]{:S(2)}) async-start(f32[128,2,3]{2,1,0:T(2,128)} %bitcast.210), calls=%async_computation.1 | async-start | bytes 262144 | tf_op jit(solution)/shard_map/all_to_all | solution.py:226

commit v4 on v3

--- a/solution.py
+++ b/solution.py
@@ -63,8 +63,8 @@
 
 
 def ghosts(values):
-    deeper = with_halo(values, (("gz", 2),), M, False)
-    return with_halo(deeper, (("gx", 0), ("gy", 1)), 1, True)
+    wider = with_halo(values, (("gx", 0), ("gy", 1)), 1, True)
+    return with_halo(wider, (("gz", 2),), M, False)
 
 
 def candidates(padded, cells_x, cells_y, cells_z):

time: 290 us -> 287 us (0.990)
  waiting for transfers between devices: 135 us -> 126 us
  starting transfers between devices: 96.2 us -> 105 us
    ppermute x9, waiting for transfers between devices: 19.5 us -> 12.4 us  [with_halo(): lax.ppermute(tail, axis, [(i, (i + 1) % count) for i in range(ends)])]
    ppermute x9, starting transfers between devices: 44.9 us -> 51 us  [with_halo(): lax.ppermute(head, axis, [((i + 1) % count, i) for i in range(ends)])]
    all_to_all x1, starting transfers between devices: 14.6 us -> 17.6 us  [per_device(): lax.all_to_all(outgoing.reshape(owner_total, capacity, slots, env_width),...]
    unnamed x97 -> x103, local copies, waits for them, and re-layouts: 6.33 us -> 6.37 us
where the time goes in v4:
time: 287 us; the launch traced here: 286 us
  waiting for transfers between devices  126 us (44%)
  starting transfers between devices  105 us (37%)
  Pallas kernels  17.6 us (6%)
  local copies, waits for them, and re-layouts  15.1 us (5%)
  matrix products  10.8 us (4%)
  other arithmetic  9.24 us (3%)
    all_to_all x1, waiting for transfers between devices, per_device(): lax.all_to_all(outgoing.reshape(owner_total, capacity, slots, env_width),...  96.9 us
    ppermute x9, starting transfers between devices, with_halo(): lax.ppermute(head, axis, [((i + 1) % count, i) for i in range(ends)])  51 us
    ppermute x9, starting transfers between devices, with_halo(): lax.ppermute(tail, axis, [(i, (i + 1) % count) for i in range(ends)])  27.1 us
    all_to_all x1, starting transfers between devices, per_device(): lax.all_to_all(outgoing.reshape(owner_total, capacity, slots, env_width),...  17.6 us
    pallas_call x1, Pallas kernels, specialist(): pl.pallas_call(specialist_kernel, grid=(env_total // block,), in_specs=[p...  17.6 us
    all_to_all x1, waiting for transfers between devices, per_device(): lax.all_to_all(results, ('gx', 'gy'), split_axis=0, concat_axis=0, tiled=...  15.6 us
    ppermute x9, waiting for transfers between devices, with_halo(): lax.ppermute(tail, axis, [(i, (i + 1) % count) for i in range(ends)])  12.4 us
    all_to_all x1, starting transfers between devices, per_device(): lax.all_to_all(results, ('gx', 'gy'), split_axis=0, concat_axis=0, tiled=...  9.33 us
  transfers between devices with their start and end apart: 20, of which 9 were waited for; matrix products, arithmetic and copies ran while one was open for 5% of the time, Pallas kernels for 0%

profile of v4, /device:TPU:1, one launch (start us, length us, event | category | flops | bytes accessed | tf_op | source)
XLA Modules:
  0.0 285.8 jit_solution(18090692381619637863)
XLA Ops:
  0.0 4.2 %collective-permute-start = (bf16[1,4,32,256]{3,2,1,0:T(8,128)(2,1)}, bf16[1,4,32,256]{3,2,1,0:T(8,128)(2,1)S(1)}, u32[]{:S(2)}, u32[]{:S(2)}) collective-permute-start(bf16[1,4,32,256]{3,2,1,0:T(8,128)(2,1)} %param.15), channel_id=1, source_target_pairs={{0,64},{64,128},{128,192},{192,256},{256,320},{320,384},{384,448},... | collective-permute-start | bytes 196616 | tf_op jit(solution)/shard_map/ppermute | solution.py:26
  4.2 3.8 %collective-permute-start.1 = (bf16[1,4,32,256]{3,2,1,0:T(8,128)(2,1)}, bf16[1,4,32,256]{3,2,1,0:T(8,128)(2,1)S(1)}, u32[]{:S(2)}, u32[]{:S(2)}) collective-permute-start(bf16[1,4,32,256]{3,2,1,0:T(8,128)(2,1)} %param.15), channel_id=1, source_target_pairs={{64,0},{128,64},{192,128},{256,192},{320,256},{384,320},{448,384},... | collective-permute-start | bytes 196616 | tf_op jit(solution)/shard_map/ppermute | solution.py:28
  9.1 4.0 %iota_compare_fusion = pred[128,64,108]{2,1,0:T(8,128)(4,1)S(1)} fusion(s32[128,64]{1,0:T(8,128)} %bitcast.297), kind=kLoop, calls=%fused_computation.6 | loop fusion | flops 884736 | bytes 917504 | tf_op jit(solution)/shard_map/eq | solution.py:169
  13.1 2.9 convolution_convert_fusion.1
  16.1 7.9 %collective-permute-start.3 = (bf16[3,1,32,256]{3,2,1,0:T(8,128)(2,1)S(1)}, bf16[3,1,32,256]{3,2,1,0:T(8,128)(2,1)S(1)}, u32[]{:S(2)}, u32[]{:S(2)}) collective-permute-start(bf16[3,1,32,256]{3,2,1,0:T(8,128)(2,1)S(1)} %get-tuple-element.82), channel_id=1, source_target_pairs={{4,0},{8,4},{12,8},{16,12},{20,16},{24,20},{28,24},{32,28},{36,32}... | collective-permute-start | bytes 147464 | tf_op jit(solution)/shard_map/ppermute | solution.py:28
  24.1 1.9 collective-permute-start.2
  26.2 5.8 %collective-permute-done.2 = bf16[3,1,32,256]{3,2,1,0:T(8,128)(2,1)S(1)} collective-permute-done((bf16[3,1,32,256]{3,2,1,0:T(8,128)(2,1)S(1)}, bf16[3,1,32,256]{3,2,1,0:T(8,128)(2,1)S(1)}, u32[]{:S(2)}, u32[]{:S(2)}) %collective-permute-start.2) | collective-permute-done | bytes 49184 | tf_op jit(solution)/shard_map/ppermute | solution.py:26
  32.0 1.3 collective-permute-start.5
  33.3 4.0 %collective-permute-start.4 = (bf16[3,6,4,256]{3,2,1,0:T(4,128)(2,1)S(1)}, bf16[3,6,4,256]{3,2,1,0:T(4,128)(2,1)S(1)}, u32[]{:S(2)}, u32[]{:S(2)}) collective-permute-start(bf16[3,6,4,256]{3,2,1,0:T(4,128)(2,1)S(1)} %get-tuple-element.66), channel_id=1, source_target_pairs={{0,1},{1,2},{2,3},{4,5},{5,6},{6,7},{8,9},{9,10},{10,11},{12,13},{... | collective-permute-start | bytes 110600 | tf_op jit(solution)/shard_map/ppermute | solution.py:26
  43.3 1.8 multiply_reduce_fusion.1
  45.3 1.9 collective-permute-start.6
  47.3 4.6 %collective-permute-start.7 = (bf16[1,4,32,256]{3,1,2,0:T(4,128)(2,1)S(1)}, bf16[1,4,32,256]{3,1,2,0:T(4,128)(2,1)S(1)}, u32[]{:S(2)}, u32[]{:S(2)}) collective-permute-start(bf16[1,4,32,256]{3,1,2,0:T(4,128)(2,1)S(1)} %copy.82), channel_id=1, source_target_pairs={{64,0},{128,64},{192,128},{256,192},{320,256},{384,320},{448,384},... | collective-permute-start | bytes 196616 | tf_op jit(solution)/shard_map/ppermute | solution.py:28
  52.0 1.2 collective-permute-done.7
  53.4 13.0 %collective-permute-start.9 = (bf16[3,1,32,256]{3,1,2,0:T(2,128)(2,1)S(1)}, bf16[3,1,32,256]{3,1,2,0:T(2,128)(2,1)S(1)}, u32[]{:S(2)}, u32[]{:S(2)}) collective-permute-start(bf16[3,1,32,256]{3,1,2,0:T(2,128)(2,1)S(1)} %get-tuple-element.77), channel_id=1, source_target_pairs={{4,0},{8,4},{12,8},{16,12},{20,16},{24,20},{28,24},{32,28},{36,32}... | collective-permute-start | bytes 147464 | tf_op jit(solution)/shard_map/ppermute | solution.py:28
  66.4 1.9 collective-permute-start.8
  70.0 1.3 collective-permute-start.11
  71.3 4.8 %collective-permute-start.10 = (bf16[3,6,4,256]{3,1,2,0:T(8,128)(2,1)S(1)}, bf16[3,6,4,256]{3,1,2,0:T(8,128)(2,1)S(1)}, u32[]{:S(2)}, u32[]{:S(2)}) collective-permute-start(bf16[3,6,4,256]{3,1,2,0:T(8,128)(2,1)S(1)} %get-tuple-element.38), channel_id=1, source_target_pairs={{0,1},{1,2},{2,3},{4,5},{5,6},{6,7},{8,9},{9,10},{10,11},{12,13},{... | collective-permute-start | bytes 110600 | tf_op jit(solution)/shard_map/ppermute | solution.py:26
  81.7 1.8 multiply_reduce_fusion
  83.7 5.2 %collective-permute-start.13 = (bf16[1,4,32,128]{3,2,1,0:T(8,128)(2,1)S(1)}, bf16[1,4,32,128]{3,2,1,0:T(8,128)(2,1)S(1)}, u32[]{:S(2)}, u32[]{:S(2)}) collective-permute-start(bf16[1,4,32,128]{3,2,1,0:T(8,128)(2,1)S(1)} %bitcast.199), channel_id=1, source_target_pairs={{64,0},{128,64},{192,128},{256,192},{320,256},{384,320},{448,384},... | collective-permute-start | bytes 98312 | tf_op jit(solution)/shard_map/ppermute | solution.py:28
  88.9 1.9 collective-permute-start.12
  90.9 3.9 %collective-permute-done.12 = bf16[1,4,32,128]{3,2,1,0:T(8,128)(2,1)S(1)} collective-permute-done((bf16[1,4,32,128]{3,2,1,0:T(8,128)(2,1)S(1)}, bf16[1,4,32,128]{3,2,1,0:T(8,128)(2,1)S(1)}, u32[]{:S(2)}, u32[]{:S(2)}) %collective-permute-start.12) | collective-permute-done | bytes 32800 | tf_op jit(solution)/shard_map/ppermute | solution.py:26
  94.8 12.6 %collective-permute-start.15 = (bf16[3,1,32,128]{3,2,1,0:T(8,128)(2,1)S(1)}, bf16[3,1,32,128]{3,2,1,0:T(8,128)(2,1)S(1)}, u32[]{:S(2)}, u32[]{:S(2)}) collective-permute-start(bf16[3,1,32,128]{3,2,1,0:T(8,128)(2,1)S(1)} %get-tuple-element.112), channel_id=1, source_target_pairs={{4,0},{8,4},{12,8},{16,12},{20,16},{24,20},{28,24},{32,28},{36,32}... | collective-permute-start | bytes 73736 | tf_op jit(solution)/shard_map/ppermute | solution.py:28
  107.4 1.9 collective-permute-start.14
  110.6 1.3 collective-permute-start.17
  111.9 4.6 %collective-permute-start.16 = (bf16[3,6,4,128]{3,2,1,0:T(4,128)(2,1)S(1)}, bf16[3,6,4,128]{3,2,1,0:T(4,128)(2,1)S(1)}, u32[]{:S(2)}, u32[]{:S(2)}) collective-permute-start(bf16[3,6,4,128]{3,2,1,0:T(4,128)(2,1)S(1)} %get-tuple-element.104), channel_id=1, source_target_pairs={{0,1},{1,2},{2,3},{4,5},{5,6},{6,7},{8,9},{9,10},{10,11},{12,13},{... | collective-permute-start | bytes 55304 | tf_op jit(solution)/shard_map/ppermute | solution.py:26
  119.9 1.2 fusion
  121.2 3.2 %copy.102 = bf16[32,8,64,128]{3,2,1,0:T(8,128)(2,1)} copy(bf16[32,8,64,128]{3,1,2,0:T(8,128)(2,1)S(1)} %fusion) | data formatting | bytes 8388608
  124.4 17.6 %all-to-all-start = ((bf16[128,2,64,128]{3,2,1,0:T(8,128)(2,1)}), bf16[128,2,64,128]{3,2,1,0:T(8,128)(2,1)}, u32[]{:S(2)}, u32[]{:S(2)}) async-start(bf16[128,2,64,128]{3,2,1,0:T(8,128)(2,1)} %bitcast.192), calls=%async_computation | async-start | bytes 8388608 | tf_op jit(solution)/shard_map/all_to_all | solution.py:216
  144.4 96.9 %all-to-all-done = bf16[128,2,64,128]{3,2,1,0:T(8,128)(2,1)} async-done(((bf16[128,2,64,128]{3,2,1,0:T(8,128)(2,1)}), bf16[128,2,64,128]{3,2,1,0:T(8,128)(2,1)}, u32[]{:S(2)}, u32[]{:S(2)}) %all-to-all-start) | async-done | bytes 4194336 | tf_op jit(solution)/shard_map/all_to_all | solution.py:216
  241.3 17.6 %shard_map.127 = f32[256,128]{1,0:T(8,128)} custom-call(bf16[16384,128]{1,0:T(8,128)(2,1)} %bitcast.103.env_ref, bf16[128,1024]{1,0:T(8,128)(2,1)} %bitcast.217, bf16[1024,128]{1,0:T(8,128)(2,1)} %scatter.4.head_ref), custom_call_target="tpu_custom_call" | custom-call | tf_op jit(solution)/shard_map/pallas_call | solution.py:134
  258.9 9.3 %all-to-all-start.1 = ((f32[128,2,3]{2,1,0:T(2,128)}), f32[128,2,3]{2,1,0:T(2,128)S(1)}, u32[]{:S(2)}, u32[]{:S(2)}) async-start(f32[128,2,3]{2,1,0:T(2,128)} %bitcast.213), calls=%async_computation.1 | async-start | bytes 262144 | tf_op jit(solution)/shard_map/all_to_all | solution.py:226
  268.6 15.6 %all-to-all-done.1 = f32[128,2,3]{2,1,0:T(2,128)S(1)} async-done(((f32[128,2,3]{2,1,0:T(2,128)}), f32[128,2,3]{2,1,0:T(2,128)S(1)}, u32[]{:S(2)}, u32[]{:S(2)}) %all-to-all-start.1) | async-done | bytes 3104 | tf_op jit(solution)/shard_map/all_to_all | solution.py:226
  (201 shorter events, 23.0 us)
Async XLA Ops:
  0.0 83.5 %copy-start = (bf16[256,128]{1,0:T(8,128)(2,1)S(1)}, bf16[256,128]{1,0:T(8,128)(2,1)}, u32[]{:S(2)}) copy-start(bf16[256,128]{1,0:T(8,128)(2,1)} %param.21) | copy-start | bytes 196612
  0.0 16.0 %copy-start.1 = (bf16[1,4,32,256]{3,2,1,0:T(8,128)(2,1)S(1)}, bf16[1,4,32,256]{3,2,1,0:T(8,128)(2,1)}, u32[]{:S(2)}) copy-start(bf16[1,4,32,256]{3,2,1,0:T(8,128)(2,1)} %param.15) | copy-start | bytes 196612
  0.0 15.9 %copy-start.3 = (s32[1,1,1,32,1]{3,4,2,1,0:T(1,128)S(1)}, s32[1,1,1,32,1]{3,4,2,1,0:T(1,128)}, u32[]{:S(2)}) copy-start(s32[1,1,1,32,1]{3,4,2,1,0:T(1,128)} %param.26) | copy-start | bytes 388
  0.0 16.0 %collective-permute-start = (bf16[1,4,32,256]{3,2,1,0:T(8,128)(2,1)}, bf16[1,4,32,256]{3,2,1,0:T(8,128)(2,1)S(1)}, u32[]{:S(2)}, u32[]{:S(2)}) collective-permute-start(bf16[1,4,32,256]{3,2,1,0:T(8,128)(2,1)} %param.15), channel_id=1, source_target_pairs={{0,64},{64,128},{128,192},{192,256},{256,320},{320,384},{384,448},... | collective-permute-start | bytes 196616 | tf_op jit(solution)/shard_map/ppermute | solution.py:26
  4.2 11.9 %collective-permute-start.1 = (bf16[1,4,32,256]{3,2,1,0:T(8,128)(2,1)}, bf16[1,4,32,256]{3,2,1,0:T(8,128)(2,1)S(1)}, u32[]{:S(2)}, u32[]{:S(2)}) collective-permute-start(bf16[1,4,32,256]{3,2,1,0:T(8,128)(2,1)} %param.15), channel_id=1, source_target_pairs={{64,0},{128,64},{192,128},{256,192},{320,256},{384,320},{448,384},... | collective-permute-start | bytes 196616 | tf_op jit(solution)/shard_map/ppermute | solution.py:28
  9.1 16.9 %copy-start.5 = (f32[2,256]{1,0:T(2,128)S(1)}, f32[2,256]{1,0:T(2,128)}, u32[]{:S(2)}) copy-start(f32[2,256]{1,0:T(2,128)} %param.20) | copy-start | bytes 6148
  16.1 10.1 %collective-permute-start.3 = (bf16[3,1,32,256]{3,2,1,0:T(8,128)(2,1)S(1)}, bf16[3,1,32,256]{3,2,1,0:T(8,128)(2,1)S(1)}, u32[]{:S(2)}, u32[]{:S(2)}) collective-permute-start(bf16[3,1,32,256]{3,2,1,0:T(8,128)(2,1)S(1)} %get-tuple-element.82), channel_id=1, source_target_pairs={{4,0},{8,4},{12,8},{16,12},{20,16},{24,20},{28,24},{32,28},{36,32}... | collective-permute-start | bytes 147464 | tf_op jit(solution)/shard_map/ppermute | solution.py:28
  24.1 7.9 %collective-permute-start.2 = (bf16[3,1,32,256]{3,2,1,0:T(8,128)(2,1)S(1)}, bf16[3,1,32,256]{3,2,1,0:T(8,128)(2,1)S(1)}, u32[]{:S(2)}, u32[]{:S(2)}) collective-permute-start(bf16[3,1,32,256]{3,2,1,0:T(8,128)(2,1)S(1)} %get-tuple-element.81), channel_id=1, source_target_pairs={{0,4},{4,8},{8,12},{12,16},{16,20},{20,24},{24,28},{28,32},{32,36}... | collective-permute-start | bytes 147464 | tf_op jit(solution)/shard_map/ppermute | solution.py:26
  32.0 5.7 %collective-permute-start.5 = (bf16[3,6,4,256]{3,2,1,0:T(4,128)(2,1)S(1)}, bf16[3,6,4,256]{3,2,1,0:T(4,128)(2,1)S(1)}, u32[]{:S(2)}, u32[]{:S(2)}) collective-permute-start(bf16[3,6,4,256]{3,2,1,0:T(4,128)(2,1)S(1)} %get-tuple-element.65), channel_id=1, source_target_pairs={{1,0},{2,1},{3,2},{5,4},{6,5},{7,6},{9,8},{10,9},{11,10},{13,12},{... | collective-permute-start | bytes 110600 | tf_op jit(solution)/shard_map/ppermute | solution.py:28
  33.3 5.0 %collective-permute-start.4 = (bf16[3,6,4,256]{3,2,1,0:T(4,128)(2,1)S(1)}, bf16[3,6,4,256]{3,2,1,0:T(4,128)(2,1)S(1)}, u32[]{:S(2)}, u32[]{:S(2)}) collective-permute-start(bf16[3,6,4,256]{3,2,1,0:T(4,128)(2,1)S(1)} %get-tuple-element.66), channel_id=1, source_target_pairs={{0,1},{1,2},{2,3},{4,5},{5,6},{6,7},{8,9},{9,10},{10,11},{12,13},{... | collective-permute-start | bytes 110600 | tf_op jit(solution)/shard_map/ppermute | solution.py:26
  42.0 1.3 copy-start.6
  43.3 3.9 %copy-start.7 = (s32[1,1,1,32]{3,2,1,0:T(1,128)S(1)}, s32[1,1,1,32]{3,2,1,0:T(1,128)}, u32[]{:S(2)}) copy-start(s32[1,1,1,32]{3,2,1,0:T(1,128)} %param.25) | copy-start | bytes 388
  45.3 6.6 %collective-permute-start.6 = (bf16[1,4,32,256]{3,1,2,0:T(4,128)(2,1)S(1)}, bf16[1,4,32,256]{3,1,2,0:T(4,128)(2,1)S(1)}, u32[]{:S(2)}, u32[]{:S(2)}) collective-permute-start(bf16[1,4,32,256]{3,1,2,0:T(4,128)(2,1)S(1)} %copy.82), channel_id=1, source_target_pairs={{0,64},{64,128},{128,192},{192,256},{256,320},{320,384},{384,448},... | collective-permute-start | bytes 196616 | tf_op jit(solution)/shard_map/ppermute | solution.py:26
  47.3 5.9 %collective-permute-start.7 = (bf16[1,4,32,256]{3,1,2,0:T(4,128)(2,1)S(1)}, bf16[1,4,32,256]{3,1,2,0:T(4,128)(2,1)S(1)}, u32[]{:S(2)}, u32[]{:S(2)}) collective-permute-start(bf16[1,4,32,256]{3,1,2,0:T(4,128)(2,1)S(1)} %copy.82), channel_id=1, source_target_pairs={{64,0},{128,64},{192,128},{256,192},{320,256},{384,320},{448,384},... | collective-permute-start | bytes 196616 | tf_op jit(solution)/shard_map/ppermute | solution.py:28
  53.4 15.8 %collective-permute-start.9 = (bf16[3,1,32,256]{3,1,2,0:T(2,128)(2,1)S(1)}, bf16[3,1,32,256]{3,1,2,0:T(2,128)(2,1)S(1)}, u32[]{:S(2)}, u32[]{:S(2)}) collective-permute-start(bf16[3,1,32,256]{3,1,2,0:T(2,128)(2,1)S(1)} %get-tuple-element.77), channel_id=1, source_target_pairs={{4,0},{8,4},{12,8},{16,12},{20,16},{24,20},{28,24},{32,28},{36,32}... | collective-permute-start | bytes 147464 | tf_op jit(solution)/shard_map/ppermute | solution.py:28
  66.4 3.5 %collective-permute-start.8 = (bf16[3,1,32,256]{3,1,2,0:T(2,128)(2,1)S(1)}, bf16[3,1,32,256]{3,1,2,0:T(2,128)(2,1)S(1)}, u32[]{:S(2)}, u32[]{:S(2)}) collective-permute-start(bf16[3,1,32,256]{3,1,2,0:T(2,128)(2,1)S(1)} %get-tuple-element.76), channel_id=1, source_target_pairs={{0,4},{4,8},{8,12},{12,16},{16,20},{20,24},{24,28},{28,32},{32,36}... | collective-permute-start | bytes 147464 | tf_op jit(solution)/shard_map/ppermute | solution.py:26
  70.0 6.5 %collective-permute-start.11 = (bf16[3,6,4,256]{3,1,2,0:T(8,128)(2,1)S(1)}, bf16[3,6,4,256]{3,1,2,0:T(8,128)(2,1)S(1)}, u32[]{:S(2)}, u32[]{:S(2)}) collective-permute-start(bf16[3,6,4,256]{3,1,2,0:T(8,128)(2,1)S(1)} %get-tuple-element.37), channel_id=1, source_target_pairs={{1,0},{2,1},{3,2},{5,4},{6,5},{7,6},{9,8},{10,9},{11,10},{13,12},{... | collective-permute-start | bytes 110600 | tf_op jit(solution)/shard_map/ppermute | solution.py:28
  71.3 5.7 %collective-permute-start.10 = (bf16[3,6,4,256]{3,1,2,0:T(8,128)(2,1)S(1)}, bf16[3,6,4,256]{3,1,2,0:T(8,128)(2,1)S(1)}, u32[]{:S(2)}, u32[]{:S(2)}) collective-permute-start(bf16[3,6,4,256]{3,1,2,0:T(8,128)(2,1)S(1)} %get-tuple-element.38), channel_id=1, source_target_pairs={{0,1},{1,2},{2,3},{4,5},{5,6},{6,7},{8,9},{9,10},{10,11},{12,13},{... | collective-permute-start | bytes 110600 | tf_op jit(solution)/shard_map/ppermute | solution.py:26
  83.7 7.1 %collective-permute-start.13 = (bf16[1,4,32,128]{3,2,1,0:T(8,128)(2,1)S(1)}, bf16[1,4,32,128]{3,2,1,0:T(8,128)(2,1)S(1)}, u32[]{:S(2)}, u32[]{:S(2)}) collective-permute-start(bf16[1,4,32,128]{3,2,1,0:T(8,128)(2,1)S(1)} %bitcast.199), channel_id=1, source_target_pairs={{64,0},{128,64},{192,128},{256,192},{320,256},{384,320},{448,384},... | collective-permute-start | bytes 98312 | tf_op jit(solution)/shard_map/ppermute | solution.py:28
  88.9 5.9 %collective-permute-start.12 = (bf16[1,4,32,128]{3,2,1,0:T(8,128)(2,1)S(1)}, bf16[1,4,32,128]{3,2,1,0:T(8,128)(2,1)S(1)}, u32[]{:S(2)}, u32[]{:S(2)}) collective-permute-start(bf16[1,4,32,128]{3,2,1,0:T(8,128)(2,1)S(1)} %bitcast.200), channel_id=1, source_target_pairs={{0,64},{64,128},{128,192},{192,256},{256,320},{320,384},{384,448},... | collective-permute-start | bytes 98312 | tf_op jit(solution)/shard_map/ppermute | solution.py:26
  94.8 15.7 %collective-permute-start.15 = (bf16[3,1,32,128]{3,2,1,0:T(8,128)(2,1)S(1)}, bf16[3,1,32,128]{3,2,1,0:T(8,128)(2,1)S(1)}, u32[]{:S(2)}, u32[]{:S(2)}) collective-permute-start(bf16[3,1,32,128]{3,2,1,0:T(8,128)(2,1)S(1)} %get-tuple-element.112), channel_id=1, source_target_pairs={{4,0},{8,4},{12,8},{16,12},{20,16},{24,20},{28,24},{32,28},{36,32}... | collective-permute-start | bytes 73736 | tf_op jit(solution)/shard_map/ppermute | solution.py:28
  107.4 3.1 %collective-permute-start.14 = (bf16[3,1,32,128]{3,2,1,0:T(8,128)(2,1)S(1)}, bf16[3,1,32,128]{3,2,1,0:T(8,128)(2,1)S(1)}, u32[]{:S(2)}, u32[]{:S(2)}) collective-permute-start(bf16[3,1,32,128]{3,2,1,0:T(8,128)(2,1)S(1)} %get-tuple-element.111), channel_id=1, source_target_pairs={{0,4},{4,8},{8,12},{12,16},{16,20},{20,24},{24,28},{28,32},{32,36}... | collective-permute-start | bytes 73736 | tf_op jit(solution)/shard_map/ppermute | solution.py:26
  110.6 6.0 %collective-permute-start.17 = (bf16[3,6,4,128]{3,2,1,0:T(4,128)(2,1)S(1)}, bf16[3,6,4,128]{3,2,1,0:T(4,128)(2,1)S(1)}, u32[]{:S(2)}, u32[]{:S(2)}) collective-permute-start(bf16[3,6,4,128]{3,2,1,0:T(4,128)(2,1)S(1)} %get-tuple-element.103), channel_id=1, source_target_pairs={{1,0},{2,1},{3,2},{5,4},{6,5},{7,6},{9,8},{10,9},{11,10},{13,12},{... | collective-permute-start | bytes 55304 | tf_op jit(solution)/shard_map/ppermute | solution.py:28
  111.9 5.5 %collective-permute-start.16 = (bf16[3,6,4,128]{3,2,1,0:T(4,128)(2,1)S(1)}, bf16[3,6,4,128]{3,2,1,0:T(4,128)(2,1)S(1)}, u32[]{:S(2)}, u32[]{:S(2)}) collective-permute-start(bf16[3,6,4,128]{3,2,1,0:T(4,128)(2,1)S(1)} %get-tuple-element.104), channel_id=1, source_target_pairs={{0,1},{1,2},{2,3},{4,5},{5,6},{6,7},{8,9},{9,10},{10,11},{12,13},{... | collective-permute-start | bytes 55304 | tf_op jit(solution)/shard_map/ppermute | solution.py:26
  124.4 17.6 %copy-start.2 = (bf16[1,3,1024]{2,1,0:T(4,128)(2,1)S(1)}, bf16[1,3,1024]{2,1,0:T(4,128)(2,1)}, u32[]{:S(2)}) copy-start(bf16[1,3,1024]{2,1,0:T(4,128)(2,1)} %param.24) | copy-start | bytes 18436
  124.4 116.9 %all-to-all-start = ((bf16[128,2,64,128]{3,2,1,0:T(8,128)(2,1)}), bf16[128,2,64,128]{3,2,1,0:T(8,128)(2,1)}, u32[]{:S(2)}, u32[]{:S(2)}) async-start(bf16[128,2,64,128]{3,2,1,0:T(8,128)(2,1)} %bitcast.192), calls=%async_computation | async-start | bytes 8388608 | tf_op jit(solution)/shard_map/all_to_all | solution.py:216
  241.3 27.0 %copy-start.4 = (bf16[3,256]{1,0:T(4,128)(2,1)S(1)}, bf16[3,256]{1,0:T(4,128)(2,1)}, u32[]{:S(2)}) copy-start(bf16[3,256]{1,0:T(4,128)(2,1)} %param.22) | copy-start | bytes 4612
  258.9 25.3 %all-to-all-start.1 = ((f32[128,2,3]{2,1,0:T(2,128)}), f32[128,2,3]{2,1,0:T(2,128)S(1)}, u32[]{:S(2)}, u32[]{:S(2)}) async-start(f32[128,2,3]{2,1,0:T(2,128)} %bitcast.213), calls=%async_computation.1 | async-start | bytes 262144 | tf_op jit(solution)/shard_map/all_to_all | solution.py:226

commit v5 on v4

--- a/solution.py
+++ b/solution.py
@@ -63,7 +63,7 @@
 
 
 def ghosts(values):
-    wider = with_halo(values, (("gx", 0), ("gy", 1)), 1, True)
+    wider = with_halo(values, (("gy", 1), ("gx", 0)), 1, True)
     return with_halo(wider, (("gz", 2),), M, False)
 
 

time: 287 us -> 286 us (level)
  starting transfers between devices: 105 us -> 99 us
  waiting for transfers between devices: 126 us -> 130 us
    ppermute x9, starting transfers between devices: 51 us -> 44.3 us  [with_halo(): lax.ppermute(head, axis, [((i + 1) % count, i) for i in range(ends)])]
    ppermute x9, waiting for transfers between devices: 12.4 us -> 16.6 us  [with_halo(): lax.ppermute(tail, axis, [(i, (i + 1) % count) for i in range(ends)])]
    unnamed x103 -> x98, local copies, waits for them, and re-layouts: 6.37 us -> 6.27 us
  transfers between devices with their start and end apart: 20 -> 20, of which waited for: 9 -> 10; matrix products, arithmetic and copies ran while one was open for 5% -> 5% of each run, Pallas kernels for 0% -> 0%
where the time goes in v5:
time: 286 us; the launch traced here: 285 us
  waiting for transfers between devices  130 us (45%)
  starting transfers between devices  99 us (35%)
  Pallas kernels  17.6 us (6%)
  local copies, waits for them, and re-layouts  16.6 us (6%)
  matrix products  10.8 us (4%)
  other arithmetic  9.4 us (3%)
    all_to_all x1, waiting for transfers between devices, per_device(): lax.all_to_all(outgoing.reshape(owner_total, capacity, slots, env_width),...  96.9 us
    ppermute x9, starting transfers between devices, with_halo(): lax.ppermute(head, axis, [((i + 1) % count, i) for i in range(ends)])  44.3 us
    ppermute x9, starting transfers between devices, with_halo(): lax.ppermute(tail, axis, [(i, (i + 1) % count) for i in range(ends)])  28.7 us
    pallas_call x1, Pallas kernels, specialist(): pl.pallas_call(specialist_kernel, grid=(env_total // block,), in_specs=[p...  17.6 us
    ppermute x9, waiting for transfers between devices, with_halo(): lax.ppermute(tail, axis, [(i, (i + 1) % count) for i in range(ends)])  16.6 us
    all_to_all x1, starting transfers between devices, per_device(): lax.all_to_all(outgoing.reshape(owner_total, capacity, slots, env_width),...  16.4 us
    all_to_all x1, waiting for transfers between devices, per_device(): lax.all_to_all(results, ('gx', 'gy'), split_axis=0, concat_axis=0, tiled=...  15.6 us
    all_to_all x1, starting transfers between devices, per_device(): lax.all_to_all(results, ('gx', 'gy'), split_axis=0, concat_axis=0, tiled=...  9.51 us
  transfers between devices with their start and end apart: 20, of which 10 were waited for; matrix products, arithmetic and copies ran while one was open for 5% of the time, Pallas kernels for 0%

profile of v5, /device:TPU:1, one launch (start us, length us, event | category | flops | bytes accessed | tf_op | source)
XLA Modules:
  0.0 284.7 jit_solution(9633223271711139990)
XLA Ops:
  0.8 8.7 %collective-permute-start.1 = (bf16[1,1,32,256]{3,2,1,0:T(8,128)(2,1)S(1)}, bf16[1,1,32,256]{3,2,1,0:T(8,128)(2,1)S(1)}, u32[]{:S(2)}, u32[]{:S(2)}) collective-permute-start(bf16[1,1,32,256]{3,2,1,0:T(8,128)(2,1)S(1)} %get-tuple-element.102), channel_id=1, source_target_pairs={{4,0},{8,4},{12,8},{16,12},{20,16},{24,20},{28,24},{32,28},{36,32}... | collective-permute-start | bytes 49160 | tf_op jit(solution)/shard_map/ppermute | solution.py:28
  9.5 1.9 collective-permute-start
  13.3 4.0 %iota_compare_fusion = pred[128,64,108]{2,1,0:T(8,128)(4,1)S(1)} fusion(s32[128,64]{1,0:T(8,128)} %bitcast.294), kind=kLoop, calls=%fused_computation.6 | loop fusion | flops 884736 | bytes 917504 | tf_op jit(solution)/shard_map/eq | solution.py:169
  18.0 2.8 convolution_convert_fusion.1
  21.7 1.9 collective-permute-start.3
  23.7 3.4 %collective-permute-start.2 = (bf16[1,6,32,256]{3,2,1,0:T(8,128)(2,1)S(1)}, bf16[1,6,32,256]{3,2,1,0:T(8,128)(2,1)S(1)}, u32[]{:S(2)}, u32[]{:S(2)}) collective-permute-start(bf16[1,6,32,256]{3,2,1,0:T(8,128)(2,1)S(1)} %constant_dynamic-update-slice_fusion), channel_id=1, source_target_pairs={{0,64},{64,128},{128,192},{192,256},{256,320},{320,384},{384,448},... | collective-permute-start | bytes 294920 | tf_op jit(solution)/shard_map/ppermute | solution.py:26
  27.4 2.9 %collective-permute-done.2 = bf16[1,6,32,256]{3,2,1,0:T(8,128)(2,1)S(1)} collective-permute-done((bf16[1,6,32,256]{3,2,1,0:T(8,128)(2,1)S(1)}, bf16[1,6,32,256]{3,2,1,0:T(8,128)(2,1)S(1)}, u32[]{:S(2)}, u32[]{:S(2)}) %collective-permute-start.2) | collective-permute-done | bytes 98336 | tf_op jit(solution)/shard_map/ppermute | solution.py:26
  30.3 1.3 collective-permute-start.5
  31.6 4.0 %collective-permute-start.4 = (bf16[3,6,4,256]{3,2,1,0:T(4,128)(2,1)S(1)}, bf16[3,6,4,256]{3,2,1,0:T(4,128)(2,1)S(1)}, u32[]{:S(2)}, u32[]{:S(2)}) collective-permute-start(bf16[3,6,4,256]{3,2,1,0:T(4,128)(2,1)S(1)} %get-tuple-element.60), channel_id=1, source_target_pairs={{0,1},{1,2},{2,3},{4,5},{5,6},{6,7},{8,9},{9,10},{10,11},{12,13},{... | collective-permute-start | bytes 110600 | tf_op jit(solution)/shard_map/ppermute | solution.py:26
  41.5 1.8 multiply_reduce_fusion.1
  43.6 12.9 %collective-permute-start.7 = (bf16[1,1,32,256]{3,1,2,0:T(2,128)(2,1)S(1)}, bf16[1,1,32,256]{3,1,2,0:T(2,128)(2,1)S(1)}, u32[]{:S(2)}, u32[]{:S(2)}) collective-permute-start(bf16[1,1,32,256]{3,1,2,0:T(2,128)(2,1)S(1)} %get-tuple-element.98), channel_id=1, source_target_pairs={{4,0},{8,4},{12,8},{16,12},{20,16},{24,20},{28,24},{32,28},{36,32}... | collective-permute-start | bytes 49160 | tf_op jit(solution)/shard_map/ppermute | solution.py:28
  56.5 1.9 collective-permute-start.6
  58.5 5.8 %collective-permute-done.6 = bf16[1,1,32,256]{3,1,2,0:T(2,128)(2,1)S(1)} collective-permute-done((bf16[1,1,32,256]{3,1,2,0:T(2,128)(2,1)S(1)}, bf16[1,1,32,256]{3,1,2,0:T(2,128)(2,1)S(1)}, u32[]{:S(2)}, u32[]{:S(2)}) %collective-permute-start.6) | collective-permute-done | bytes 16416 | tf_op jit(solution)/shard_map/ppermute | solution.py:26
  64.4 2.1 collective-permute-start.9
  66.5 3.2 %collective-permute-start.8 = (bf16[1,6,32,256]{3,1,2,0:T(8,128)(2,1)S(1)}, bf16[1,6,32,256]{3,1,2,0:T(8,128)(2,1)S(1)}, u32[]{:S(2)}, u32[]{:S(2)}) collective-permute-start(bf16[1,6,32,256]{3,1,2,0:T(8,128)(2,1)S(1)} %pad_maximum_fusion.3), channel_id=1, source_target_pairs={{0,64},{64,128},{128,192},{192,256},{256,320},{320,384},{384,448},... | collective-permute-start | bytes 294920 | tf_op jit(solution)/shard_map/ppermute | solution.py:26
  70.4 3.0 %collective-permute-done.8 = bf16[1,6,32,256]{3,1,2,0:T(8,128)(2,1)S(1)} collective-permute-done((bf16[1,6,32,256]{3,1,2,0:T(8,128)(2,1)S(1)}, bf16[1,6,32,256]{3,1,2,0:T(8,128)(2,1)S(1)}, u32[]{:S(2)}, u32[]{:S(2)}) %collective-permute-start.8) | collective-permute-done | bytes 98336 | tf_op jit(solution)/shard_map/ppermute | solution.py:26
  73.5 1.3 collective-permute-start.11
  74.8 4.5 %collective-permute-start.10 = (bf16[3,6,4,256]{3,1,2,0:T(8,128)(2,1)S(1)}, bf16[3,6,4,256]{3,1,2,0:T(8,128)(2,1)S(1)}, u32[]{:S(2)}, u32[]{:S(2)}) collective-permute-start(bf16[3,6,4,256]{3,1,2,0:T(8,128)(2,1)S(1)} %get-tuple-element.38), channel_id=1, source_target_pairs={{0,1},{1,2},{2,3},{4,5},{5,6},{6,7},{8,9},{9,10},{10,11},{12,13},{... | collective-permute-start | bytes 110600 | tf_op jit(solution)/shard_map/ppermute | solution.py:26
  84.4 1.8 multiply_reduce_fusion
  86.5 12.9 %collective-permute-start.13 = (bf16[1,1,32,128]{3,2,1,0:T(8,128)(2,1)S(1)}, bf16[1,1,32,128]{3,2,1,0:T(8,128)(2,1)S(1)}, u32[]{:S(2)}, u32[]{:S(2)}) collective-permute-start(bf16[1,1,32,128]{3,2,1,0:T(8,128)(2,1)S(1)} %get-tuple-element.113), channel_id=1, source_target_pairs={{4,0},{8,4},{12,8},{16,12},{20,16},{24,20},{28,24},{32,28},{36,32}... | collective-permute-start | bytes 24584 | tf_op jit(solution)/shard_map/ppermute | solution.py:28
  99.3 1.9 collective-permute-start.12
  102.5 1.9 collective-permute-start.15
  104.4 3.4 %collective-permute-start.14 = (bf16[1,6,32,128]{3,2,1,0:T(8,128)(2,1)S(1)}, bf16[1,6,32,128]{3,2,1,0:T(8,128)(2,1)S(1)}, u32[]{:S(2)}, u32[]{:S(2)}) collective-permute-start(bf16[1,6,32,128]{3,2,1,0:T(8,128)(2,1)S(1)} %pad_maximum_fusion.13), channel_id=1, source_target_pairs={{0,64},{64,128},{128,192},{192,256},{256,320},{320,384},{384,448},... | collective-permute-start | bytes 147464 | tf_op jit(solution)/shard_map/ppermute | solution.py:26
  107.8 2.6 collective-permute-done.14
  110.5 1.3 collective-permute-start.17
  111.8 4.6 %collective-permute-start.16 = (bf16[3,6,4,128]{3,2,1,0:T(4,128)(2,1)S(1)}, bf16[3,6,4,128]{3,2,1,0:T(4,128)(2,1)S(1)}, u32[]{:S(2)}, u32[]{:S(2)}) collective-permute-start(bf16[3,6,4,128]{3,2,1,0:T(4,128)(2,1)S(1)} %get-tuple-element.82), channel_id=1, source_target_pairs={{0,1},{1,2},{2,3},{4,5},{5,6},{6,7},{8,9},{9,10},{10,11},{12,13},{... | collective-permute-start | bytes 55304 | tf_op jit(solution)/shard_map/ppermute | solution.py:26
  121.1 3.2 %copy.104 = bf16[32,8,64,128]{3,2,1,0:T(8,128)(2,1)} copy(bf16[32,8,64,128]{3,1,2,0:T(8,128)(2,1)S(1)} %fusion) | data formatting | bytes 8388608
  124.3 16.4 %all-to-all-start = ((bf16[128,2,64,128]{3,2,1,0:T(8,128)(2,1)}), bf16[128,2,64,128]{3,2,1,0:T(8,128)(2,1)}, u32[]{:S(2)}, u32[]{:S(2)}) async-start(bf16[128,2,64,128]{3,2,1,0:T(8,128)(2,1)} %bitcast.192), calls=%async_computation | async-start | bytes 8388608 | tf_op jit(solution)/shard_map/all_to_all | solution.py:216
  143.2 96.9 %all-to-all-done = bf16[128,2,64,128]{3,2,1,0:T(8,128)(2,1)} async-done(((bf16[128,2,64,128]{3,2,1,0:T(8,128)(2,1)}), bf16[128,2,64,128]{3,2,1,0:T(8,128)(2,1)}, u32[]{:S(2)}, u32[]{:S(2)}) %all-to-all-start) | async-done | bytes 4194336 | tf_op jit(solution)/shard_map/all_to_all | solution.py:216
  240.1 17.6 %shard_map.127 = f32[256,128]{1,0:T(8,128)} custom-call(bf16[16384,128]{1,0:T(8,128)(2,1)} %bitcast.103.env_ref, bf16[128,1024]{1,0:T(8,128)(2,1)} %bitcast.213, bf16[1024,128]{1,0:T(8,128)(2,1)} %scatter.4.head_ref), custom_call_target="tpu_custom_call" | custom-call | tf_op jit(solution)/shard_map/pallas_call | solution.py:134
  257.7 9.5 %all-to-all-start.1 = ((f32[128,2,3]{2,1,0:T(2,128)}), f32[128,2,3]{2,1,0:T(2,128)S(1)}, u32[]{:S(2)}, u32[]{:S(2)}) async-start(f32[128,2,3]{2,1,0:T(2,128)} %bitcast.208), calls=%async_computation.1 | async-start | bytes 262144 | tf_op jit(solution)/shard_map/all_to_all | solution.py:226
  267.6 15.6 %all-to-all-done.1 = f32[128,2,3]{2,1,0:T(2,128)S(1)} async-done(((f32[128,2,3]{2,1,0:T(2,128)}), f32[128,2,3]{2,1,0:T(2,128)S(1)}, u32[]{:S(2)}, u32[]{:S(2)}) %all-to-all-start.1) | async-done | bytes 3104 | tf_op jit(solution)/shard_map/all_to_all | solution.py:226
  (202 shorter events, 25.9 us)
Async XLA Ops:
  0.0 86.2 %copy-start = (bf16[256,128]{1,0:T(8,128)(2,1)S(1)}, bf16[256,128]{1,0:T(8,128)(2,1)}, u32[]{:S(2)}) copy-start(bf16[256,128]{1,0:T(8,128)(2,1)} %param.21) | copy-start | bytes 196612
  0.0 20.9 %copy-start.1 = (bf16[1,4,32,256]{3,2,1,0:T(8,128)(2,1)S(1)}, bf16[1,4,32,256]{3,2,1,0:T(8,128)(2,1)}, u32[]{:S(2)}) copy-start(bf16[1,4,32,256]{3,2,1,0:T(8,128)(2,1)} %param.15) | copy-start | bytes 196612
  0.0 20.9 %copy-start.6 = (s32[1,1,1,32]{3,2,1,0:T(1,128)S(1)}, s32[1,1,1,32]{3,2,1,0:T(1,128)}, u32[]{:S(2)}) copy-start(s32[1,1,1,32]{3,2,1,0:T(1,128)} %param.25) | copy-start | bytes 388
  0.8 20.9 %collective-permute-start.1 = (bf16[1,1,32,256]{3,2,1,0:T(8,128)(2,1)S(1)}, bf16[1,1,32,256]{3,2,1,0:T(8,128)(2,1)S(1)}, u32[]{:S(2)}, u32[]{:S(2)}) collective-permute-start(bf16[1,1,32,256]{3,2,1,0:T(8,128)(2,1)S(1)} %get-tuple-element.102), channel_id=1, source_target_pairs={{4,0},{8,4},{12,8},{16,12},{20,16},{24,20},{28,24},{32,28},{36,32}... | collective-permute-start | bytes 49160 | tf_op jit(solution)/shard_map/ppermute | solution.py:28
  9.5 12.1 %collective-permute-start = (bf16[1,1,32,256]{3,2,1,0:T(8,128)(2,1)S(1)}, bf16[1,1,32,256]{3,2,1,0:T(8,128)(2,1)S(1)}, u32[]{:S(2)}, u32[]{:S(2)}) collective-permute-start(bf16[1,1,32,256]{3,2,1,0:T(8,128)(2,1)S(1)} %get-tuple-element.103), channel_id=1, source_target_pairs={{0,4},{4,8},{8,12},{12,16},{16,20},{20,24},{24,28},{28,32},{32,36}... | collective-permute-start | bytes 49160 | tf_op jit(solution)/shard_map/ppermute | solution.py:26
  13.3 13.7 %copy-start.3 = (s32[1,1,1,32,1]{3,4,2,1,0:T(1,128)S(1)}, s32[1,1,1,32,1]{3,4,2,1,0:T(1,128)}, u32[]{:S(2)}) copy-start(s32[1,1,1,32,1]{3,4,2,1,0:T(1,128)} %param.26) | copy-start | bytes 388
  21.7 5.6 %collective-permute-start.3 = (bf16[1,6,32,256]{3,2,1,0:T(8,128)(2,1)S(1)}, bf16[1,6,32,256]{3,2,1,0:T(8,128)(2,1)S(1)}, u32[]{:S(2)}, u32[]{:S(2)}) collective-permute-start(bf16[1,6,32,256]{3,2,1,0:T(8,128)(2,1)S(1)} %constant_dynamic-update-slice_fusion), channel_id=1, source_target_pairs={{64,0},{128,64},{192,128},{256,192},{320,256},{384,320},{448,384},... | collective-permute-start | bytes 294920 | tf_op jit(solution)/shard_map/ppermute | solution.py:28
  23.7 6.6 %collective-permute-start.2 = (bf16[1,6,32,256]{3,2,1,0:T(8,128)(2,1)S(1)}, bf16[1,6,32,256]{3,2,1,0:T(8,128)(2,1)S(1)}, u32[]{:S(2)}, u32[]{:S(2)}) collective-permute-start(bf16[1,6,32,256]{3,2,1,0:T(8,128)(2,1)S(1)} %constant_dynamic-update-slice_fusion), channel_id=1, source_target_pairs={{0,64},{64,128},{128,192},{192,256},{256,320},{320,384},{384,448},... | collective-permute-start | bytes 294920 | tf_op jit(solution)/shard_map/ppermute | solution.py:26
  30.3 5.7 %collective-permute-start.5 = (bf16[3,6,4,256]{3,2,1,0:T(4,128)(2,1)S(1)}, bf16[3,6,4,256]{3,2,1,0:T(4,128)(2,1)S(1)}, u32[]{:S(2)}, u32[]{:S(2)}) collective-permute-start(bf16[3,6,4,256]{3,2,1,0:T(4,128)(2,1)S(1)} %get-tuple-element.59), channel_id=1, source_target_pairs={{1,0},{2,1},{3,2},{5,4},{6,5},{7,6},{9,8},{10,9},{11,10},{13,12},{... | collective-permute-start | bytes 110600 | tf_op jit(solution)/shard_map/ppermute | solution.py:28
  31.6 5.0 %collective-permute-start.4 = (bf16[3,6,4,256]{3,2,1,0:T(4,128)(2,1)S(1)}, bf16[3,6,4,256]{3,2,1,0:T(4,128)(2,1)S(1)}, u32[]{:S(2)}, u32[]{:S(2)}) collective-permute-start(bf16[3,6,4,256]{3,2,1,0:T(4,128)(2,1)S(1)} %get-tuple-element.60), channel_id=1, source_target_pairs={{0,1},{1,2},{2,3},{4,5},{5,6},{6,7},{8,9},{9,10},{10,11},{12,13},{... | collective-permute-start | bytes 110600 | tf_op jit(solution)/shard_map/ppermute | solution.py:26
  40.2 1.3 copy-start.5
  43.6 14.9 %collective-permute-start.7 = (bf16[1,1,32,256]{3,1,2,0:T(2,128)(2,1)S(1)}, bf16[1,1,32,256]{3,1,2,0:T(2,128)(2,1)S(1)}, u32[]{:S(2)}, u32[]{:S(2)}) collective-permute-start(bf16[1,1,32,256]{3,1,2,0:T(2,128)(2,1)S(1)} %get-tuple-element.98), channel_id=1, source_target_pairs={{4,0},{8,4},{12,8},{16,12},{20,16},{24,20},{28,24},{32,28},{36,32}... | collective-permute-start | bytes 49160 | tf_op jit(solution)/shard_map/ppermute | solution.py:28
  56.5 7.8 %collective-permute-start.6 = (bf16[1,1,32,256]{3,1,2,0:T(2,128)(2,1)S(1)}, bf16[1,1,32,256]{3,1,2,0:T(2,128)(2,1)S(1)}, u32[]{:S(2)}, u32[]{:S(2)}) collective-permute-start(bf16[1,1,32,256]{3,1,2,0:T(2,128)(2,1)S(1)} %get-tuple-element.97), channel_id=1, source_target_pairs={{0,4},{4,8},{8,12},{12,16},{16,20},{20,24},{24,28},{28,32},{32,36}... | collective-permute-start | bytes 49160 | tf_op jit(solution)/shard_map/ppermute | solution.py:26
  64.4 6.0 %collective-permute-start.9 = (bf16[1,6,32,256]{3,1,2,0:T(8,128)(2,1)S(1)}, bf16[1,6,32,256]{3,1,2,0:T(8,128)(2,1)S(1)}, u32[]{:S(2)}, u32[]{:S(2)}) collective-permute-start(bf16[1,6,32,256]{3,1,2,0:T(8,128)(2,1)S(1)} %pad_maximum_fusion.3), channel_id=1, source_target_pairs={{64,0},{128,64},{192,128},{256,192},{320,256},{384,320},{448,384},... | collective-permute-start | bytes 294920 | tf_op jit(solution)/shard_map/ppermute | solution.py:28
  66.5 6.9 %collective-permute-start.8 = (bf16[1,6,32,256]{3,1,2,0:T(8,128)(2,1)S(1)}, bf16[1,6,32,256]{3,1,2,0:T(8,128)(2,1)S(1)}, u32[]{:S(2)}, u32[]{:S(2)}) collective-permute-start(bf16[1,6,32,256]{3,1,2,0:T(8,128)(2,1)S(1)} %pad_maximum_fusion.3), channel_id=1, source_target_pairs={{0,64},{64,128},{128,192},{192,256},{256,320},{320,384},{384,448},... | collective-permute-start | bytes 294920 | tf_op jit(solution)/shard_map/ppermute | solution.py:26
  73.5 5.9 %collective-permute-start.11 = (bf16[3,6,4,256]{3,1,2,0:T(8,128)(2,1)S(1)}, bf16[3,6,4,256]{3,1,2,0:T(8,128)(2,1)S(1)}, u32[]{:S(2)}, u32[]{:S(2)}) collective-permute-start(bf16[3,6,4,256]{3,1,2,0:T(8,128)(2,1)S(1)} %get-tuple-element.37), channel_id=1, source_target_pairs={{1,0},{2,1},{3,2},{5,4},{6,5},{7,6},{9,8},{10,9},{11,10},{13,12},{... | collective-permute-start | bytes 110600 | tf_op jit(solution)/shard_map/ppermute | solution.py:28
  74.8 5.4 %collective-permute-start.10 = (bf16[3,6,4,256]{3,1,2,0:T(8,128)(2,1)S(1)}, bf16[3,6,4,256]{3,1,2,0:T(8,128)(2,1)S(1)}, u32[]{:S(2)}, u32[]{:S(2)}) collective-permute-start(bf16[3,6,4,256]{3,1,2,0:T(8,128)(2,1)S(1)} %get-tuple-element.38), channel_id=1, source_target_pairs={{0,1},{1,2},{2,3},{4,5},{5,6},{6,7},{8,9},{9,10},{10,11},{12,13},{... | collective-permute-start | bytes 110600 | tf_op jit(solution)/shard_map/ppermute | solution.py:26
  86.5 16.0 %collective-permute-start.13 = (bf16[1,1,32,128]{3,2,1,0:T(8,128)(2,1)S(1)}, bf16[1,1,32,128]{3,2,1,0:T(8,128)(2,1)S(1)}, u32[]{:S(2)}, u32[]{:S(2)}) collective-permute-start(bf16[1,1,32,128]{3,2,1,0:T(8,128)(2,1)S(1)} %get-tuple-element.113), channel_id=1, source_target_pairs={{4,0},{8,4},{12,8},{16,12},{20,16},{24,20},{28,24},{32,28},{36,32}... | collective-permute-start | bytes 24584 | tf_op jit(solution)/shard_map/ppermute | solution.py:28
  99.3 3.1 %collective-permute-start.12 = (bf16[1,1,32,128]{3,2,1,0:T(8,128)(2,1)S(1)}, bf16[1,1,32,128]{3,2,1,0:T(8,128)(2,1)S(1)}, u32[]{:S(2)}, u32[]{:S(2)}) collective-permute-start(bf16[1,1,32,128]{3,2,1,0:T(8,128)(2,1)S(1)} %get-tuple-element.112), channel_id=1, source_target_pairs={{0,4},{4,8},{8,12},{12,16},{16,20},{20,24},{24,28},{28,32},{32,36}... | collective-permute-start | bytes 24584 | tf_op jit(solution)/shard_map/ppermute | solution.py:26
  102.5 5.3 %collective-permute-start.15 = (bf16[1,6,32,128]{3,2,1,0:T(8,128)(2,1)S(1)}, bf16[1,6,32,128]{3,2,1,0:T(8,128)(2,1)S(1)}, u32[]{:S(2)}, u32[]{:S(2)}) collective-permute-start(bf16[1,6,32,128]{3,2,1,0:T(8,128)(2,1)S(1)} %pad_maximum_fusion.13), channel_id=1, source_target_pairs={{64,0},{128,64},{192,128},{256,192},{320,256},{384,320},{448,384},... | collective-permute-start | bytes 147464 | tf_op jit(solution)/shard_map/ppermute | solution.py:28
  104.4 6.0 %collective-permute-start.14 = (bf16[1,6,32,128]{3,2,1,0:T(8,128)(2,1)S(1)}, bf16[1,6,32,128]{3,2,1,0:T(8,128)(2,1)S(1)}, u32[]{:S(2)}, u32[]{:S(2)}) collective-permute-start(bf16[1,6,32,128]{3,2,1,0:T(8,128)(2,1)S(1)} %pad_maximum_fusion.13), channel_id=1, source_target_pairs={{0,64},{64,128},{128,192},{192,256},{256,320},{320,384},{384,448},... | collective-permute-start | bytes 147464 | tf_op jit(solution)/shard_map/ppermute | solution.py:26
  110.5 5.9 %collective-permute-start.17 = (bf16[3,6,4,128]{3,2,1,0:T(4,128)(2,1)S(1)}, bf16[3,6,4,128]{3,2,1,0:T(4,128)(2,1)S(1)}, u32[]{:S(2)}, u32[]{:S(2)}) collective-permute-start(bf16[3,6,4,128]{3,2,1,0:T(4,128)(2,1)S(1)} %get-tuple-element.81), channel_id=1, source_target_pairs={{1,0},{2,1},{3,2},{5,4},{6,5},{7,6},{9,8},{10,9},{11,10},{13,12},{... | collective-permute-start | bytes 55304 | tf_op jit(solution)/shard_map/ppermute | solution.py:28
  111.8 5.5 %collective-permute-start.16 = (bf16[3,6,4,128]{3,2,1,0:T(4,128)(2,1)S(1)}, bf16[3,6,4,128]{3,2,1,0:T(4,128)(2,1)S(1)}, u32[]{:S(2)}, u32[]{:S(2)}) collective-permute-start(bf16[3,6,4,128]{3,2,1,0:T(4,128)(2,1)S(1)} %get-tuple-element.82), channel_id=1, source_target_pairs={{0,1},{1,2},{2,3},{4,5},{5,6},{6,7},{8,9},{9,10},{10,11},{12,13},{... | collective-permute-start | bytes 55304 | tf_op jit(solution)/shard_map/ppermute | solution.py:26
  124.3 16.4 %copy-start.2 = (bf16[1,3,1024]{2,1,0:T(4,128)(2,1)S(1)}, bf16[1,3,1024]{2,1,0:T(4,128)(2,1)}, u32[]{:S(2)}) copy-start(bf16[1,3,1024]{2,1,0:T(4,128)(2,1)} %param.24) | copy-start | bytes 18436
  124.3 115.7 %all-to-all-start = ((bf16[128,2,64,128]{3,2,1,0:T(8,128)(2,1)}), bf16[128,2,64,128]{3,2,1,0:T(8,128)(2,1)}, u32[]{:S(2)}, u32[]{:S(2)}) async-start(bf16[128,2,64,128]{3,2,1,0:T(8,128)(2,1)} %bitcast.192), calls=%async_computation | async-start | bytes 8388608 | tf_op jit(solution)/shard_map/all_to_all | solution.py:216
  240.1 27.1 %copy-start.4 = (bf16[3,256]{1,0:T(4,128)(2,1)S(1)}, bf16[3,256]{1,0:T(4,128)(2,1)}, u32[]{:S(2)}) copy-start(bf16[3,256]{1,0:T(4,128)(2,1)} %param.22) | copy-start | bytes 4612
  257.7 25.5 %all-to-all-start.1 = ((f32[128,2,3]{2,1,0:T(2,128)}), f32[128,2,3]{2,1,0:T(2,128)S(1)}, u32[]{:S(2)}, u32[]{:S(2)}) async-start(f32[128,2,3]{2,1,0:T(2,128)} %bitcast.208), calls=%async_computation.1 | async-start | bytes 262144 | tf_op jit(solution)/shard_map/all_to_all | solution.py:226

commit v6 on v5

--- a/solution.py
+++ b/solution.py
@@ -204,12 +204,15 @@
     before = jnp.cumsum(same, axis=0) - same
     slot_index = jnp.sum(before * same, axis=1)
     target = jnp.where(live_rows, owner * capacity + slot_index, owner_total * capacity)
-    placing = (
-        jnp.arange(owner_total * capacity, dtype=jnp.int32)[:, None] == target[None, :]
-    ).astype(jnp.bfloat16)
-    outgoing = jnp.dot(
-        placing, environ.reshape(flag_total, slots * env_width), preferred_element_type=jnp.float32
-    ).astype(jnp.bfloat16)
+    source_row = (
+        jnp.full((owner_total * capacity,), flag_total, jnp.int32)
+        .at[target]
+        .set(jnp.arange(flag_total, dtype=jnp.int32), mode="drop")
+    )
+    padded_environ = jnp.concatenate(
+        [environ, jnp.zeros((1, slots, env_width), environ.dtype)], axis=0
+    )
+    outgoing = padded_environ[source_row]
     local_first = w_first[0]
     local_head = w_head[0]
     results = specialist(

time: 286 us -> 287 us (level)
    unnamed x98 -> x95, local copies, waits for them, and re-layouts: 6.27 us -> 3.04 us
    gather x0 -> x1, local copies, waits for them, and re-layouts: none -> 3.12 us  [per_device(): outgoing = padded_environ[source_row]]
  transfers between devices with their start and end apart: 20 -> 20, of which waited for: 10 -> 10; matrix products, arithmetic and copies ran while one was open for 5% -> 6% of each run, Pallas kernels for 0% -> 0%
where the time goes in v6:
time: 287 us; the launch traced here: 286 us
  waiting for transfers between devices  130 us (45%)
  starting transfers between devices  99 us (34%)
  Pallas kernels  17.6 us (6%)
  local copies, waits for them, and re-layouts  17.3 us (6%)
  other arithmetic  10.5 us (4%)
  matrix products  9.53 us (3%)
    all_to_all x1, waiting for transfers between devices, per_device(): lax.all_to_all(outgoing.reshape(owner_total, capacity, slots, env_width),...  97.1 us
    ppermute x9, starting transfers between devices, with_halo(): lax.ppermute(head, axis, [((i + 1) % count, i) for i in range(ends)])  44.3 us
    ppermute x9, starting transfers between devices, with_halo(): lax.ppermute(tail, axis, [(i, (i + 1) % count) for i in range(ends)])  28.7 us
    pallas_call x1, Pallas kernels, specialist(): pl.pallas_call(specialist_kernel, grid=(env_total // block,), in_specs=[p...  17.6 us
    ppermute x9, waiting for transfers between devices, with_halo(): lax.ppermute(tail, axis, [(i, (i + 1) % count) for i in range(ends)])  16.7 us
    all_to_all x1, starting transfers between devices, per_device(): lax.all_to_all(outgoing.reshape(owner_total, capacity, slots, env_width),...  16.4 us
    all_to_all x1, waiting for transfers between devices, per_device(): lax.all_to_all(results, ('gx', 'gy'), split_axis=0, concat_axis=0, tiled=...  15.6 us
    all_to_all x1, starting transfers between devices, per_device(): lax.all_to_all(results, ('gx', 'gy'), split_axis=0, concat_axis=0, tiled=...  9.5 us
  transfers between devices with their start and end apart: 20, of which 10 were waited for; matrix products, arithmetic and copies ran while one was open for 6% of the time, Pallas kernels for 0%

profile of v6, /device:TPU:1, one launch (start us, length us, event | category | flops | bytes accessed | tf_op | source)
XLA Modules:
  0.0 285.6 jit_solution(13820964049253004643)
XLA Ops:
  0.8 8.7 %collective-permute-start.1 = (bf16[1,1,32,256]{3,2,1,0:T(8,128)(2,1)S(1)}, bf16[1,1,32,256]{3,2,1,0:T(8,128)(2,1)S(1)}, u32[]{:S(2)}, u32[]{:S(2)}) collective-permute-start(bf16[1,1,32,256]{3,2,1,0:T(8,128)(2,1)S(1)} %get-tuple-element.104), channel_id=1, source_target_pairs={{4,0},{8,4},{12,8},{16,12},{20,16},{24,20},{28,24},{32,28},{36,32}... | collective-permute-start | bytes 49160 | tf_op jit(solution)/shard_map/ppermute | solution.py:28
  9.5 1.9 collective-permute-start
  14.0 4.0 %iota_compare_fusion = pred[128,64,108]{2,1,0:T(8,128)(4,1)S(1)} fusion(s32[128,64]{1,0:T(8,128)} %bitcast.284), kind=kLoop, calls=%fused_computation.7 | loop fusion | flops 884736 | bytes 917504 | tf_op jit(solution)/shard_map/eq | solution.py:169
  20.3 2.9 convolution_convert_fusion
  23.9 1.9 collective-permute-start.3
  25.8 3.4 %collective-permute-start.2 = (bf16[1,6,32,256]{3,2,1,0:T(8,128)(2,1)S(1)}, bf16[1,6,32,256]{3,2,1,0:T(8,128)(2,1)S(1)}, u32[]{:S(2)}, u32[]{:S(2)}) collective-permute-start(bf16[1,6,32,256]{3,2,1,0:T(8,128)(2,1)S(1)} %constant_dynamic-update-slice_fusion), channel_id=1, source_target_pairs={{0,64},{64,128},{128,192},{192,256},{256,320},{320,384},{384,448},... | collective-permute-start | bytes 294920 | tf_op jit(solution)/shard_map/ppermute | solution.py:26
  29.4 3.0 %collective-permute-done.2 = bf16[1,6,32,256]{3,2,1,0:T(8,128)(2,1)S(1)} collective-permute-done((bf16[1,6,32,256]{3,2,1,0:T(8,128)(2,1)S(1)}, bf16[1,6,32,256]{3,2,1,0:T(8,128)(2,1)S(1)}, u32[]{:S(2)}, u32[]{:S(2)}) %collective-permute-start.2) | collective-permute-done | bytes 98336 | tf_op jit(solution)/shard_map/ppermute | solution.py:26
  32.5 1.3 collective-permute-start.5
  33.8 4.0 %collective-permute-start.4 = (bf16[3,6,4,256]{3,2,1,0:T(4,128)(2,1)S(1)}, bf16[3,6,4,256]{3,2,1,0:T(4,128)(2,1)S(1)}, u32[]{:S(2)}, u32[]{:S(2)}) collective-permute-start(bf16[3,6,4,256]{3,2,1,0:T(4,128)(2,1)S(1)} %get-tuple-element.62), channel_id=1, source_target_pairs={{0,1},{1,2},{2,3},{4,5},{5,6},{6,7},{8,9},{9,10},{10,11},{12,13},{... | collective-permute-start | bytes 110600 | tf_op jit(solution)/shard_map/ppermute | solution.py:26
  43.8 1.8 multiply_reduce_fusion.1
  45.8 12.9 %collective-permute-start.7 = (bf16[1,1,32,256]{3,1,2,0:T(2,128)(2,1)S(1)}, bf16[1,1,32,256]{3,1,2,0:T(2,128)(2,1)S(1)}, u32[]{:S(2)}, u32[]{:S(2)}) collective-permute-start(bf16[1,1,32,256]{3,1,2,0:T(2,128)(2,1)S(1)} %get-tuple-element.100), channel_id=1, source_target_pairs={{4,0},{8,4},{12,8},{16,12},{20,16},{24,20},{28,24},{32,28},{36,32}... | collective-permute-start | bytes 49160 | tf_op jit(solution)/shard_map/ppermute | solution.py:28
  58.7 1.9 collective-permute-start.6
  60.7 5.8 %collective-permute-done.6 = bf16[1,1,32,256]{3,1,2,0:T(2,128)(2,1)S(1)} collective-permute-done((bf16[1,1,32,256]{3,1,2,0:T(2,128)(2,1)S(1)}, bf16[1,1,32,256]{3,1,2,0:T(2,128)(2,1)S(1)}, u32[]{:S(2)}, u32[]{:S(2)}) %collective-permute-start.6) | collective-permute-done | bytes 16416 | tf_op jit(solution)/shard_map/ppermute | solution.py:26
  66.7 2.1 collective-permute-start.9
  68.7 3.2 %collective-permute-start.8 = (bf16[1,6,32,256]{3,1,2,0:T(8,128)(2,1)S(1)}, bf16[1,6,32,256]{3,1,2,0:T(8,128)(2,1)S(1)}, u32[]{:S(2)}, u32[]{:S(2)}) collective-permute-start(bf16[1,6,32,256]{3,1,2,0:T(8,128)(2,1)S(1)} %pad_maximum_fusion.3), channel_id=1, source_target_pairs={{0,64},{64,128},{128,192},{192,256},{256,320},{320,384},{384,448},... | collective-permute-start | bytes 294920 | tf_op jit(solution)/shard_map/ppermute | solution.py:26
  72.7 3.0 %collective-permute-done.8 = bf16[1,6,32,256]{3,1,2,0:T(8,128)(2,1)S(1)} collective-permute-done((bf16[1,6,32,256]{3,1,2,0:T(8,128)(2,1)S(1)}, bf16[1,6,32,256]{3,1,2,0:T(8,128)(2,1)S(1)}, u32[]{:S(2)}, u32[]{:S(2)}) %collective-permute-start.8) | collective-permute-done | bytes 98336 | tf_op jit(solution)/shard_map/ppermute | solution.py:26
  75.7 1.3 collective-permute-start.11
  77.0 4.5 %collective-permute-start.10 = (bf16[3,6,4,256]{3,1,2,0:T(8,128)(2,1)S(1)}, bf16[3,6,4,256]{3,1,2,0:T(8,128)(2,1)S(1)}, u32[]{:S(2)}, u32[]{:S(2)}) collective-permute-start(bf16[3,6,4,256]{3,1,2,0:T(8,128)(2,1)S(1)} %get-tuple-element.40), channel_id=1, source_target_pairs={{0,1},{1,2},{2,3},{4,5},{5,6},{6,7},{8,9},{9,10},{10,11},{12,13},{... | collective-permute-start | bytes 110600 | tf_op jit(solution)/shard_map/ppermute | solution.py:26
  86.7 1.8 multiply_reduce_fusion
  88.8 12.9 %collective-permute-start.13 = (bf16[1,1,32,128]{3,2,1,0:T(8,128)(2,1)S(1)}, bf16[1,1,32,128]{3,2,1,0:T(8,128)(2,1)S(1)}, u32[]{:S(2)}, u32[]{:S(2)}) collective-permute-start(bf16[1,1,32,128]{3,2,1,0:T(8,128)(2,1)S(1)} %get-tuple-element.115), channel_id=1, source_target_pairs={{4,0},{8,4},{12,8},{16,12},{20,16},{24,20},{28,24},{32,28},{36,32}... | collective-permute-start | bytes 24584 | tf_op jit(solution)/shard_map/ppermute | solution.py:28
  101.6 1.9 collective-permute-start.12
  104.8 1.9 collective-permute-start.15
  106.7 3.4 %collective-permute-start.14 = (bf16[1,6,32,128]{3,2,1,0:T(8,128)(2,1)S(1)}, bf16[1,6,32,128]{3,2,1,0:T(8,128)(2,1)S(1)}, u32[]{:S(2)}, u32[]{:S(2)}) collective-permute-start(bf16[1,6,32,128]{3,2,1,0:T(8,128)(2,1)S(1)} %pad_maximum_fusion.13), channel_id=1, source_target_pairs={{0,64},{64,128},{128,192},{192,256},{256,320},{320,384},{384,448},... | collective-permute-start | bytes 147464 | tf_op jit(solution)/shard_map/ppermute | solution.py:26
  110.1 2.6 collective-permute-done.14
  112.8 1.3 collective-permute-start.17
  114.1 4.6 %collective-permute-start.16 = (bf16[3,6,4,128]{3,2,1,0:T(4,128)(2,1)S(1)}, bf16[3,6,4,128]{3,2,1,0:T(4,128)(2,1)S(1)}, u32[]{:S(2)}, u32[]{:S(2)}) collective-permute-start(bf16[3,6,4,128]{3,2,1,0:T(4,128)(2,1)S(1)} %get-tuple-element.84), channel_id=1, source_target_pairs={{0,1},{1,2},{2,3},{4,5},{5,6},{6,7},{8,9},{9,10},{10,11},{12,13},{... | collective-permute-start | bytes 55304 | tf_op jit(solution)/shard_map/ppermute | solution.py:26
  122.2 3.1 %gather_fusion.3 = bf16[256,64,128]{2,1,0:T(8,128)(2,1)} fusion(bf16[33,64,128]{2,1,0:T(8,128)(2,1)S(1)} %concatenate.128, s32[1024]{0:T(1024)S(1)} %pad_clamp_fusion.1), kind=kCustom, calls=%fused_computation.3 | custom fusion | bytes 8389632 | tf_op jit(solution)/shard_map/gather | solution.py:215
  125.3 16.4 %all-to-all-start = ((bf16[128,2,64,128]{3,2,1,0:T(8,128)(2,1)}), bf16[128,2,64,128]{3,2,1,0:T(8,128)(2,1)}, u32[]{:S(2)}, u32[]{:S(2)}) async-start(bf16[128,2,64,128]{3,2,1,0:T(8,128)(2,1)} %bitcast.183), calls=%async_computation | async-start | bytes 8388608 | tf_op jit(solution)/shard_map/all_to_all | solution.py:219
  144.0 97.1 %all-to-all-done = bf16[128,2,64,128]{3,2,1,0:T(8,128)(2,1)} async-done(((bf16[128,2,64,128]{3,2,1,0:T(8,128)(2,1)}), bf16[128,2,64,128]{3,2,1,0:T(8,128)(2,1)}, u32[]{:S(2)}, u32[]{:S(2)}) %all-to-all-start) | async-done | bytes 4194336 | tf_op jit(solution)/shard_map/all_to_all | solution.py:219
  241.0 17.6 %shard_map.127 = f32[256,128]{1,0:T(8,128)} custom-call(bf16[16384,128]{1,0:T(8,128)(2,1)} %bitcast.107.env_ref, bf16[128,1024]{1,0:T(8,128)(2,1)} %bitcast.203, bf16[1024,128]{1,0:T(8,128)(2,1)} %scatter.13.head_ref), custom_call_target="tpu_custom_call" | custom-call | tf_op jit(solution)/shard_map/pallas_call | solution.py:134
  258.7 9.5 %all-to-all-start.1 = ((f32[128,2,3]{2,1,0:T(2,128)}), f32[128,2,3]{2,1,0:T(2,128)S(1)}, u32[]{:S(2)}, u32[]{:S(2)}) async-start(f32[128,2,3]{2,1,0:T(2,128)} %bitcast.198), calls=%async_computation.1 | async-start | bytes 262144 | tf_op jit(solution)/shard_map/all_to_all | solution.py:229
  268.5 15.6 %all-to-all-done.1 = f32[128,2,3]{2,1,0:T(2,128)S(1)} async-done(((f32[128,2,3]{2,1,0:T(2,128)}), f32[128,2,3]{2,1,0:T(2,128)S(1)}, u32[]{:S(2)}, u32[]{:S(2)}) %all-to-all-start.1) | async-done | bytes 3104 | tf_op jit(solution)/shard_map/all_to_all | solution.py:229
  (204 shorter events, 26.6 us)
Async XLA Ops:
  0.0 88.5 %copy-start = (bf16[256,128]{1,0:T(8,128)(2,1)S(1)}, bf16[256,128]{1,0:T(8,128)(2,1)}, u32[]{:S(2)}) copy-start(bf16[256,128]{1,0:T(8,128)(2,1)} %param.21) | copy-start | bytes 196612
  0.0 23.9 %copy-start.1 = (bf16[1,4,32,256]{3,2,1,0:T(8,128)(2,1)S(1)}, bf16[1,4,32,256]{3,2,1,0:T(8,128)(2,1)}, u32[]{:S(2)}) copy-start(bf16[1,4,32,256]{3,2,1,0:T(8,128)(2,1)} %param.15) | copy-start | bytes 196612
  0.8 23.1 %collective-permute-start.1 = (bf16[1,1,32,256]{3,2,1,0:T(8,128)(2,1)S(1)}, bf16[1,1,32,256]{3,2,1,0:T(8,128)(2,1)S(1)}, u32[]{:S(2)}, u32[]{:S(2)}) collective-permute-start(bf16[1,1,32,256]{3,2,1,0:T(8,128)(2,1)S(1)} %get-tuple-element.104), channel_id=1, source_target_pairs={{4,0},{8,4},{12,8},{16,12},{20,16},{24,20},{28,24},{32,28},{36,32}... | collective-permute-start | bytes 49160 | tf_op jit(solution)/shard_map/ppermute | solution.py:28
  9.5 14.3 %collective-permute-start = (bf16[1,1,32,256]{3,2,1,0:T(8,128)(2,1)S(1)}, bf16[1,1,32,256]{3,2,1,0:T(8,128)(2,1)S(1)}, u32[]{:S(2)}, u32[]{:S(2)}) collective-permute-start(bf16[1,1,32,256]{3,2,1,0:T(8,128)(2,1)S(1)} %get-tuple-element.105), channel_id=1, source_target_pairs={{0,4},{4,8},{8,12},{12,16},{16,20},{20,24},{24,28},{28,32},{32,36}... | collective-permute-start | bytes 49160 | tf_op jit(solution)/shard_map/ppermute | solution.py:26
  14.0 15.3 %copy-start.5 = (s32[1,1,1,32]{3,2,1,0:T(1,128)S(1)}, s32[1,1,1,32]{3,2,1,0:T(1,128)}, u32[]{:S(2)}) copy-start(s32[1,1,1,32]{3,2,1,0:T(1,128)} %param.25) | copy-start | bytes 388
  23.9 5.5 %collective-permute-start.3 = (bf16[1,6,32,256]{3,2,1,0:T(8,128)(2,1)S(1)}, bf16[1,6,32,256]{3,2,1,0:T(8,128)(2,1)S(1)}, u32[]{:S(2)}, u32[]{:S(2)}) collective-permute-start(bf16[1,6,32,256]{3,2,1,0:T(8,128)(2,1)S(1)} %constant_dynamic-update-slice_fusion), channel_id=1, source_target_pairs={{64,0},{128,64},{192,128},{256,192},{320,256},{384,320},{448,384},... | collective-permute-start | bytes 294920 | tf_op jit(solution)/shard_map/ppermute | solution.py:28
  25.8 6.6 %collective-permute-start.2 = (bf16[1,6,32,256]{3,2,1,0:T(8,128)(2,1)S(1)}, bf16[1,6,32,256]{3,2,1,0:T(8,128)(2,1)S(1)}, u32[]{:S(2)}, u32[]{:S(2)}) collective-permute-start(bf16[1,6,32,256]{3,2,1,0:T(8,128)(2,1)S(1)} %constant_dynamic-update-slice_fusion), channel_id=1, source_target_pairs={{0,64},{64,128},{128,192},{192,256},{256,320},{320,384},{384,448},... | collective-permute-start | bytes 294920 | tf_op jit(solution)/shard_map/ppermute | solution.py:26
  32.5 5.7 %collective-permute-start.5 = (bf16[3,6,4,256]{3,2,1,0:T(4,128)(2,1)S(1)}, bf16[3,6,4,256]{3,2,1,0:T(4,128)(2,1)S(1)}, u32[]{:S(2)}, u32[]{:S(2)}) collective-permute-start(bf16[3,6,4,256]{3,2,1,0:T(4,128)(2,1)S(1)} %get-tuple-element.61), channel_id=1, source_target_pairs={{1,0},{2,1},{3,2},{5,4},{6,5},{7,6},{9,8},{10,9},{11,10},{13,12},{... | collective-permute-start | bytes 110600 | tf_op jit(solution)/shard_map/ppermute | solution.py:28
  33.8 5.0 %collective-permute-start.4 = (bf16[3,6,4,256]{3,2,1,0:T(4,128)(2,1)S(1)}, bf16[3,6,4,256]{3,2,1,0:T(4,128)(2,1)S(1)}, u32[]{:S(2)}, u32[]{:S(2)}) collective-permute-start(bf16[3,6,4,256]{3,2,1,0:T(4,128)(2,1)S(1)} %get-tuple-element.62), channel_id=1, source_target_pairs={{0,1},{1,2},{2,3},{4,5},{5,6},{6,7},{8,9},{9,10},{10,11},{12,13},{... | collective-permute-start | bytes 110600 | tf_op jit(solution)/shard_map/ppermute | solution.py:26
  42.5 1.3 copy-start.4
  45.8 14.9 %collective-permute-start.7 = (bf16[1,1,32,256]{3,1,2,0:T(2,128)(2,1)S(1)}, bf16[1,1,32,256]{3,1,2,0:T(2,128)(2,1)S(1)}, u32[]{:S(2)}, u32[]{:S(2)}) collective-permute-start(bf16[1,1,32,256]{3,1,2,0:T(2,128)(2,1)S(1)} %get-tuple-element.100), channel_id=1, source_target_pairs={{4,0},{8,4},{12,8},{16,12},{20,16},{24,20},{28,24},{32,28},{36,32}... | collective-permute-start | bytes 49160 | tf_op jit(solution)/shard_map/ppermute | solution.py:28
  58.7 7.8 %collective-permute-start.6 = (bf16[1,1,32,256]{3,1,2,0:T(2,128)(2,1)S(1)}, bf16[1,1,32,256]{3,1,2,0:T(2,128)(2,1)S(1)}, u32[]{:S(2)}, u32[]{:S(2)}) collective-permute-start(bf16[1,1,32,256]{3,1,2,0:T(2,128)(2,1)S(1)} %get-tuple-element.99), channel_id=1, source_target_pairs={{0,4},{4,8},{8,12},{12,16},{16,20},{20,24},{24,28},{28,32},{32,36}... | collective-permute-start | bytes 49160 | tf_op jit(solution)/shard_map/ppermute | solution.py:26
  66.7 6.0 %collective-permute-start.9 = (bf16[1,6,32,256]{3,1,2,0:T(8,128)(2,1)S(1)}, bf16[1,6,32,256]{3,1,2,0:T(8,128)(2,1)S(1)}, u32[]{:S(2)}, u32[]{:S(2)}) collective-permute-start(bf16[1,6,32,256]{3,1,2,0:T(8,128)(2,1)S(1)} %pad_maximum_fusion.3), channel_id=1, source_target_pairs={{64,0},{128,64},{192,128},{256,192},{320,256},{384,320},{448,384},... | collective-permute-start | bytes 294920 | tf_op jit(solution)/shard_map/ppermute | solution.py:28
  68.7 6.9 %collective-permute-start.8 = (bf16[1,6,32,256]{3,1,2,0:T(8,128)(2,1)S(1)}, bf16[1,6,32,256]{3,1,2,0:T(8,128)(2,1)S(1)}, u32[]{:S(2)}, u32[]{:S(2)}) collective-permute-start(bf16[1,6,32,256]{3,1,2,0:T(8,128)(2,1)S(1)} %pad_maximum_fusion.3), channel_id=1, source_target_pairs={{0,64},{64,128},{128,192},{192,256},{256,320},{320,384},{384,448},... | collective-permute-start | bytes 294920 | tf_op jit(solution)/shard_map/ppermute | solution.py:26
  75.7 5.9 %collective-permute-start.11 = (bf16[3,6,4,256]{3,1,2,0:T(8,128)(2,1)S(1)}, bf16[3,6,4,256]{3,1,2,0:T(8,128)(2,1)S(1)}, u32[]{:S(2)}, u32[]{:S(2)}) collective-permute-start(bf16[3,6,4,256]{3,1,2,0:T(8,128)(2,1)S(1)} %get-tuple-element.39), channel_id=1, source_target_pairs={{1,0},{2,1},{3,2},{5,4},{6,5},{7,6},{9,8},{10,9},{11,10},{13,12},{... | collective-permute-start | bytes 110600 | tf_op jit(solution)/shard_map/ppermute | solution.py:28
  77.0 5.4 %collective-permute-start.10 = (bf16[3,6,4,256]{3,1,2,0:T(8,128)(2,1)S(1)}, bf16[3,6,4,256]{3,1,2,0:T(8,128)(2,1)S(1)}, u32[]{:S(2)}, u32[]{:S(2)}) collective-permute-start(bf16[3,6,4,256]{3,1,2,0:T(8,128)(2,1)S(1)} %get-tuple-element.40), channel_id=1, source_target_pairs={{0,1},{1,2},{2,3},{4,5},{5,6},{6,7},{8,9},{9,10},{10,11},{12,13},{... | collective-permute-start | bytes 110600 | tf_op jit(solution)/shard_map/ppermute | solution.py:26
  88.8 16.0 %collective-permute-start.13 = (bf16[1,1,32,128]{3,2,1,0:T(8,128)(2,1)S(1)}, bf16[1,1,32,128]{3,2,1,0:T(8,128)(2,1)S(1)}, u32[]{:S(2)}, u32[]{:S(2)}) collective-permute-start(bf16[1,1,32,128]{3,2,1,0:T(8,128)(2,1)S(1)} %get-tuple-element.115), channel_id=1, source_target_pairs={{4,0},{8,4},{12,8},{16,12},{20,16},{24,20},{28,24},{32,28},{36,32}... | collective-permute-start | bytes 24584 | tf_op jit(solution)/shard_map/ppermute | solution.py:28
  101.6 3.1 %collective-permute-start.12 = (bf16[1,1,32,128]{3,2,1,0:T(8,128)(2,1)S(1)}, bf16[1,1,32,128]{3,2,1,0:T(8,128)(2,1)S(1)}, u32[]{:S(2)}, u32[]{:S(2)}) collective-permute-start(bf16[1,1,32,128]{3,2,1,0:T(8,128)(2,1)S(1)} %get-tuple-element.114), channel_id=1, source_target_pairs={{0,4},{4,8},{8,12},{12,16},{16,20},{20,24},{24,28},{28,32},{32,36}... | collective-permute-start | bytes 24584 | tf_op jit(solution)/shard_map/ppermute | solution.py:26
  104.8 5.3 %collective-permute-start.15 = (bf16[1,6,32,128]{3,2,1,0:T(8,128)(2,1)S(1)}, bf16[1,6,32,128]{3,2,1,0:T(8,128)(2,1)S(1)}, u32[]{:S(2)}, u32[]{:S(2)}) collective-permute-start(bf16[1,6,32,128]{3,2,1,0:T(8,128)(2,1)S(1)} %pad_maximum_fusion.13), channel_id=1, source_target_pairs={{64,0},{128,64},{192,128},{256,192},{320,256},{384,320},{448,384},... | collective-permute-start | bytes 147464 | tf_op jit(solution)/shard_map/ppermute | solution.py:28
  106.7 6.0 %collective-permute-start.14 = (bf16[1,6,32,128]{3,2,1,0:T(8,128)(2,1)S(1)}, bf16[1,6,32,128]{3,2,1,0:T(8,128)(2,1)S(1)}, u32[]{:S(2)}, u32[]{:S(2)}) collective-permute-start(bf16[1,6,32,128]{3,2,1,0:T(8,128)(2,1)S(1)} %pad_maximum_fusion.13), channel_id=1, source_target_pairs={{0,64},{64,128},{128,192},{192,256},{256,320},{320,384},{384,448},... | collective-permute-start | bytes 147464 | tf_op jit(solution)/shard_map/ppermute | solution.py:26
  112.8 5.9 %collective-permute-start.17 = (bf16[3,6,4,128]{3,2,1,0:T(4,128)(2,1)S(1)}, bf16[3,6,4,128]{3,2,1,0:T(4,128)(2,1)S(1)}, u32[]{:S(2)}, u32[]{:S(2)}) collective-permute-start(bf16[3,6,4,128]{3,2,1,0:T(4,128)(2,1)S(1)} %get-tuple-element.83), channel_id=1, source_target_pairs={{1,0},{2,1},{3,2},{5,4},{6,5},{7,6},{9,8},{10,9},{11,10},{13,12},{... | collective-permute-start | bytes 55304 | tf_op jit(solution)/shard_map/ppermute | solution.py:28
  114.1 5.5 %collective-permute-start.16 = (bf16[3,6,4,128]{3,2,1,0:T(4,128)(2,1)S(1)}, bf16[3,6,4,128]{3,2,1,0:T(4,128)(2,1)S(1)}, u32[]{:S(2)}, u32[]{:S(2)}) collective-permute-start(bf16[3,6,4,128]{3,2,1,0:T(4,128)(2,1)S(1)} %get-tuple-element.84), channel_id=1, source_target_pairs={{0,1},{1,2},{2,3},{4,5},{5,6},{6,7},{8,9},{9,10},{10,11},{12,13},{... | collective-permute-start | bytes 55304 | tf_op jit(solution)/shard_map/ppermute | solution.py:26
  125.3 16.4 %copy-start.2 = (bf16[1,3,1024]{2,1,0:T(4,128)(2,1)S(1)}, bf16[1,3,1024]{2,1,0:T(4,128)(2,1)}, u32[]{:S(2)}) copy-start(bf16[1,3,1024]{2,1,0:T(4,128)(2,1)} %param.24) | copy-start | bytes 18436
  125.3 115.8 %all-to-all-start = ((bf16[128,2,64,128]{3,2,1,0:T(8,128)(2,1)}), bf16[128,2,64,128]{3,2,1,0:T(8,128)(2,1)}, u32[]{:S(2)}, u32[]{:S(2)}) async-start(bf16[128,2,64,128]{3,2,1,0:T(8,128)(2,1)} %bitcast.183), calls=%async_computation | async-start | bytes 8388608 | tf_op jit(solution)/shard_map/all_to_all | solution.py:219
  241.0 27.1 %copy-start.3 = (bf16[3,256]{1,0:T(4,128)(2,1)S(1)}, bf16[3,256]{1,0:T(4,128)(2,1)}, u32[]{:S(2)}) copy-start(bf16[3,256]{1,0:T(4,128)(2,1)} %param.22) | copy-start | bytes 4612
  258.7 25.4 %all-to-all-start.1 = ((f32[128,2,3]{2,1,0:T(2,128)}), f32[128,2,3]{2,1,0:T(2,128)S(1)}, u32[]{:S(2)}, u32[]{:S(2)}) async-start(f32[128,2,3]{2,1,0:T(2,128)} %bitcast.198), calls=%async_computation.1 | async-start | bytes 262144 | tf_op jit(solution)/shard_map/all_to_all | solution.py:229

commit v7 on v6

--- a/solution.py
+++ b/solution.py
@@ -102,7 +102,7 @@
 
 
 def specialist_kernel(env_ref, first_ref, head_ref, out_ref):
-    piece = 64
+    piece = 128
     slots = env_ref.shape[0] // out_ref.shape[0]
     span = piece * slots
     column = lax.broadcasted_iota(jnp.int32, (piece, span), 1)
@@ -129,7 +129,7 @@
     sources, item_count, slots, env_width = received.shape
     env_total = sources * item_count
     hidden_width = w_first.shape[-1]
-    block = math.gcd(env_total, 64)
+    block = math.gcd(env_total, 128)
     head = jnp.zeros((hidden_width, 128), jnp.bfloat16).at[:, : w_head.shape[0]].set(w_head.T)
     results = pl.pallas_call(
         specialist_kernel,

time: 287 us -> 286 us (level)
  no operation moved by 1% of the time
where the time goes in v7:
time: 286 us; the launch traced here: 285 us
  waiting for transfers between devices  130 us (45%)
  starting transfers between devices  99 us (35%)
  local copies, waits for them, and re-layouts  17.3 us (6%)
  Pallas kernels  16.6 us (6%)
  other arithmetic  10.5 us (4%)
  matrix products  9.53 us (3%)
    all_to_all x1, waiting for transfers between devices, per_device(): lax.all_to_all(outgoing.reshape(owner_total, capacity, slots, env_width),...  97.1 us
    ppermute x9, starting transfers between devices, with_halo(): lax.ppermute(head, axis, [((i + 1) % count, i) for i in range(ends)])  44.3 us
    ppermute x9, starting transfers between devices, with_halo(): lax.ppermute(tail, axis, [(i, (i + 1) % count) for i in range(ends)])  28.7 us
    ppermute x9, waiting for transfers between devices, with_halo(): lax.ppermute(tail, axis, [(i, (i + 1) % count) for i in range(ends)])  16.7 us
    pallas_call x1, Pallas kernels, specialist(): pl.pallas_call(specialist_kernel, grid=(env_total // block,), in_specs=[p...  16.6 us
    all_to_all x1, starting transfers between devices, per_device(): lax.all_to_all(outgoing.reshape(owner_total, capacity, slots, env_width),...  16.4 us
    all_to_all x1, waiting for transfers between devices, per_device(): lax.all_to_all(results, ('gx', 'gy'), split_axis=0, concat_axis=0, tiled=...  15.6 us
    all_to_all x1, starting transfers between devices, per_device(): lax.all_to_all(results, ('gx', 'gy'), split_axis=0, concat_axis=0, tiled=...  9.49 us
  transfers between devices with their start and end apart: 20, of which 10 were waited for; matrix products, arithmetic and copies ran while one was open for 6% of the time, Pallas kernels for 0%

profile of v7, /device:TPU:1, one launch (start us, length us, event | category | flops | bytes accessed | tf_op | source)
XLA Modules:
  0.0 284.6 jit_solution(17738882946897741016)
XLA Ops:
  0.8 8.7 %collective-permute-start.1 = (bf16[1,1,32,256]{3,2,1,0:T(8,128)(2,1)S(1)}, bf16[1,1,32,256]{3,2,1,0:T(8,128)(2,1)S(1)}, u32[]{:S(2)}, u32[]{:S(2)}) collective-permute-start(bf16[1,1,32,256]{3,2,1,0:T(8,128)(2,1)S(1)} %get-tuple-element.104), channel_id=1, source_target_pairs={{4,0},{8,4},{12,8},{16,12},{20,16},{24,20},{28,24},{32,28},{36,32}... | collective-permute-start | bytes 49160 | tf_op jit(solution)/shard_map/ppermute | solution.py:28
  9.5 1.9 collective-permute-start
  14.0 4.0 %iota_compare_fusion = pred[128,64,108]{2,1,0:T(8,128)(4,1)S(1)} fusion(s32[128,64]{1,0:T(8,128)} %bitcast.284), kind=kLoop, calls=%fused_computation.7 | loop fusion | flops 884736 | bytes 917504 | tf_op jit(solution)/shard_map/eq | solution.py:169
  20.3 2.9 %convolution_convert_fusion = bf16[128,8,108]{2,1,0:T(8,128)(2,1)S(1)} fusion(f32[128,64]{1,0:T(8,128)S(1)} %add_multiply_fusion, f32[8]{0:T(128)S(1)} %multiply_add_fusion, f32[128,64]{1,0:T(8,128)} %bitcast.286, s32[128,64]{1,0:T(8,128)} %bitcast.285), kind=kOutput, calls=%fused_computation.16 | convolution fusion | flops 15478784 | bytes 319520 | tf_op jit(solution)/shard_map/ask,asc->akc/dot_general | solution.py:170
  23.9 1.9 collective-permute-start.3
  25.8 3.4 %collective-permute-start.2 = (bf16[1,6,32,256]{3,2,1,0:T(8,128)(2,1)S(1)}, bf16[1,6,32,256]{3,2,1,0:T(8,128)(2,1)S(1)}, u32[]{:S(2)}, u32[]{:S(2)}) collective-permute-start(bf16[1,6,32,256]{3,2,1,0:T(8,128)(2,1)S(1)} %constant_dynamic-update-slice_fusion), channel_id=1, source_target_pairs={{0,64},{64,128},{128,192},{192,256},{256,320},{320,384},{384,448},... | collective-permute-start | bytes 294920 | tf_op jit(solution)/shard_map/ppermute | solution.py:26
  29.4 3.0 %collective-permute-done.2 = bf16[1,6,32,256]{3,2,1,0:T(8,128)(2,1)S(1)} collective-permute-done((bf16[1,6,32,256]{3,2,1,0:T(8,128)(2,1)S(1)}, bf16[1,6,32,256]{3,2,1,0:T(8,128)(2,1)S(1)}, u32[]{:S(2)}, u32[]{:S(2)}) %collective-permute-start.2) | collective-permute-done | bytes 98336 | tf_op jit(solution)/shard_map/ppermute | solution.py:26
  32.5 1.3 collective-permute-start.5
  33.8 4.0 %collective-permute-start.4 = (bf16[3,6,4,256]{3,2,1,0:T(4,128)(2,1)S(1)}, bf16[3,6,4,256]{3,2,1,0:T(4,128)(2,1)S(1)}, u32[]{:S(2)}, u32[]{:S(2)}) collective-permute-start(bf16[3,6,4,256]{3,2,1,0:T(4,128)(2,1)S(1)} %get-tuple-element.62), channel_id=1, source_target_pairs={{0,1},{1,2},{2,3},{4,5},{5,6},{6,7},{8,9},{9,10},{10,11},{12,13},{... | collective-permute-start | bytes 110600 | tf_op jit(solution)/shard_map/ppermute | solution.py:26
  43.8 1.8 multiply_reduce_fusion.1
  45.8 12.9 %collective-permute-start.7 = (bf16[1,1,32,256]{3,1,2,0:T(2,128)(2,1)S(1)}, bf16[1,1,32,256]{3,1,2,0:T(2,128)(2,1)S(1)}, u32[]{:S(2)}, u32[]{:S(2)}) collective-permute-start(bf16[1,1,32,256]{3,1,2,0:T(2,128)(2,1)S(1)} %get-tuple-element.100), channel_id=1, source_target_pairs={{4,0},{8,4},{12,8},{16,12},{20,16},{24,20},{28,24},{32,28},{36,32}... | collective-permute-start | bytes 49160 | tf_op jit(solution)/shard_map/ppermute | solution.py:28
  58.7 1.9 collective-permute-start.6
  60.7 5.8 %collective-permute-done.6 = bf16[1,1,32,256]{3,1,2,0:T(2,128)(2,1)S(1)} collective-permute-done((bf16[1,1,32,256]{3,1,2,0:T(2,128)(2,1)S(1)}, bf16[1,1,32,256]{3,1,2,0:T(2,128)(2,1)S(1)}, u32[]{:S(2)}, u32[]{:S(2)}) %collective-permute-start.6) | collective-permute-done | bytes 16416 | tf_op jit(solution)/shard_map/ppermute | solution.py:26
  66.7 2.1 collective-permute-start.9
  68.7 3.2 %collective-permute-start.8 = (bf16[1,6,32,256]{3,1,2,0:T(8,128)(2,1)S(1)}, bf16[1,6,32,256]{3,1,2,0:T(8,128)(2,1)S(1)}, u32[]{:S(2)}, u32[]{:S(2)}) collective-permute-start(bf16[1,6,32,256]{3,1,2,0:T(8,128)(2,1)S(1)} %pad_maximum_fusion.3), channel_id=1, source_target_pairs={{0,64},{64,128},{128,192},{192,256},{256,320},{320,384},{384,448},... | collective-permute-start | bytes 294920 | tf_op jit(solution)/shard_map/ppermute | solution.py:26
  72.7 3.0 %collective-permute-done.8 = bf16[1,6,32,256]{3,1,2,0:T(8,128)(2,1)S(1)} collective-permute-done((bf16[1,6,32,256]{3,1,2,0:T(8,128)(2,1)S(1)}, bf16[1,6,32,256]{3,1,2,0:T(8,128)(2,1)S(1)}, u32[]{:S(2)}, u32[]{:S(2)}) %collective-permute-start.8) | collective-permute-done | bytes 98336 | tf_op jit(solution)/shard_map/ppermute | solution.py:26
  75.7 1.3 collective-permute-start.11
  77.0 4.5 %collective-permute-start.10 = (bf16[3,6,4,256]{3,1,2,0:T(8,128)(2,1)S(1)}, bf16[3,6,4,256]{3,1,2,0:T(8,128)(2,1)S(1)}, u32[]{:S(2)}, u32[]{:S(2)}) collective-permute-start(bf16[3,6,4,256]{3,1,2,0:T(8,128)(2,1)S(1)} %get-tuple-element.40), channel_id=1, source_target_pairs={{0,1},{1,2},{2,3},{4,5},{5,6},{6,7},{8,9},{9,10},{10,11},{12,13},{... | collective-permute-start | bytes 110600 | tf_op jit(solution)/shard_map/ppermute | solution.py:26
  86.7 1.8 multiply_reduce_fusion
  88.8 12.9 %collective-permute-start.13 = (bf16[1,1,32,128]{3,2,1,0:T(8,128)(2,1)S(1)}, bf16[1,1,32,128]{3,2,1,0:T(8,128)(2,1)S(1)}, u32[]{:S(2)}, u32[]{:S(2)}) collective-permute-start(bf16[1,1,32,128]{3,2,1,0:T(8,128)(2,1)S(1)} %get-tuple-element.115), channel_id=1, source_target_pairs={{4,0},{8,4},{12,8},{16,12},{20,16},{24,20},{28,24},{32,28},{36,32}... | collective-permute-start | bytes 24584 | tf_op jit(solution)/shard_map/ppermute | solution.py:28
  101.6 1.9 collective-permute-start.12
  104.8 1.9 collective-permute-start.15
  106.7 3.4 %collective-permute-start.14 = (bf16[1,6,32,128]{3,2,1,0:T(8,128)(2,1)S(1)}, bf16[1,6,32,128]{3,2,1,0:T(8,128)(2,1)S(1)}, u32[]{:S(2)}, u32[]{:S(2)}) collective-permute-start(bf16[1,6,32,128]{3,2,1,0:T(8,128)(2,1)S(1)} %pad_maximum_fusion.13), channel_id=1, source_target_pairs={{0,64},{64,128},{128,192},{192,256},{256,320},{320,384},{384,448},... | collective-permute-start | bytes 147464 | tf_op jit(solution)/shard_map/ppermute | solution.py:26
  110.1 2.6 collective-permute-done.14
  112.8 1.3 collective-permute-start.17
  114.1 4.6 %collective-permute-start.16 = (bf16[3,6,4,128]{3,2,1,0:T(4,128)(2,1)S(1)}, bf16[3,6,4,128]{3,2,1,0:T(4,128)(2,1)S(1)}, u32[]{:S(2)}, u32[]{:S(2)}) collective-permute-start(bf16[3,6,4,128]{3,2,1,0:T(4,128)(2,1)S(1)} %get-tuple-element.84), channel_id=1, source_target_pairs={{0,1},{1,2},{2,3},{4,5},{5,6},{6,7},{8,9},{9,10},{10,11},{12,13},{... | collective-permute-start | bytes 55304 | tf_op jit(solution)/shard_map/ppermute | solution.py:26
  122.2 3.1 %gather_fusion.3 = bf16[256,64,128]{2,1,0:T(8,128)(2,1)} fusion(bf16[33,64,128]{2,1,0:T(8,128)(2,1)S(1)} %concatenate.128, s32[1024]{0:T(1024)S(1)} %pad_clamp_fusion.1), kind=kCustom, calls=%fused_computation.3 | custom fusion | bytes 8389632 | tf_op jit(solution)/shard_map/gather | solution.py:215
  125.3 16.4 %all-to-all-start = ((bf16[128,2,64,128]{3,2,1,0:T(8,128)(2,1)}), bf16[128,2,64,128]{3,2,1,0:T(8,128)(2,1)}, u32[]{:S(2)}, u32[]{:S(2)}) async-start(bf16[128,2,64,128]{3,2,1,0:T(8,128)(2,1)} %bitcast.183), calls=%async_computation | async-start | bytes 8388608 | tf_op jit(solution)/shard_map/all_to_all | solution.py:219
  144.0 97.1 %all-to-all-done = bf16[128,2,64,128]{3,2,1,0:T(8,128)(2,1)} async-done(((bf16[128,2,64,128]{3,2,1,0:T(8,128)(2,1)}), bf16[128,2,64,128]{3,2,1,0:T(8,128)(2,1)}, u32[]{:S(2)}, u32[]{:S(2)}) %all-to-all-start) | async-done | bytes 4194336 | tf_op jit(solution)/shard_map/all_to_all | solution.py:219
  241.0 16.6 %shard_map.127 = f32[256,128]{1,0:T(8,128)} custom-call(bf16[16384,128]{1,0:T(8,128)(2,1)} %bitcast.107.env_ref, bf16[128,1024]{1,0:T(8,128)(2,1)} %bitcast.203, bf16[1024,128]{1,0:T(8,128)(2,1)} %scatter.13.head_ref), custom_call_target="tpu_custom_call" | custom-call | tf_op jit(solution)/shard_map/pallas_call | solution.py:134
  257.7 9.5 %all-to-all-start.1 = ((f32[128,2,3]{2,1,0:T(2,128)}), f32[128,2,3]{2,1,0:T(2,128)S(1)}, u32[]{:S(2)}, u32[]{:S(2)}) async-start(f32[128,2,3]{2,1,0:T(2,128)} %bitcast.198), calls=%async_computation.1 | async-start | bytes 262144 | tf_op jit(solution)/shard_map/all_to_all | solution.py:229
  267.5 15.6 %all-to-all-done.1 = f32[128,2,3]{2,1,0:T(2,128)S(1)} async-done(((f32[128,2,3]{2,1,0:T(2,128)}), f32[128,2,3]{2,1,0:T(2,128)S(1)}, u32[]{:S(2)}, u32[]{:S(2)}) %all-to-all-start.1) | async-done | bytes 3104 | tf_op jit(solution)/shard_map/all_to_all | solution.py:229
  (204 shorter events, 26.6 us)
Async XLA Ops:
  0.0 88.5 %copy-start = (bf16[256,128]{1,0:T(8,128)(2,1)S(1)}, bf16[256,128]{1,0:T(8,128)(2,1)}, u32[]{:S(2)}) copy-start(bf16[256,128]{1,0:T(8,128)(2,1)} %param.21) | copy-start | bytes 196612
  0.0 23.9 %copy-start.1 = (bf16[1,4,32,256]{3,2,1,0:T(8,128)(2,1)S(1)}, bf16[1,4,32,256]{3,2,1,0:T(8,128)(2,1)}, u32[]{:S(2)}) copy-start(bf16[1,4,32,256]{3,2,1,0:T(8,128)(2,1)} %param.15) | copy-start | bytes 196612
  0.8 23.1 %collective-permute-start.1 = (bf16[1,1,32,256]{3,2,1,0:T(8,128)(2,1)S(1)}, bf16[1,1,32,256]{3,2,1,0:T(8,128)(2,1)S(1)}, u32[]{:S(2)}, u32[]{:S(2)}) collective-permute-start(bf16[1,1,32,256]{3,2,1,0:T(8,128)(2,1)S(1)} %get-tuple-element.104), channel_id=1, source_target_pairs={{4,0},{8,4},{12,8},{16,12},{20,16},{24,20},{28,24},{32,28},{36,32}... | collective-permute-start | bytes 49160 | tf_op jit(solution)/shard_map/ppermute | solution.py:28
  9.5 14.3 %collective-permute-start = (bf16[1,1,32,256]{3,2,1,0:T(8,128)(2,1)S(1)}, bf16[1,1,32,256]{3,2,1,0:T(8,128)(2,1)S(1)}, u32[]{:S(2)}, u32[]{:S(2)}) collective-permute-start(bf16[1,1,32,256]{3,2,1,0:T(8,128)(2,1)S(1)} %get-tuple-element.105), channel_id=1, source_target_pairs={{0,4},{4,8},{8,12},{12,16},{16,20},{20,24},{24,28},{28,32},{32,36}... | collective-permute-start | bytes 49160 | tf_op jit(solution)/shard_map/ppermute | solution.py:26
  14.0 15.3 %copy-start.5 = (s32[1,1,1,32]{3,2,1,0:T(1,128)S(1)}, s32[1,1,1,32]{3,2,1,0:T(1,128)}, u32[]{:S(2)}) copy-start(s32[1,1,1,32]{3,2,1,0:T(1,128)} %param.25) | copy-start | bytes 388
  23.9 5.5 %collective-permute-start.3 = (bf16[1,6,32,256]{3,2,1,0:T(8,128)(2,1)S(1)}, bf16[1,6,32,256]{3,2,1,0:T(8,128)(2,1)S(1)}, u32[]{:S(2)}, u32[]{:S(2)}) collective-permute-start(bf16[1,6,32,256]{3,2,1,0:T(8,128)(2,1)S(1)} %constant_dynamic-update-slice_fusion), channel_id=1, source_target_pairs={{64,0},{128,64},{192,128},{256,192},{320,256},{384,320},{448,384},... | collective-permute-start | bytes 294920 | tf_op jit(solution)/shard_map/ppermute | solution.py:28
  25.8 6.6 %collective-permute-start.2 = (bf16[1,6,32,256]{3,2,1,0:T(8,128)(2,1)S(1)}, bf16[1,6,32,256]{3,2,1,0:T(8,128)(2,1)S(1)}, u32[]{:S(2)}, u32[]{:S(2)}) collective-permute-start(bf16[1,6,32,256]{3,2,1,0:T(8,128)(2,1)S(1)} %constant_dynamic-update-slice_fusion), channel_id=1, source_target_pairs={{0,64},{64,128},{128,192},{192,256},{256,320},{320,384},{384,448},... | collective-permute-start | bytes 294920 | tf_op jit(solution)/shard_map/ppermute | solution.py:26
  32.5 5.7 %collective-permute-start.5 = (bf16[3,6,4,256]{3,2,1,0:T(4,128)(2,1)S(1)}, bf16[3,6,4,256]{3,2,1,0:T(4,128)(2,1)S(1)}, u32[]{:S(2)}, u32[]{:S(2)}) collective-permute-start(bf16[3,6,4,256]{3,2,1,0:T(4,128)(2,1)S(1)} %get-tuple-element.61), channel_id=1, source_target_pairs={{1,0},{2,1},{3,2},{5,4},{6,5},{7,6},{9,8},{10,9},{11,10},{13,12},{... | collective-permute-start | bytes 110600 | tf_op jit(solution)/shard_map/ppermute | solution.py:28
  33.8 5.0 %collective-permute-start.4 = (bf16[3,6,4,256]{3,2,1,0:T(4,128)(2,1)S(1)}, bf16[3,6,4,256]{3,2,1,0:T(4,128)(2,1)S(1)}, u32[]{:S(2)}, u32[]{:S(2)}) collective-permute-start(bf16[3,6,4,256]{3,2,1,0:T(4,128)(2,1)S(1)} %get-tuple-element.62), channel_id=1, source_target_pairs={{0,1},{1,2},{2,3},{4,5},{5,6},{6,7},{8,9},{9,10},{10,11},{12,13},{... | collective-permute-start | bytes 110600 | tf_op jit(solution)/shard_map/ppermute | solution.py:26
  42.5 1.3 copy-start.4
  45.8 14.9 %collective-permute-start.7 = (bf16[1,1,32,256]{3,1,2,0:T(2,128)(2,1)S(1)}, bf16[1,1,32,256]{3,1,2,0:T(2,128)(2,1)S(1)}, u32[]{:S(2)}, u32[]{:S(2)}) collective-permute-start(bf16[1,1,32,256]{3,1,2,0:T(2,128)(2,1)S(1)} %get-tuple-element.100), channel_id=1, source_target_pairs={{4,0},{8,4},{12,8},{16,12},{20,16},{24,20},{28,24},{32,28},{36,32}... | collective-permute-start | bytes 49160 | tf_op jit(solution)/shard_map/ppermute | solution.py:28
  58.7 7.8 %collective-permute-start.6 = (bf16[1,1,32,256]{3,1,2,0:T(2,128)(2,1)S(1)}, bf16[1,1,32,256]{3,1,2,0:T(2,128)(2,1)S(1)}, u32[]{:S(2)}, u32[]{:S(2)}) collective-permute-start(bf16[1,1,32,256]{3,1,2,0:T(2,128)(2,1)S(1)} %get-tuple-element.99), channel_id=1, source_target_pairs={{0,4},{4,8},{8,12},{12,16},{16,20},{20,24},{24,28},{28,32},{32,36}... | collective-permute-start | bytes 49160 | tf_op jit(solution)/shard_map/ppermute | solution.py:26
  66.7 6.0 %collective-permute-start.9 = (bf16[1,6,32,256]{3,1,2,0:T(8,128)(2,1)S(1)}, bf16[1,6,32,256]{3,1,2,0:T(8,128)(2,1)S(1)}, u32[]{:S(2)}, u32[]{:S(2)}) collective-permute-start(bf16[1,6,32,256]{3,1,2,0:T(8,128)(2,1)S(1)} %pad_maximum_fusion.3), channel_id=1, source_target_pairs={{64,0},{128,64},{192,128},{256,192},{320,256},{384,320},{448,384},... | collective-permute-start | bytes 294920 | tf_op jit(solution)/shard_map/ppermute | solution.py:28
  68.7 6.9 %collective-permute-start.8 = (bf16[1,6,32,256]{3,1,2,0:T(8,128)(2,1)S(1)}, bf16[1,6,32,256]{3,1,2,0:T(8,128)(2,1)S(1)}, u32[]{:S(2)}, u32[]{:S(2)}) collective-permute-start(bf16[1,6,32,256]{3,1,2,0:T(8,128)(2,1)S(1)} %pad_maximum_fusion.3), channel_id=1, source_target_pairs={{0,64},{64,128},{128,192},{192,256},{256,320},{320,384},{384,448},... | collective-permute-start | bytes 294920 | tf_op jit(solution)/shard_map/ppermute | solution.py:26
  75.7 5.9 %collective-permute-start.11 = (bf16[3,6,4,256]{3,1,2,0:T(8,128)(2,1)S(1)}, bf16[3,6,4,256]{3,1,2,0:T(8,128)(2,1)S(1)}, u32[]{:S(2)}, u32[]{:S(2)}) collective-permute-start(bf16[3,6,4,256]{3,1,2,0:T(8,128)(2,1)S(1)} %get-tuple-element.39), channel_id=1, source_target_pairs={{1,0},{2,1},{3,2},{5,4},{6,5},{7,6},{9,8},{10,9},{11,10},{13,12},{... | collective-permute-start | bytes 110600 | tf_op jit(solution)/shard_map/ppermute | solution.py:28
  77.0 5.4 %collective-permute-start.10 = (bf16[3,6,4,256]{3,1,2,0:T(8,128)(2,1)S(1)}, bf16[3,6,4,256]{3,1,2,0:T(8,128)(2,1)S(1)}, u32[]{:S(2)}, u32[]{:S(2)}) collective-permute-start(bf16[3,6,4,256]{3,1,2,0:T(8,128)(2,1)S(1)} %get-tuple-element.40), channel_id=1, source_target_pairs={{0,1},{1,2},{2,3},{4,5},{5,6},{6,7},{8,9},{9,10},{10,11},{12,13},{... | collective-permute-start | bytes 110600 | tf_op jit(solution)/shard_map/ppermute | solution.py:26
  88.8 16.0 %collective-permute-start.13 = (bf16[1,1,32,128]{3,2,1,0:T(8,128)(2,1)S(1)}, bf16[1,1,32,128]{3,2,1,0:T(8,128)(2,1)S(1)}, u32[]{:S(2)}, u32[]{:S(2)}) collective-permute-start(bf16[1,1,32,128]{3,2,1,0:T(8,128)(2,1)S(1)} %get-tuple-element.115), channel_id=1, source_target_pairs={{4,0},{8,4},{12,8},{16,12},{20,16},{24,20},{28,24},{32,28},{36,32}... | collective-permute-start | bytes 24584 | tf_op jit(solution)/shard_map/ppermute | solution.py:28
  101.6 3.1 %collective-permute-start.12 = (bf16[1,1,32,128]{3,2,1,0:T(8,128)(2,1)S(1)}, bf16[1,1,32,128]{3,2,1,0:T(8,128)(2,1)S(1)}, u32[]{:S(2)}, u32[]{:S(2)}) collective-permute-start(bf16[1,1,32,128]{3,2,1,0:T(8,128)(2,1)S(1)} %get-tuple-element.114), channel_id=1, source_target_pairs={{0,4},{4,8},{8,12},{12,16},{16,20},{20,24},{24,28},{28,32},{32,36}... | collective-permute-start | bytes 24584 | tf_op jit(solution)/shard_map/ppermute | solution.py:26
  104.8 5.3 %collective-permute-start.15 = (bf16[1,6,32,128]{3,2,1,0:T(8,128)(2,1)S(1)}, bf16[1,6,32,128]{3,2,1,0:T(8,128)(2,1)S(1)}, u32[]{:S(2)}, u32[]{:S(2)}) collective-permute-start(bf16[1,6,32,128]{3,2,1,0:T(8,128)(2,1)S(1)} %pad_maximum_fusion.13), channel_id=1, source_target_pairs={{64,0},{128,64},{192,128},{256,192},{320,256},{384,320},{448,384},... | collective-permute-start | bytes 147464 | tf_op jit(solution)/shard_map/ppermute | solution.py:28
  106.7 6.0 %collective-permute-start.14 = (bf16[1,6,32,128]{3,2,1,0:T(8,128)(2,1)S(1)}, bf16[1,6,32,128]{3,2,1,0:T(8,128)(2,1)S(1)}, u32[]{:S(2)}, u32[]{:S(2)}) collective-permute-start(bf16[1,6,32,128]{3,2,1,0:T(8,128)(2,1)S(1)} %pad_maximum_fusion.13), channel_id=1, source_target_pairs={{0,64},{64,128},{128,192},{192,256},{256,320},{320,384},{384,448},... | collective-permute-start | bytes 147464 | tf_op jit(solution)/shard_map/ppermute | solution.py:26
  112.8 5.9 %collective-permute-start.17 = (bf16[3,6,4,128]{3,2,1,0:T(4,128)(2,1)S(1)}, bf16[3,6,4,128]{3,2,1,0:T(4,128)(2,1)S(1)}, u32[]{:S(2)}, u32[]{:S(2)}) collective-permute-start(bf16[3,6,4,128]{3,2,1,0:T(4,128)(2,1)S(1)} %get-tuple-element.83), channel_id=1, source_target_pairs={{1,0},{2,1},{3,2},{5,4},{6,5},{7,6},{9,8},{10,9},{11,10},{13,12},{... | collective-permute-start | bytes 55304 | tf_op jit(solution)/shard_map/ppermute | solution.py:28
  114.1 5.5 %collective-permute-start.16 = (bf16[3,6,4,128]{3,2,1,0:T(4,128)(2,1)S(1)}, bf16[3,6,4,128]{3,2,1,0:T(4,128)(2,1)S(1)}, u32[]{:S(2)}, u32[]{:S(2)}) collective-permute-start(bf16[3,6,4,128]{3,2,1,0:T(4,128)(2,1)S(1)} %get-tuple-element.84), channel_id=1, source_target_pairs={{0,1},{1,2},{2,3},{4,5},{5,6},{6,7},{8,9},{9,10},{10,11},{12,13},{... | collective-permute-start | bytes 55304 | tf_op jit(solution)/shard_map/ppermute | solution.py:26
  125.3 16.4 %copy-start.2 = (bf16[1,3,1024]{2,1,0:T(4,128)(2,1)S(1)}, bf16[1,3,1024]{2,1,0:T(4,128)(2,1)}, u32[]{:S(2)}) copy-start(bf16[1,3,1024]{2,1,0:T(4,128)(2,1)} %param.24) | copy-start | bytes 18436
  125.3 115.8 %all-to-all-start = ((bf16[128,2,64,128]{3,2,1,0:T(8,128)(2,1)}), bf16[128,2,64,128]{3,2,1,0:T(8,128)(2,1)}, u32[]{:S(2)}, u32[]{:S(2)}) async-start(bf16[128,2,64,128]{3,2,1,0:T(8,128)(2,1)} %bitcast.183), calls=%async_computation | async-start | bytes 8388608 | tf_op jit(solution)/shard_map/all_to_all | solution.py:219
  241.0 26.1 %copy-start.3 = (bf16[3,256]{1,0:T(4,128)(2,1)S(1)}, bf16[3,256]{1,0:T(4,128)(2,1)}, u32[]{:S(2)}) copy-start(bf16[3,256]{1,0:T(4,128)(2,1)} %param.22) | copy-start | bytes 4612
  257.7 25.4 %all-to-all-start.1 = ((f32[128,2,3]{2,1,0:T(2,128)}), f32[128,2,3]{2,1,0:T(2,128)S(1)}, u32[]{:S(2)}, u32[]{:S(2)}) async-start(f32[128,2,3]{2,1,0:T(2,128)} %bitcast.198), calls=%async_computation.1 | async-start | bytes 262144 | tf_op jit(solution)/shard_map/all_to_all | solution.py:229

commit v8 on v5

--- a/solution.py
+++ b/solution.py
@@ -69,18 +69,13 @@
 
 def candidates(padded, cells_x, cells_y, cells_z):
     feature_width = padded.shape[-1]
-    pieces = []
-    for step_x in range(3):
-        for step_y in range(3):
-            for step_z in range(3):
-                piece = padded[
-                    step_x : step_x + cells_x,
-                    step_y : step_y + cells_y,
-                    step_z * M : step_z * M + cells_z * M,
-                ]
-                pieces.append(piece.reshape(cells_x, cells_y, cells_z, M, feature_width))
-    stacked = jnp.stack(pieces, axis=3)
-    return stacked.reshape(cells_x * cells_y * cells_z, 27 * M, feature_width)
+    deep = jnp.stack(
+        [padded[:, :, step * M : step * M + cells_z * M] for step in range(3)], axis=2
+    ).reshape(cells_x + 2, cells_y + 2, 3, cells_z, M, feature_width)
+    wide = jnp.stack([deep[:, step : step + cells_y] for step in range(3)], axis=1)
+    full = jnp.stack([wide[step : step + cells_x] for step in range(3)], axis=0)
+    full = jnp.transpose(full, (1, 3, 5, 0, 2, 4, 6, 7))
+    return full.reshape(cells_x * cells_y * cells_z, 27 * M, feature_width)
 
 
 def cheap_layer(state, weights, w_message, w_update, gain):

time: 286 us -> 292 us (1.021)
  other arithmetic: 9.4 us -> 14.8 us
  starting transfers between devices: 99 us -> 104 us
  waiting for transfers between devices: 130 us -> 126 us
    all_to_all x1, starting transfers between devices: 16.4 us -> 22 us  [per_device(): lax.all_to_all(outgoing.reshape(owner_total, capacity, slots, env_width),...]
    ppermute x9, waiting for transfers between devices: 16.6 us -> 11.4 us  [with_halo(): lax.ppermute(tail, axis, [(i, (i + 1) % count) for i in range(ends)])]
    another operation x2 -> x6, other arithmetic: 1.43 us -> 5.47 us  [the longest x3 3.78 us: candidates(): jnp.stack([deep[:, step:step + cells_y] for step in range(3)], axis=1)]
    transpose x0 -> x3, other arithmetic: none -> 3.78 us  [candidates(): full = jnp.transpose(full, (1, 3, 5, 0, 2, 4, 6, 7))]
    unnamed x98 -> x30, local copies, waits for them, and re-layouts: 6.27 us -> 5.12 us
  transfers between devices with their start and end apart: 20 -> 20, of which waited for: 10 -> 11; matrix products, arithmetic and copies ran while one was open for 5% -> 4% of each run, Pallas kernels for 0% -> 0%
where the time goes in v8:
time: 292 us; the launch traced here: 291 us
  waiting for transfers between devices  126 us (43%)
  starting transfers between devices  104 us (36%)
  Pallas kernels  17.6 us (6%)
  local copies, waits for them, and re-layouts  16 us (5%)
  other arithmetic  14.8 us (5%)
  matrix products  10.8 us (4%)
    all_to_all x1, waiting for transfers between devices, per_device(): lax.all_to_all(outgoing.reshape(owner_total, capacity, slots, env_width),...  96.7 us
    ppermute x9, starting transfers between devices, with_halo(): lax.ppermute(head, axis, [((i + 1) % count, i) for i in range(ends)])  41.7 us
    ppermute x9, starting transfers between devices, with_halo(): lax.ppermute(tail, axis, [(i, (i + 1) % count) for i in range(ends)])  30.5 us
    all_to_all x1, starting transfers between devices, per_device(): lax.all_to_all(outgoing.reshape(owner_total, capacity, slots, env_width),...  22 us
    pallas_call x1, Pallas kernels, specialist(): pl.pallas_call(specialist_kernel, grid=(env_total // block,), in_specs=[p...  17.6 us
    all_to_all x1, waiting for transfers between devices, per_device(): lax.all_to_all(results, ('gx', 'gy'), split_axis=0, concat_axis=0, tiled=...  15.6 us
    ppermute x9, waiting for transfers between devices, with_halo(): lax.ppermute(tail, axis, [(i, (i + 1) % count) for i in range(ends)])  11.4 us
    all_to_all x1, starting transfers between devices, per_device(): lax.all_to_all(results, ('gx', 'gy'), split_axis=0, concat_axis=0, tiled=...  9.46 us
  transfers between devices with their start and end apart: 20, of which 11 were waited for; matrix products, arithmetic and copies ran while one was open for 4% of the time, Pallas kernels for 0%

profile of v8, /device:TPU:1, one launch (start us, length us, event | category | flops | bytes accessed | tf_op | source)
XLA Modules:
  0.0 290.5 jit_solution(16785091639765407238)
XLA Ops:
  0.8 4.5 %collective-permute-start = (bf16[1,1,32,256]{3,2,1,0:T(8,128)(2,1)S(1)}, bf16[1,1,32,256]{3,2,1,0:T(8,128)(2,1)S(1)}, u32[]{:S(2)}, u32[]{:S(2)}) collective-permute-start(bf16[1,1,32,256]{3,2,1,0:T(8,128)(2,1)S(1)} %get-tuple-element.50), channel_id=1, source_target_pairs={{0,4},{4,8},{8,12},{12,16},{16,20},{20,24},{24,28},{28,32},{32,36}... | collective-permute-start | bytes 49160 | tf_op jit(solution)/shard_map/ppermute | solution.py:26
  5.3 6.2 %collective-permute-start.1 = (bf16[1,1,32,256]{3,2,1,0:T(8,128)(2,1)S(1)}, bf16[1,1,32,256]{3,2,1,0:T(8,128)(2,1)S(1)}, u32[]{:S(2)}, u32[]{:S(2)}) collective-permute-start(bf16[1,1,32,256]{3,2,1,0:T(8,128)(2,1)S(1)} %get-tuple-element.49), channel_id=1, source_target_pairs={{4,0},{8,4},{12,8},{16,12},{20,16},{24,20},{28,24},{32,28},{36,32}... | collective-permute-start | bytes 49160 | tf_op jit(solution)/shard_map/ppermute | solution.py:28
  13.4 2.0 collective-permute-start.3
  15.4 3.3 %collective-permute-start.2 = (bf16[1,6,32,256]{3,2,1,0:T(8,128)(2,1)S(1)}, bf16[1,6,32,256]{3,2,1,0:T(8,128)(2,1)S(1)}, u32[]{:S(2)}, u32[]{:S(2)}) collective-permute-start(bf16[1,6,32,256]{3,2,1,0:T(8,128)(2,1)S(1)} %constant_dynamic-update-slice_fusion), channel_id=1, source_target_pairs={{0,64},{64,128},{128,192},{192,256},{256,320},{320,384},{384,448},... | collective-permute-start | bytes 294920 | tf_op jit(solution)/shard_map/ppermute | solution.py:26
  18.7 2.9 convolution_convert_fusion.1
  23.4 4.6 %collective-permute-start.4 = (bf16[3,6,4,256]{3,2,1,0:T(4,128)(2,1)S(1)}, bf16[3,6,4,256]{3,2,1,0:T(4,128)(2,1)S(1)}, u32[]{:S(2)}, u32[]{:S(2)}) collective-permute-start(bf16[3,6,4,256]{3,2,1,0:T(4,128)(2,1)S(1)} %get-tuple-element.42), channel_id=1, source_target_pairs={{0,1},{1,2},{2,3},{4,5},{5,6},{6,7},{8,9},{9,10},{10,11},{12,13},{... | collective-permute-start | bytes 110600 | tf_op jit(solution)/shard_map/ppermute | solution.py:26
  33.2 1.5 maximum_bitcast_fusion
  36.4 1.8 multiply_reduce_fusion.1
  38.3 12.2 %collective-permute-start.7 = (bf16[1,1,32,256]{3,2,1,0:T(8,128)(2,1)S(1)}, bf16[1,1,32,256]{3,2,1,0:T(8,128)(2,1)S(1)}, u32[]{:S(2)}, u32[]{:S(2)}) collective-permute-start(bf16[1,1,32,256]{3,2,1,0:T(8,128)(2,1)S(1)} %get-tuple-element.48), channel_id=1, source_target_pairs={{4,0},{8,4},{12,8},{16,12},{20,16},{24,20},{28,24},{32,28},{36,32}... | collective-permute-start | bytes 49160 | tf_op jit(solution)/shard_map/ppermute | solution.py:28
  50.6 1.9 collective-permute-start.6
  52.5 2.6 iota_compare_fusion
  55.1 2.7 collective-permute-done.6
  57.8 2.8 collective-permute-start.9
  60.6 2.5 collective-permute-start.8
  63.5 3.7 %collective-permute-done.8 = bf16[1,6,32,256]{3,2,1,0:T(8,128)(2,1)S(1)} collective-permute-done((bf16[1,6,32,256]{3,2,1,0:T(8,128)(2,1)S(1)}, bf16[1,6,32,256]{3,2,1,0:T(8,128)(2,1)S(1)}, u32[]{:S(2)}, u32[]{:S(2)}) %collective-permute-start.8) | collective-permute-done | bytes 98336 | tf_op jit(solution)/shard_map/ppermute | solution.py:26
  68.6 4.5 %collective-permute-start.10 = (bf16[3,6,4,256]{3,2,1,0:T(4,128)(2,1)S(1)}, bf16[3,6,4,256]{3,2,1,0:T(4,128)(2,1)S(1)}, u32[]{:S(2)}, u32[]{:S(2)}) collective-permute-start(bf16[3,6,4,256]{3,2,1,0:T(4,128)(2,1)S(1)} %get-tuple-element.38), channel_id=1, source_target_pairs={{0,1},{1,2},{2,3},{4,5},{5,6},{6,7},{8,9},{9,10},{10,11},{12,13},{... | collective-permute-start | bytes 110600 | tf_op jit(solution)/shard_map/ppermute | solution.py:26
  75.6 1.5 pad_maximum_fusion.1
  78.3 1.5 maximum_bitcast_fusion.1
  81.5 1.8 multiply_reduce_fusion
  83.5 12.7 %collective-permute-start.13 = (bf16[1,1,32,128]{3,2,1,0:T(8,128)(2,1)S(1)}, bf16[1,1,32,128]{3,2,1,0:T(8,128)(2,1)S(1)}, u32[]{:S(2)}, u32[]{:S(2)}) collective-permute-start(bf16[1,1,32,128]{3,2,1,0:T(8,128)(2,1)S(1)} %get-tuple-element.52), channel_id=1, source_target_pairs={{4,0},{8,4},{12,8},{16,12},{20,16},{24,20},{28,24},{32,28},{36,32}... | collective-permute-start | bytes 24584 | tf_op jit(solution)/shard_map/ppermute | solution.py:28
  96.2 1.9 collective-permute-start.12
  99.3 1.9 collective-permute-start.15
  101.2 3.4 %collective-permute-start.14 = (bf16[1,6,32,128]{3,2,1,0:T(8,128)(2,1)S(1)}, bf16[1,6,32,128]{3,2,1,0:T(8,128)(2,1)S(1)}, u32[]{:S(2)}, u32[]{:S(2)}) collective-permute-start(bf16[1,6,32,128]{3,2,1,0:T(8,128)(2,1)S(1)} %pad_maximum_fusion.34), channel_id=1, source_target_pairs={{0,64},{64,128},{128,192},{192,256},{256,320},{320,384},{384,448},... | collective-permute-start | bytes 147464 | tf_op jit(solution)/shard_map/ppermute | solution.py:26
  104.6 2.7 collective-permute-done.14
  107.3 3.9 %collective-permute-start.16 = (bf16[3,6,4,128]{3,2,1,0:T(4,128)(2,1)S(1)}, bf16[3,6,4,128]{3,2,1,0:T(4,128)(2,1)S(1)}, u32[]{:S(2)}, u32[]{:S(2)}) collective-permute-start(bf16[3,6,4,128]{3,2,1,0:T(4,128)(2,1)S(1)} %get-tuple-element.45), channel_id=1, source_target_pairs={{0,1},{1,2},{2,3},{4,5},{5,6},{6,7},{8,9},{9,10},{10,11},{12,13},{... | collective-permute-start | bytes 55304 | tf_op jit(solution)/shard_map/ppermute | solution.py:26
  113.7 2.3 collective-permute-done.17
  121.6 3.2 %copy.81 = bf16[32,8,64,128]{3,2,1,0:T(8,128)(2,1)} copy(bf16[32,8,64,128]{3,1,2,0:T(8,128)(2,1)S(1)} %fusion) | data formatting | bytes 8388608
  124.8 22.0 %all-to-all-start = ((bf16[128,2,64,128]{3,2,1,0:T(8,128)(2,1)}), bf16[128,2,64,128]{3,2,1,0:T(8,128)(2,1)}, u32[]{:S(2)}, u32[]{:S(2)}) async-start(bf16[128,2,64,128]{3,2,1,0:T(8,128)(2,1)} %bitcast.181), calls=%async_computation | async-start | bytes 8388608 | tf_op jit(solution)/shard_map/all_to_all | solution.py:211
  149.2 96.7 %all-to-all-done = bf16[128,2,64,128]{3,2,1,0:T(8,128)(2,1)} async-done(((bf16[128,2,64,128]{3,2,1,0:T(8,128)(2,1)}), bf16[128,2,64,128]{3,2,1,0:T(8,128)(2,1)}, u32[]{:S(2)}, u32[]{:S(2)}) %all-to-all-start) | async-done | bytes 4194336 | tf_op jit(solution)/shard_map/all_to_all | solution.py:211
  245.9 17.6 %shard_map.127 = f32[256,128]{1,0:T(8,128)} custom-call(bf16[16384,128]{1,0:T(8,128)(2,1)} %bitcast.47.env_ref, bf16[128,1024]{1,0:T(8,128)(2,1)} %bitcast.205, bf16[1024,128]{1,0:T(8,128)(2,1)} %scatter.4.head_ref), custom_call_target="tpu_custom_call" | custom-call | tf_op jit(solution)/shard_map/pallas_call | solution.py:129
  263.6 9.5 %all-to-all-start.1 = ((f32[128,2,3]{2,1,0:T(2,128)}), f32[128,2,3]{2,1,0:T(2,128)S(1)}, u32[]{:S(2)}, u32[]{:S(2)}) async-start(f32[128,2,3]{2,1,0:T(2,128)} %bitcast.201), calls=%async_computation.1 | async-start | bytes 262144 | tf_op jit(solution)/shard_map/all_to_all | solution.py:221
  273.4 15.6 %all-to-all-done.1 = f32[128,2,3]{2,1,0:T(2,128)S(1)} async-done(((f32[128,2,3]{2,1,0:T(2,128)}), f32[128,2,3]{2,1,0:T(2,128)S(1)}, u32[]{:S(2)}, u32[]{:S(2)}) %all-to-all-start.1) | async-done | bytes 3104 | tf_op jit(solution)/shard_map/all_to_all | solution.py:221
  (113 shorter events, 31.2 us)
Async XLA Ops:
  0.0 83.3 %copy-start = (bf16[256,128]{1,0:T(8,128)(2,1)S(1)}, bf16[256,128]{1,0:T(8,128)(2,1)}, u32[]{:S(2)}) copy-start(bf16[256,128]{1,0:T(8,128)(2,1)} %param.21) | copy-start | bytes 196612
  0.0 28.0 %copy-start.6 = (f32[2,256]{1,0:T(2,128)S(1)}, f32[2,256]{1,0:T(2,128)}, u32[]{:S(2)}) copy-start(f32[2,256]{1,0:T(2,128)} %param.20) | copy-start | bytes 6148
  0.8 11.8 %collective-permute-start = (bf16[1,1,32,256]{3,2,1,0:T(8,128)(2,1)S(1)}, bf16[1,1,32,256]{3,2,1,0:T(8,128)(2,1)S(1)}, u32[]{:S(2)}, u32[]{:S(2)}) collective-permute-start(bf16[1,1,32,256]{3,2,1,0:T(8,128)(2,1)S(1)} %get-tuple-element.50), channel_id=1, source_target_pairs={{0,4},{4,8},{8,12},{12,16},{16,20},{20,24},{24,28},{28,32},{32,36}... | collective-permute-start | bytes 49160 | tf_op jit(solution)/shard_map/ppermute | solution.py:26
  5.3 8.1 %collective-permute-start.1 = (bf16[1,1,32,256]{3,2,1,0:T(8,128)(2,1)S(1)}, bf16[1,1,32,256]{3,2,1,0:T(8,128)(2,1)S(1)}, u32[]{:S(2)}, u32[]{:S(2)}) collective-permute-start(bf16[1,1,32,256]{3,2,1,0:T(8,128)(2,1)S(1)} %get-tuple-element.49), channel_id=1, source_target_pairs={{4,0},{8,4},{12,8},{16,12},{20,16},{24,20},{28,24},{32,28},{36,32}... | collective-permute-start | bytes 49160 | tf_op jit(solution)/shard_map/ppermute | solution.py:28
  13.4 8.2 %collective-permute-start.3 = (bf16[1,6,32,256]{3,2,1,0:T(8,128)(2,1)S(1)}, bf16[1,6,32,256]{3,2,1,0:T(8,128)(2,1)S(1)}, u32[]{:S(2)}, u32[]{:S(2)}) collective-permute-start(bf16[1,6,32,256]{3,2,1,0:T(8,128)(2,1)S(1)} %constant_dynamic-update-slice_fusion), channel_id=1, source_target_pairs={{64,0},{128,64},{192,128},{256,192},{320,256},{384,320},{448,384},... | collective-permute-start | bytes 294920 | tf_op jit(solution)/shard_map/ppermute | solution.py:28
  15.4 6.6 %collective-permute-start.2 = (bf16[1,6,32,256]{3,2,1,0:T(8,128)(2,1)S(1)}, bf16[1,6,32,256]{3,2,1,0:T(8,128)(2,1)S(1)}, u32[]{:S(2)}, u32[]{:S(2)}) collective-permute-start(bf16[1,6,32,256]{3,2,1,0:T(8,128)(2,1)S(1)} %constant_dynamic-update-slice_fusion), channel_id=1, source_target_pairs={{0,64},{64,128},{128,192},{192,256},{256,320},{320,384},{384,448},... | collective-permute-start | bytes 294920 | tf_op jit(solution)/shard_map/ppermute | solution.py:26
  22.1 6.0 %collective-permute-start.5 = (bf16[3,6,4,256]{3,2,1,0:T(4,128)(2,1)S(1)}, bf16[3,6,4,256]{3,2,1,0:T(4,128)(2,1)S(1)}, u32[]{:S(2)}, u32[]{:S(2)}) collective-permute-start(bf16[3,6,4,256]{3,2,1,0:T(4,128)(2,1)S(1)} %get-tuple-element.41), channel_id=1, source_target_pairs={{1,0},{2,1},{3,2},{5,4},{6,5},{7,6},{9,8},{10,9},{11,10},{13,12},{... | collective-permute-start | bytes 110600 | tf_op jit(solution)/shard_map/ppermute | solution.py:28
  23.4 5.7 %collective-permute-start.4 = (bf16[3,6,4,256]{3,2,1,0:T(4,128)(2,1)S(1)}, bf16[3,6,4,256]{3,2,1,0:T(4,128)(2,1)S(1)}, u32[]{:S(2)}, u32[]{:S(2)}) collective-permute-start(bf16[3,6,4,256]{3,2,1,0:T(4,128)(2,1)S(1)} %get-tuple-element.42), channel_id=1, source_target_pairs={{0,1},{1,2},{2,3},{4,5},{5,6},{6,7},{8,9},{9,10},{10,11},{12,13},{... | collective-permute-start | bytes 110600 | tf_op jit(solution)/shard_map/ppermute | solution.py:26
  35.1 1.3 copy-start.1
  35.1 1.3 copy-start.7
  36.2 16.2 %copy-start.2 = (s32[1,4,32,64]{3,2,1,0:T(8,128)S(1)}, s32[1,4,32,64]{3,2,1,0:T(8,128)}, u32[]{:S(2)}) copy-start(s32[1,4,32,64]{3,2,1,0:T(8,128)} %param.16) | copy-start | bytes 98308
  36.4 26.7 %copy-start.4 = (s32[1,1,1,32,1]{3,4,2,1,0:T(1,128)S(1)}, s32[1,1,1,32,1]{3,4,2,1,0:T(1,128)}, u32[]{:S(2)}) copy-start(s32[1,1,1,32,1]{3,4,2,1,0:T(1,128)} %param.26) | copy-start | bytes 388
  38.2 34.8 %copy-start.9 = (s32[1,1,1,32]{3,2,1,0:T(1,128)S(1)}, s32[1,1,1,32]{3,2,1,0:T(1,128)}, u32[]{:S(2)}) copy-start(s32[1,1,1,32]{3,2,1,0:T(1,128)} %param.25) | copy-start | bytes 388
  38.3 16.8 %collective-permute-start.7 = (bf16[1,1,32,256]{3,2,1,0:T(8,128)(2,1)S(1)}, bf16[1,1,32,256]{3,2,1,0:T(8,128)(2,1)S(1)}, u32[]{:S(2)}, u32[]{:S(2)}) collective-permute-start(bf16[1,1,32,256]{3,2,1,0:T(8,128)(2,1)S(1)} %get-tuple-element.48), channel_id=1, source_target_pairs={{4,0},{8,4},{12,8},{16,12},{20,16},{24,20},{28,24},{32,28},{36,32}... | collective-permute-start | bytes 49160 | tf_op jit(solution)/shard_map/ppermute | solution.py:28
  50.6 7.2 %collective-permute-start.6 = (bf16[1,1,32,256]{3,2,1,0:T(8,128)(2,1)S(1)}, bf16[1,1,32,256]{3,2,1,0:T(8,128)(2,1)S(1)}, u32[]{:S(2)}, u32[]{:S(2)}) collective-permute-start(bf16[1,1,32,256]{3,2,1,0:T(8,128)(2,1)S(1)} %get-tuple-element.47), channel_id=1, source_target_pairs={{0,4},{4,8},{8,12},{12,16},{16,20},{20,24},{24,28},{28,32},{32,36}... | collective-permute-start | bytes 49160 | tf_op jit(solution)/shard_map/ppermute | solution.py:26
  57.8 5.7 %collective-permute-start.9 = (bf16[1,6,32,256]{3,2,1,0:T(8,128)(2,1)S(1)}, bf16[1,6,32,256]{3,2,1,0:T(8,128)(2,1)S(1)}, u32[]{:S(2)}, u32[]{:S(2)}) collective-permute-start(bf16[1,6,32,256]{3,2,1,0:T(8,128)(2,1)S(1)} %pad_maximum_fusion.33), channel_id=1, source_target_pairs={{64,0},{128,64},{192,128},{256,192},{320,256},{384,320},{448,384},... | collective-permute-start | bytes 294920 | tf_op jit(solution)/shard_map/ppermute | solution.py:28
  60.6 6.6 %collective-permute-start.8 = (bf16[1,6,32,256]{3,2,1,0:T(8,128)(2,1)S(1)}, bf16[1,6,32,256]{3,2,1,0:T(8,128)(2,1)S(1)}, u32[]{:S(2)}, u32[]{:S(2)}) collective-permute-start(bf16[1,6,32,256]{3,2,1,0:T(8,128)(2,1)S(1)} %pad_maximum_fusion.33), channel_id=1, source_target_pairs={{0,64},{64,128},{128,192},{192,256},{256,320},{320,384},{384,448},... | collective-permute-start | bytes 294920 | tf_op jit(solution)/shard_map/ppermute | solution.py:26
  67.3 5.9 %collective-permute-start.11 = (bf16[3,6,4,256]{3,2,1,0:T(4,128)(2,1)S(1)}, bf16[3,6,4,256]{3,2,1,0:T(4,128)(2,1)S(1)}, u32[]{:S(2)}, u32[]{:S(2)}) collective-permute-start(bf16[3,6,4,256]{3,2,1,0:T(4,128)(2,1)S(1)} %get-tuple-element.37), channel_id=1, source_target_pairs={{1,0},{2,1},{3,2},{5,4},{6,5},{7,6},{9,8},{10,9},{11,10},{13,12},{... | collective-permute-start | bytes 110600 | tf_op jit(solution)/shard_map/ppermute | solution.py:28
  68.6 5.3 %collective-permute-start.10 = (bf16[3,6,4,256]{3,2,1,0:T(4,128)(2,1)S(1)}, bf16[3,6,4,256]{3,2,1,0:T(4,128)(2,1)S(1)}, u32[]{:S(2)}, u32[]{:S(2)}) collective-permute-start(bf16[3,6,4,256]{3,2,1,0:T(4,128)(2,1)S(1)} %get-tuple-element.38), channel_id=1, source_target_pairs={{0,1},{1,2},{2,3},{4,5},{5,6},{6,7},{8,9},{9,10},{10,11},{12,13},{... | collective-permute-start | bytes 110600 | tf_op jit(solution)/shard_map/ppermute | solution.py:26
  80.2 1.3 copy-start.8
  83.5 15.5 %collective-permute-start.13 = (bf16[1,1,32,128]{3,2,1,0:T(8,128)(2,1)S(1)}, bf16[1,1,32,128]{3,2,1,0:T(8,128)(2,1)S(1)}, u32[]{:S(2)}, u32[]{:S(2)}) collective-permute-start(bf16[1,1,32,128]{3,2,1,0:T(8,128)(2,1)S(1)} %get-tuple-element.52), channel_id=1, source_target_pairs={{4,0},{8,4},{12,8},{16,12},{20,16},{24,20},{28,24},{32,28},{36,32}... | collective-permute-start | bytes 24584 | tf_op jit(solution)/shard_map/ppermute | solution.py:28
  96.2 3.1 %collective-permute-start.12 = (bf16[1,1,32,128]{3,2,1,0:T(8,128)(2,1)S(1)}, bf16[1,1,32,128]{3,2,1,0:T(8,128)(2,1)S(1)}, u32[]{:S(2)}, u32[]{:S(2)}) collective-permute-start(bf16[1,1,32,128]{3,2,1,0:T(8,128)(2,1)S(1)} %get-tuple-element.51), channel_id=1, source_target_pairs={{0,4},{4,8},{8,12},{12,16},{16,20},{20,24},{24,28},{28,32},{32,36}... | collective-permute-start | bytes 24584 | tf_op jit(solution)/shard_map/ppermute | solution.py:26
  99.3 5.3 %collective-permute-start.15 = (bf16[1,6,32,128]{3,2,1,0:T(8,128)(2,1)S(1)}, bf16[1,6,32,128]{3,2,1,0:T(8,128)(2,1)S(1)}, u32[]{:S(2)}, u32[]{:S(2)}) collective-permute-start(bf16[1,6,32,128]{3,2,1,0:T(8,128)(2,1)S(1)} %pad_maximum_fusion.34), channel_id=1, source_target_pairs={{64,0},{128,64},{192,128},{256,192},{320,256},{384,320},{448,384},... | collective-permute-start | bytes 147464 | tf_op jit(solution)/shard_map/ppermute | solution.py:28
  101.2 6.0 %collective-permute-start.14 = (bf16[1,6,32,128]{3,2,1,0:T(8,128)(2,1)S(1)}, bf16[1,6,32,128]{3,2,1,0:T(8,128)(2,1)S(1)}, u32[]{:S(2)}, u32[]{:S(2)}) collective-permute-start(bf16[1,6,32,128]{3,2,1,0:T(8,128)(2,1)S(1)} %pad_maximum_fusion.34), channel_id=1, source_target_pairs={{0,64},{64,128},{128,192},{192,256},{256,320},{320,384},{384,448},... | collective-permute-start | bytes 147464 | tf_op jit(solution)/shard_map/ppermute | solution.py:26
  107.3 6.5 %collective-permute-start.16 = (bf16[3,6,4,128]{3,2,1,0:T(4,128)(2,1)S(1)}, bf16[3,6,4,128]{3,2,1,0:T(4,128)(2,1)S(1)}, u32[]{:S(2)}, u32[]{:S(2)}) collective-permute-start(bf16[3,6,4,128]{3,2,1,0:T(4,128)(2,1)S(1)} %get-tuple-element.45), channel_id=1, source_target_pairs={{0,1},{1,2},{2,3},{4,5},{5,6},{6,7},{8,9},{9,10},{10,11},{12,13},{... | collective-permute-start | bytes 55304 | tf_op jit(solution)/shard_map/ppermute | solution.py:26
  111.2 4.8 %collective-permute-start.17 = (bf16[3,6,4,128]{3,2,1,0:T(4,128)(2,1)S(1)}, bf16[3,6,4,128]{3,2,1,0:T(4,128)(2,1)S(1)}, u32[]{:S(2)}, u32[]{:S(2)}) collective-permute-start(bf16[3,6,4,128]{3,2,1,0:T(4,128)(2,1)S(1)} %get-tuple-element.46), channel_id=1, source_target_pairs={{1,0},{2,1},{3,2},{5,4},{6,5},{7,6},{9,8},{10,9},{11,10},{13,12},{... | collective-permute-start | bytes 55304 | tf_op jit(solution)/shard_map/ppermute | solution.py:28
  124.8 22.0 %copy-start.3 = (bf16[1,3,1024]{2,1,0:T(4,128)(2,1)S(1)}, bf16[1,3,1024]{2,1,0:T(4,128)(2,1)}, u32[]{:S(2)}) copy-start(bf16[1,3,1024]{2,1,0:T(4,128)(2,1)} %param.24) | copy-start | bytes 18436
  124.8 121.1 %all-to-all-start = ((bf16[128,2,64,128]{3,2,1,0:T(8,128)(2,1)}), bf16[128,2,64,128]{3,2,1,0:T(8,128)(2,1)}, u32[]{:S(2)}, u32[]{:S(2)}) async-start(bf16[128,2,64,128]{3,2,1,0:T(8,128)(2,1)} %bitcast.181), calls=%async_computation | async-start | bytes 8388608 | tf_op jit(solution)/shard_map/all_to_all | solution.py:211
  245.9 27.1 %copy-start.5 = (bf16[3,256]{1,0:T(4,128)(2,1)S(1)}, bf16[3,256]{1,0:T(4,128)(2,1)}, u32[]{:S(2)}) copy-start(bf16[3,256]{1,0:T(4,128)(2,1)} %param.22) | copy-start | bytes 4612
  263.6 25.4 %all-to-all-start.1 = ((f32[128,2,3]{2,1,0:T(2,128)}), f32[128,2,3]{2,1,0:T(2,128)S(1)}, u32[]{:S(2)}, u32[]{:S(2)}) async-start(f32[128,2,3]{2,1,0:T(2,128)} %bitcast.201), calls=%async_computation.1 | async-start | bytes 262144 | tf_op jit(solution)/shard_map/all_to_all | solution.py:221

commit v9 on v3

--- a/solution.py
+++ b/solution.py
@@ -64,7 +64,7 @@
 
 def ghosts(values):
     deeper = with_halo(values, (("gz", 2),), M, False)
-    return with_halo(deeper, (("gx", 0), ("gy", 1)), 1, True)
+    return with_halo(deeper, (("gy", 1), ("gx", 0)), 1, True)
 
 
 def candidates(padded, cells_x, cells_y, cells_z):

time: 290 us -> 286 us (0.986)
  waiting for transfers between devices: 135 us -> 128 us
  starting transfers between devices: 96.2 us -> 101 us
    ppermute x9, waiting for transfers between devices: 19.5 us -> 8.02 us  [with_halo(): lax.ppermute(tail, axis, [(i, (i + 1) % count) for i in range(ends)])]
    ppermute x9, waiting for transfers between devices: 3.03 us -> 7.67 us  [with_halo(): lax.ppermute(head, axis, [((i + 1) % count, i) for i in range(ends)])]
    unnamed x97 -> x99, local copies, waits for them, and re-layouts: 6.33 us -> 6.33 us
  transfers between devices with their start and end apart: 20 -> 20, of which waited for: 9 -> 11; matrix products, arithmetic and copies ran while one was open for 5% -> 6% of each run, Pallas kernels for 0% -> 0%
where the time goes in v9:
time: 286 us; the launch traced here: 285 us
  waiting for transfers between devices  128 us (45%)
  starting transfers between devices  101 us (35%)
  Pallas kernels  17.6 us (6%)
  local copies, waits for them, and re-layouts  16.4 us (6%)
  matrix products  10.7 us (4%)
  other arithmetic  9.02 us (3%)
    all_to_all x1, waiting for transfers between devices, per_device(): lax.all_to_all(outgoing.reshape(owner_total, capacity, slots, env_width),...  96.9 us
    ppermute x9, starting transfers between devices, with_halo(): lax.ppermute(head, axis, [((i + 1) % count, i) for i in range(ends)])  46.5 us
    ppermute x9, starting transfers between devices, with_halo(): lax.ppermute(tail, axis, [(i, (i + 1) % count) for i in range(ends)])  29.6 us
    pallas_call x1, Pallas kernels, specialist(): pl.pallas_call(specialist_kernel, grid=(env_total // block,), in_specs=[p...  17.6 us
    all_to_all x1, starting transfers between devices, per_device(): lax.all_to_all(outgoing.reshape(owner_total, capacity, slots, env_width),...  15.7 us
    all_to_all x1, waiting for transfers between devices, per_device(): lax.all_to_all(results, ('gx', 'gy'), split_axis=0, concat_axis=0, tiled=...  15.6 us
    all_to_all x1, starting transfers between devices, per_device(): lax.all_to_all(results, ('gx', 'gy'), split_axis=0, concat_axis=0, tiled=...  9.57 us
    ppermute x9, waiting for transfers between devices, with_halo(): lax.ppermute(tail, axis, [(i, (i + 1) % count) for i in range(ends)])  8.02 us
  transfers between devices with their start and end apart: 20, of which 11 were waited for; matrix products, arithmetic and copies ran while one was open for 6% of the time, Pallas kernels for 0%

profile of v9, /device:TPU:1, one launch (start us, length us, event | category | flops | bytes accessed | tf_op | source)
XLA Modules:
  0.0 285.0 jit_solution(13552067015827310242)
XLA Ops:
  0.8 1.3 collective-permute-start.1
  2.1 5.4 %collective-permute-start = (bf16[1,4,4,256]{3,2,1,0:T(4,128)(2,1)S(1)}, bf16[1,4,4,256]{3,2,1,0:T(4,128)(2,1)S(1)}, u32[]{:S(2)}, u32[]{:S(2)}) collective-permute-start(bf16[1,4,4,256]{3,2,1,0:T(4,128)(2,1)S(1)} %get-tuple-element.80), channel_id=1, source_target_pairs={{0,1},{1,2},{2,3},{4,5},{5,6},{6,7},{8,9},{9,10},{10,11},{12,13},{... | collective-permute-start | bytes 24584 | tf_op jit(solution)/shard_map/ppermute | solution.py:26
  9.4 4.0 %iota_compare_fusion = pred[128,64,108]{2,1,0:T(8,128)(4,1)S(1)} fusion(s32[128,64]{1,0:T(8,128)} %bitcast.295), kind=kLoop, calls=%fused_computation.6 | loop fusion | flops 884736 | bytes 917504 | tf_op jit(solution)/shard_map/eq | solution.py:169
  14.1 2.8 convolution_convert_fusion.1
  17.2 7.9 %collective-permute-start.3 = (bf16[1,1,40,256]{3,2,1,0:T(8,128)(2,1)S(1)}, bf16[1,1,40,256]{3,2,1,0:T(8,128)(2,1)S(1)}, u32[]{:S(2)}, u32[]{:S(2)}) collective-permute-start(bf16[1,1,40,256]{3,2,1,0:T(8,128)(2,1)S(1)} %get-tuple-element.73), channel_id=1, source_target_pairs={{4,0},{8,4},{12,8},{16,12},{20,16},{24,20},{28,24},{32,28},{36,32}... | collective-permute-start | bytes 61448 | tf_op jit(solution)/shard_map/ppermute | solution.py:28
  25.0 1.9 collective-permute-start.2
  27.1 5.2 %collective-permute-done.2 = bf16[1,1,40,256]{3,2,1,0:T(8,128)(2,1)S(1)} collective-permute-done((bf16[1,1,40,256]{3,2,1,0:T(8,128)(2,1)S(1)}, bf16[1,1,40,256]{3,2,1,0:T(8,128)(2,1)S(1)}, u32[]{:S(2)}, u32[]{:S(2)}) %collective-permute-start.2) | collective-permute-done | bytes 20512 | tf_op jit(solution)/shard_map/ppermute | solution.py:26
  32.4 3.2 %collective-permute-start.4 = (bf16[1,6,40,256]{3,2,1,0:T(8,128)(2,1)S(1)}, bf16[1,6,40,256]{3,2,1,0:T(8,128)(2,1)S(1)}, u32[]{:S(2)}, u32[]{:S(2)}) collective-permute-start(bf16[1,6,40,256]{3,2,1,0:T(8,128)(2,1)S(1)} %pad_maximum_fusion.1), channel_id=1, source_target_pairs={{0,64},{64,128},{128,192},{192,256},{256,320},{320,384},{384,448},... | collective-permute-start | bytes 368648 | tf_op jit(solution)/shard_map/ppermute | solution.py:26
  35.6 3.8 %collective-permute-start.5 = (bf16[1,6,40,256]{3,2,1,0:T(8,128)(2,1)S(1)}, bf16[1,6,40,256]{3,2,1,0:T(8,128)(2,1)S(1)}, u32[]{:S(2)}, u32[]{:S(2)}) collective-permute-start(bf16[1,6,40,256]{3,2,1,0:T(8,128)(2,1)S(1)} %pad_maximum_fusion.1), channel_id=1, source_target_pairs={{64,0},{128,64},{192,128},{256,192},{320,256},{384,320},{448,384},... | collective-permute-start | bytes 368648 | tf_op jit(solution)/shard_map/ppermute | solution.py:28
  45.3 1.8 multiply_reduce_fusion.1
  47.3 3.1 %collective-permute-start.6 = (bf16[1,4,4,256]{3,1,2,0:T(4,128)(2,1)S(1)}, bf16[1,4,4,256]{3,1,2,0:T(4,128)(2,1)S(1)}, u32[]{:S(2)}, u32[]{:S(2)}) collective-permute-start(bf16[1,4,4,256]{3,1,2,0:T(4,128)(2,1)S(1)} %get-tuple-element.77), channel_id=1, source_target_pairs={{0,1},{1,2},{2,3},{4,5},{5,6},{6,7},{8,9},{9,10},{10,11},{12,13},{... | collective-permute-start | bytes 24584 | tf_op jit(solution)/shard_map/ppermute | solution.py:26
  51.2 1.3 collective-permute-start.7
  52.6 3.0 %collective-permute-done.7 = bf16[1,4,4,256]{3,1,2,0:T(4,128)(2,1)S(1)} collective-permute-done((bf16[1,4,4,256]{3,1,2,0:T(4,128)(2,1)S(1)}, bf16[1,4,4,256]{3,1,2,0:T(4,128)(2,1)S(1)}, u32[]{:S(2)}, u32[]{:S(2)}) %collective-permute-start.7) | collective-permute-done | bytes 8224 | tf_op jit(solution)/shard_map/ppermute | solution.py:28
  55.7 13.5 %collective-permute-start.9 = (bf16[1,1,40,256]{3,1,2,0:T(2,128)(2,1)S(1)}, bf16[1,1,40,256]{3,1,2,0:T(2,128)(2,1)S(1)}, u32[]{:S(2)}, u32[]{:S(2)}) collective-permute-start(bf16[1,1,40,256]{3,1,2,0:T(2,128)(2,1)S(1)} %get-tuple-element.69), channel_id=1, source_target_pairs={{4,0},{8,4},{12,8},{16,12},{20,16},{24,20},{28,24},{32,28},{36,32}... | collective-permute-start | bytes 61448 | tf_op jit(solution)/shard_map/ppermute | solution.py:28
  69.2 1.9 collective-permute-start.8
  72.4 3.2 %collective-permute-start.10 = (bf16[1,6,40,256]{3,1,2,0:T(8,128)(2,1)S(1)}, bf16[1,6,40,256]{3,1,2,0:T(8,128)(2,1)S(1)}, u32[]{:S(2)}, u32[]{:S(2)}) collective-permute-start(bf16[1,6,40,256]{3,1,2,0:T(8,128)(2,1)S(1)} %pad_maximum_fusion), channel_id=1, source_target_pairs={{0,64},{64,128},{128,192},{192,256},{256,320},{320,384},{384,448},... | collective-permute-start | bytes 368648 | tf_op jit(solution)/shard_map/ppermute | solution.py:26
  75.7 3.6 %collective-permute-start.11 = (bf16[1,6,40,256]{3,1,2,0:T(8,128)(2,1)S(1)}, bf16[1,6,40,256]{3,1,2,0:T(8,128)(2,1)S(1)}, u32[]{:S(2)}, u32[]{:S(2)}) collective-permute-start(bf16[1,6,40,256]{3,1,2,0:T(8,128)(2,1)S(1)} %pad_maximum_fusion), channel_id=1, source_target_pairs={{64,0},{128,64},{192,128},{256,192},{320,256},{384,320},{448,384},... | collective-permute-start | bytes 368648 | tf_op jit(solution)/shard_map/ppermute | solution.py:28
  81.1 1.3 collective-permute-done.11
  85.3 1.8 multiply_reduce_fusion
  87.4 1.3 collective-permute-start.13
  88.7 4.0 %collective-permute-start.12 = (bf16[1,4,4,128]{3,2,1,0:T(4,128)(2,1)S(1)}, bf16[1,4,4,128]{3,2,1,0:T(4,128)(2,1)S(1)}, u32[]{:S(2)}, u32[]{:S(2)}) collective-permute-start(bf16[1,4,4,128]{3,2,1,0:T(4,128)(2,1)S(1)} %get-tuple-element.112), channel_id=1, source_target_pairs={{0,1},{1,2},{2,3},{4,5},{5,6},{6,7},{8,9},{9,10},{10,11},{12,13},{... | collective-permute-start | bytes 12296 | tf_op jit(solution)/shard_map/ppermute | solution.py:26
  93.9 11.9 %collective-permute-start.15 = (bf16[1,1,40,128]{3,2,1,0:T(8,128)(2,1)S(1)}, bf16[1,1,40,128]{3,2,1,0:T(8,128)(2,1)S(1)}, u32[]{:S(2)}, u32[]{:S(2)}) collective-permute-start(bf16[1,1,40,128]{3,2,1,0:T(8,128)(2,1)S(1)} %get-tuple-element.109), channel_id=1, source_target_pairs={{4,0},{8,4},{12,8},{16,12},{20,16},{24,20},{28,24},{32,28},{36,32}... | collective-permute-start | bytes 30728 | tf_op jit(solution)/shard_map/ppermute | solution.py:28
  105.8 1.9 collective-permute-start.14
  108.9 4.8 %collective-permute-start.16 = (bf16[1,6,40,128]{3,2,1,0:T(8,128)(2,1)S(1)}, bf16[1,6,40,128]{3,2,1,0:T(8,128)(2,1)S(1)}, u32[]{:S(2)}, u32[]{:S(2)}) collective-permute-start(bf16[1,6,40,128]{3,2,1,0:T(8,128)(2,1)S(1)} %pad_maximum_fusion.9), channel_id=1, source_target_pairs={{0,64},{64,128},{128,192},{192,256},{256,320},{320,384},{384,448},... | collective-permute-start | bytes 184328 | tf_op jit(solution)/shard_map/ppermute | solution.py:26
  113.8 1.9 collective-permute-start.17
  116.3 2.7 collective-permute-done.17
  122.2 3.2 %copy.104 = bf16[32,8,64,128]{3,2,1,0:T(8,128)(2,1)} copy(bf16[32,8,64,128]{3,1,2,0:T(8,128)(2,1)S(1)} %fusion) | data formatting | bytes 8388608
  125.5 15.7 %all-to-all-start = ((bf16[128,2,64,128]{3,2,1,0:T(8,128)(2,1)}), bf16[128,2,64,128]{3,2,1,0:T(8,128)(2,1)}, u32[]{:S(2)}, u32[]{:S(2)}) async-start(bf16[128,2,64,128]{3,2,1,0:T(8,128)(2,1)} %bitcast.192), calls=%async_computation | async-start | bytes 8388608 | tf_op jit(solution)/shard_map/all_to_all | solution.py:216
  143.4 96.9 %all-to-all-done = bf16[128,2,64,128]{3,2,1,0:T(8,128)(2,1)} async-done(((bf16[128,2,64,128]{3,2,1,0:T(8,128)(2,1)}), bf16[128,2,64,128]{3,2,1,0:T(8,128)(2,1)}, u32[]{:S(2)}, u32[]{:S(2)}) %all-to-all-start) | async-done | bytes 4194336 | tf_op jit(solution)/shard_map/all_to_all | solution.py:216
  240.3 17.6 %shard_map.127 = f32[256,128]{1,0:T(8,128)} custom-call(bf16[16384,128]{1,0:T(8,128)(2,1)} %bitcast.103.env_ref, bf16[128,1024]{1,0:T(8,128)(2,1)} %bitcast.214, bf16[1024,128]{1,0:T(8,128)(2,1)} %scatter.4.head_ref), custom_call_target="tpu_custom_call" | custom-call | tf_op jit(solution)/shard_map/pallas_call | solution.py:134
  257.9 9.6 %all-to-all-start.1 = ((f32[128,2,3]{2,1,0:T(2,128)}), f32[128,2,3]{2,1,0:T(2,128)S(1)}, u32[]{:S(2)}, u32[]{:S(2)}) async-start(f32[128,2,3]{2,1,0:T(2,128)} %bitcast.210), calls=%async_computation.1 | async-start | bytes 262144 | tf_op jit(solution)/shard_map/all_to_all | solution.py:226
  267.8 15.6 %all-to-all-done.1 = f32[128,2,3]{2,1,0:T(2,128)S(1)} async-done(((f32[128,2,3]{2,1,0:T(2,128)}), f32[128,2,3]{2,1,0:T(2,128)S(1)}, u32[]{:S(2)}, u32[]{:S(2)}) %all-to-all-start.1) | async-done | bytes 3104 | tf_op jit(solution)/shard_map/all_to_all | solution.py:226
  (202 shorter events, 25.9 us)
Async XLA Ops:
  0.0 87.1 %copy-start = (bf16[256,128]{1,0:T(8,128)(2,1)S(1)}, bf16[256,128]{1,0:T(8,128)(2,1)}, u32[]{:S(2)}) copy-start(bf16[256,128]{1,0:T(8,128)(2,1)} %param.21) | copy-start | bytes 196612
  0.0 17.0 %copy-start.1 = (bf16[1,4,32,256]{3,2,1,0:T(8,128)(2,1)S(1)}, bf16[1,4,32,256]{3,2,1,0:T(8,128)(2,1)}, u32[]{:S(2)}) copy-start(bf16[1,4,32,256]{3,2,1,0:T(8,128)(2,1)} %param.15) | copy-start | bytes 196612
  0.0 17.0 %copy-start.6 = (s32[1,1,1,32]{3,2,1,0:T(1,128)S(1)}, s32[1,1,1,32]{3,2,1,0:T(1,128)}, u32[]{:S(2)}) copy-start(s32[1,1,1,32]{3,2,1,0:T(1,128)} %param.25) | copy-start | bytes 388
  0.8 16.3 %collective-permute-start.1 = (bf16[1,4,4,256]{3,2,1,0:T(4,128)(2,1)S(1)}, bf16[1,4,4,256]{3,2,1,0:T(4,128)(2,1)S(1)}, u32[]{:S(2)}, u32[]{:S(2)}) collective-permute-start(bf16[1,4,4,256]{3,2,1,0:T(4,128)(2,1)S(1)} %get-tuple-element.81), channel_id=1, source_target_pairs={{1,0},{2,1},{3,2},{5,4},{6,5},{7,6},{9,8},{10,9},{11,10},{13,12},{... | collective-permute-start | bytes 24584 | tf_op jit(solution)/shard_map/ppermute | solution.py:28
  2.1 15.0 %collective-permute-start = (bf16[1,4,4,256]{3,2,1,0:T(4,128)(2,1)S(1)}, bf16[1,4,4,256]{3,2,1,0:T(4,128)(2,1)S(1)}, u32[]{:S(2)}, u32[]{:S(2)}) collective-permute-start(bf16[1,4,4,256]{3,2,1,0:T(4,128)(2,1)S(1)} %get-tuple-element.80), channel_id=1, source_target_pairs={{0,1},{1,2},{2,3},{4,5},{5,6},{6,7},{8,9},{9,10},{10,11},{12,13},{... | collective-permute-start | bytes 24584 | tf_op jit(solution)/shard_map/ppermute | solution.py:26
  17.2 10.0 %collective-permute-start.3 = (bf16[1,1,40,256]{3,2,1,0:T(8,128)(2,1)S(1)}, bf16[1,1,40,256]{3,2,1,0:T(8,128)(2,1)S(1)}, u32[]{:S(2)}, u32[]{:S(2)}) collective-permute-start(bf16[1,1,40,256]{3,2,1,0:T(8,128)(2,1)S(1)} %get-tuple-element.73), channel_id=1, source_target_pairs={{4,0},{8,4},{12,8},{16,12},{20,16},{24,20},{28,24},{32,28},{36,32}... | collective-permute-start | bytes 61448 | tf_op jit(solution)/shard_map/ppermute | solution.py:28
  25.0 7.3 %collective-permute-start.2 = (bf16[1,1,40,256]{3,2,1,0:T(8,128)(2,1)S(1)}, bf16[1,1,40,256]{3,2,1,0:T(8,128)(2,1)S(1)}, u32[]{:S(2)}, u32[]{:S(2)}) collective-permute-start(bf16[1,1,40,256]{3,2,1,0:T(8,128)(2,1)S(1)} %get-tuple-element.72), channel_id=1, source_target_pairs={{0,4},{4,8},{8,12},{12,16},{16,20},{20,24},{24,28},{28,32},{32,36}... | collective-permute-start | bytes 61448 | tf_op jit(solution)/shard_map/ppermute | solution.py:26
  32.4 7.7 %collective-permute-start.4 = (bf16[1,6,40,256]{3,2,1,0:T(8,128)(2,1)S(1)}, bf16[1,6,40,256]{3,2,1,0:T(8,128)(2,1)S(1)}, u32[]{:S(2)}, u32[]{:S(2)}) collective-permute-start(bf16[1,6,40,256]{3,2,1,0:T(8,128)(2,1)S(1)} %pad_maximum_fusion.1), channel_id=1, source_target_pairs={{0,64},{64,128},{128,192},{192,256},{256,320},{320,384},{384,448},... | collective-permute-start | bytes 368648 | tf_op jit(solution)/shard_map/ppermute | solution.py:26
  35.6 5.7 %collective-permute-start.5 = (bf16[1,6,40,256]{3,2,1,0:T(8,128)(2,1)S(1)}, bf16[1,6,40,256]{3,2,1,0:T(8,128)(2,1)S(1)}, u32[]{:S(2)}, u32[]{:S(2)}) collective-permute-start(bf16[1,6,40,256]{3,2,1,0:T(8,128)(2,1)S(1)} %pad_maximum_fusion.1), channel_id=1, source_target_pairs={{64,0},{128,64},{192,128},{256,192},{320,256},{384,320},{448,384},... | collective-permute-start | bytes 368648 | tf_op jit(solution)/shard_map/ppermute | solution.py:28
  44.0 1.3 copy-start.5
  45.3 5.1 %copy-start.3 = (s32[1,1,1,32,1]{3,4,2,1,0:T(1,128)S(1)}, s32[1,1,1,32,1]{3,4,2,1,0:T(1,128)}, u32[]{:S(2)}) copy-start(s32[1,1,1,32,1]{3,4,2,1,0:T(1,128)} %param.26) | copy-start | bytes 388
  47.3 5.3 %collective-permute-start.6 = (bf16[1,4,4,256]{3,1,2,0:T(4,128)(2,1)S(1)}, bf16[1,4,4,256]{3,1,2,0:T(4,128)(2,1)S(1)}, u32[]{:S(2)}, u32[]{:S(2)}) collective-permute-start(bf16[1,4,4,256]{3,1,2,0:T(4,128)(2,1)S(1)} %get-tuple-element.77), channel_id=1, source_target_pairs={{0,1},{1,2},{2,3},{4,5},{5,6},{6,7},{8,9},{9,10},{10,11},{12,13},{... | collective-permute-start | bytes 24584 | tf_op jit(solution)/shard_map/ppermute | solution.py:26
  51.2 4.4 %collective-permute-start.7 = (bf16[1,4,4,256]{3,1,2,0:T(4,128)(2,1)S(1)}, bf16[1,4,4,256]{3,1,2,0:T(4,128)(2,1)S(1)}, u32[]{:S(2)}, u32[]{:S(2)}) collective-permute-start(bf16[1,4,4,256]{3,1,2,0:T(4,128)(2,1)S(1)} %get-tuple-element.76), channel_id=1, source_target_pairs={{1,0},{2,1},{3,2},{5,4},{6,5},{7,6},{9,8},{10,9},{11,10},{13,12},{... | collective-permute-start | bytes 24584 | tf_op jit(solution)/shard_map/ppermute | solution.py:28
  55.7 15.5 %collective-permute-start.9 = (bf16[1,1,40,256]{3,1,2,0:T(2,128)(2,1)S(1)}, bf16[1,1,40,256]{3,1,2,0:T(2,128)(2,1)S(1)}, u32[]{:S(2)}, u32[]{:S(2)}) collective-permute-start(bf16[1,1,40,256]{3,1,2,0:T(2,128)(2,1)S(1)} %get-tuple-element.69), channel_id=1, source_target_pairs={{4,0},{8,4},{12,8},{16,12},{20,16},{24,20},{28,24},{32,28},{36,32}... | collective-permute-start | bytes 61448 | tf_op jit(solution)/shard_map/ppermute | solution.py:28
  69.2 3.1 %collective-permute-start.8 = (bf16[1,1,40,256]{3,1,2,0:T(2,128)(2,1)S(1)}, bf16[1,1,40,256]{3,1,2,0:T(2,128)(2,1)S(1)}, u32[]{:S(2)}, u32[]{:S(2)}) collective-permute-start(bf16[1,1,40,256]{3,1,2,0:T(2,128)(2,1)S(1)} %get-tuple-element.68), channel_id=1, source_target_pairs={{0,4},{4,8},{8,12},{12,16},{16,20},{20,24},{24,28},{28,32},{32,36}... | collective-permute-start | bytes 61448 | tf_op jit(solution)/shard_map/ppermute | solution.py:26
  72.4 7.7 %collective-permute-start.10 = (bf16[1,6,40,256]{3,1,2,0:T(8,128)(2,1)S(1)}, bf16[1,6,40,256]{3,1,2,0:T(8,128)(2,1)S(1)}, u32[]{:S(2)}, u32[]{:S(2)}) collective-permute-start(bf16[1,6,40,256]{3,1,2,0:T(8,128)(2,1)S(1)} %pad_maximum_fusion), channel_id=1, source_target_pairs={{0,64},{64,128},{128,192},{192,256},{256,320},{320,384},{384,448},... | collective-permute-start | bytes 368648 | tf_op jit(solution)/shard_map/ppermute | solution.py:26
  75.7 6.7 %collective-permute-start.11 = (bf16[1,6,40,256]{3,1,2,0:T(8,128)(2,1)S(1)}, bf16[1,6,40,256]{3,1,2,0:T(8,128)(2,1)S(1)}, u32[]{:S(2)}, u32[]{:S(2)}) collective-permute-start(bf16[1,6,40,256]{3,1,2,0:T(8,128)(2,1)S(1)} %pad_maximum_fusion), channel_id=1, source_target_pairs={{64,0},{128,64},{192,128},{256,192},{320,256},{384,320},{448,384},... | collective-permute-start | bytes 368648 | tf_op jit(solution)/shard_map/ppermute | solution.py:28
  87.4 6.5 %collective-permute-start.13 = (bf16[1,4,4,128]{3,2,1,0:T(4,128)(2,1)S(1)}, bf16[1,4,4,128]{3,2,1,0:T(4,128)(2,1)S(1)}, u32[]{:S(2)}, u32[]{:S(2)}) collective-permute-start(bf16[1,4,4,128]{3,2,1,0:T(4,128)(2,1)S(1)} %get-tuple-element.113), channel_id=1, source_target_pairs={{1,0},{2,1},{3,2},{5,4},{6,5},{7,6},{9,8},{10,9},{11,10},{13,12},{... | collective-permute-start | bytes 12296 | tf_op jit(solution)/shard_map/ppermute | solution.py:28
  88.7 5.2 %collective-permute-start.12 = (bf16[1,4,4,128]{3,2,1,0:T(4,128)(2,1)S(1)}, bf16[1,4,4,128]{3,2,1,0:T(4,128)(2,1)S(1)}, u32[]{:S(2)}, u32[]{:S(2)}) collective-permute-start(bf16[1,4,4,128]{3,2,1,0:T(4,128)(2,1)S(1)} %get-tuple-element.112), channel_id=1, source_target_pairs={{0,1},{1,2},{2,3},{4,5},{5,6},{6,7},{8,9},{9,10},{10,11},{12,13},{... | collective-permute-start | bytes 12296 | tf_op jit(solution)/shard_map/ppermute | solution.py:26
  93.9 13.9 %collective-permute-start.15 = (bf16[1,1,40,128]{3,2,1,0:T(8,128)(2,1)S(1)}, bf16[1,1,40,128]{3,2,1,0:T(8,128)(2,1)S(1)}, u32[]{:S(2)}, u32[]{:S(2)}) collective-permute-start(bf16[1,1,40,128]{3,2,1,0:T(8,128)(2,1)S(1)} %get-tuple-element.109), channel_id=1, source_target_pairs={{4,0},{8,4},{12,8},{16,12},{20,16},{24,20},{28,24},{32,28},{36,32}... | collective-permute-start | bytes 30728 | tf_op jit(solution)/shard_map/ppermute | solution.py:28
  105.8 3.1 %collective-permute-start.14 = (bf16[1,1,40,128]{3,2,1,0:T(8,128)(2,1)S(1)}, bf16[1,1,40,128]{3,2,1,0:T(8,128)(2,1)S(1)}, u32[]{:S(2)}, u32[]{:S(2)}) collective-permute-start(bf16[1,1,40,128]{3,2,1,0:T(8,128)(2,1)S(1)} %get-tuple-element.108), channel_id=1, source_target_pairs={{0,4},{4,8},{8,12},{12,16},{16,20},{20,24},{24,28},{28,32},{32,36}... | collective-permute-start | bytes 30728 | tf_op jit(solution)/shard_map/ppermute | solution.py:26
  108.9 6.9 %collective-permute-start.16 = (bf16[1,6,40,128]{3,2,1,0:T(8,128)(2,1)S(1)}, bf16[1,6,40,128]{3,2,1,0:T(8,128)(2,1)S(1)}, u32[]{:S(2)}, u32[]{:S(2)}) collective-permute-start(bf16[1,6,40,128]{3,2,1,0:T(8,128)(2,1)S(1)} %pad_maximum_fusion.9), channel_id=1, source_target_pairs={{0,64},{64,128},{128,192},{192,256},{256,320},{320,384},{384,448},... | collective-permute-start | bytes 184328 | tf_op jit(solution)/shard_map/ppermute | solution.py:26
  113.8 5.2 %collective-permute-start.17 = (bf16[1,6,40,128]{3,2,1,0:T(8,128)(2,1)S(1)}, bf16[1,6,40,128]{3,2,1,0:T(8,128)(2,1)S(1)}, u32[]{:S(2)}, u32[]{:S(2)}) collective-permute-start(bf16[1,6,40,128]{3,2,1,0:T(8,128)(2,1)S(1)} %pad_maximum_fusion.9), channel_id=1, source_target_pairs={{64,0},{128,64},{192,128},{256,192},{320,256},{384,320},{448,384},... | collective-permute-start | bytes 184328 | tf_op jit(solution)/shard_map/ppermute | solution.py:28
  125.5 15.7 %copy-start.2 = (bf16[1,3,1024]{2,1,0:T(4,128)(2,1)S(1)}, bf16[1,3,1024]{2,1,0:T(4,128)(2,1)}, u32[]{:S(2)}) copy-start(bf16[1,3,1024]{2,1,0:T(4,128)(2,1)} %param.24) | copy-start | bytes 18436
  125.5 114.8 %all-to-all-start = ((bf16[128,2,64,128]{3,2,1,0:T(8,128)(2,1)}), bf16[128,2,64,128]{3,2,1,0:T(8,128)(2,1)}, u32[]{:S(2)}, u32[]{:S(2)}) async-start(bf16[128,2,64,128]{3,2,1,0:T(8,128)(2,1)} %bitcast.192), calls=%async_computation | async-start | bytes 8388608 | tf_op jit(solution)/shard_map/all_to_all | solution.py:216
  240.3 27.2 %copy-start.4 = (bf16[3,256]{1,0:T(4,128)(2,1)S(1)}, bf16[3,256]{1,0:T(4,128)(2,1)}, u32[]{:S(2)}) copy-start(bf16[3,256]{1,0:T(4,128)(2,1)} %param.22) | copy-start | bytes 4612
  257.9 25.5 %all-to-all-start.1 = ((f32[128,2,3]{2,1,0:T(2,128)}), f32[128,2,3]{2,1,0:T(2,128)S(1)}, u32[]{:S(2)}, u32[]{:S(2)}) async-start(f32[128,2,3]{2,1,0:T(2,128)} %bitcast.210), calls=%async_computation.1 | async-start | bytes 262144 | tf_op jit(solution)/shard_map/all_to_all | solution.py:226

commit v10 on v9

--- a/solution.py
+++ b/solution.py
@@ -102,7 +102,7 @@
 
 
 def specialist_kernel(env_ref, first_ref, head_ref, out_ref):
-    piece = 64
+    piece = 128
     slots = env_ref.shape[0] // out_ref.shape[0]
     span = piece * slots
     column = lax.broadcasted_iota(jnp.int32, (piece, span), 1)
@@ -129,7 +129,7 @@
     sources, item_count, slots, env_width = received.shape
     env_total = sources * item_count
     hidden_width = w_first.shape[-1]
-    block = math.gcd(env_total, 64)
+    block = math.gcd(env_total, 128)
     head = jnp.zeros((hidden_width, 128), jnp.bfloat16).at[:, : w_head.shape[0]].set(w_head.T)
     results = pl.pallas_call(
         specialist_kernel,

time: 286 us -> 285 us (level)
  no operation moved by 1% of the time
where the time goes in v10:
time: 285 us; the launch traced here: 284 us
  waiting for transfers between devices  128 us (45%)
  starting transfers between devices  101 us (35%)
  Pallas kernels  16.6 us (6%)
  local copies, waits for them, and re-layouts  16.4 us (6%)
  matrix products  10.7 us (4%)
  other arithmetic  9.02 us (3%)
    all_to_all x1, waiting for transfers between devices, per_device(): lax.all_to_all(outgoing.reshape(owner_total, capacity, slots, env_width),...  96.9 us
    ppermute x9, starting transfers between devices, with_halo(): lax.ppermute(head, axis, [((i + 1) % count, i) for i in range(ends)])  46.5 us
    ppermute x9, starting transfers between devices, with_halo(): lax.ppermute(tail, axis, [(i, (i + 1) % count) for i in range(ends)])  29.6 us
    pallas_call x1, Pallas kernels, specialist(): pl.pallas_call(specialist_kernel, grid=(env_total // block,), in_specs=[p...  16.6 us
    all_to_all x1, starting transfers between devices, per_device(): lax.all_to_all(outgoing.reshape(owner_total, capacity, slots, env_width),...  15.7 us
    all_to_all x1, waiting for transfers between devices, per_device(): lax.all_to_all(results, ('gx', 'gy'), split_axis=0, concat_axis=0, tiled=...  15.6 us
    all_to_all x1, starting transfers between devices, per_device(): lax.all_to_all(results, ('gx', 'gy'), split_axis=0, concat_axis=0, tiled=...  9.57 us
    ppermute x9, waiting for transfers between devices, with_halo(): lax.ppermute(tail, axis, [(i, (i + 1) % count) for i in range(ends)])  8.02 us
  transfers between devices with their start and end apart: 20, of which 11 were waited for; matrix products, arithmetic and copies ran while one was open for 6% of the time, Pallas kernels for 0%

profile of v10, /device:TPU:1, one launch (start us, length us, event | category | flops | bytes accessed | tf_op | source)
XLA Modules:
  0.0 283.9 jit_solution(4237959453653331821)
XLA Ops:
  0.8 1.3 collective-permute-start.1
  2.1 5.4 %collective-permute-start = (bf16[1,4,4,256]{3,2,1,0:T(4,128)(2,1)S(1)}, bf16[1,4,4,256]{3,2,1,0:T(4,128)(2,1)S(1)}, u32[]{:S(2)}, u32[]{:S(2)}) collective-permute-start(bf16[1,4,4,256]{3,2,1,0:T(4,128)(2,1)S(1)} %get-tuple-element.80), channel_id=1, source_target_pairs={{0,1},{1,2},{2,3},{4,5},{5,6},{6,7},{8,9},{9,10},{10,11},{12,13},{... | collective-permute-start | bytes 24584 | tf_op jit(solution)/shard_map/ppermute | solution.py:26
  9.4 4.0 %iota_compare_fusion = pred[128,64,108]{2,1,0:T(8,128)(4,1)S(1)} fusion(s32[128,64]{1,0:T(8,128)} %bitcast.295), kind=kLoop, calls=%fused_computation.6 | loop fusion | flops 884736 | bytes 917504 | tf_op jit(solution)/shard_map/eq | solution.py:169
  14.1 2.8 %convolution_convert_fusion.1 = bf16[128,8,108]{2,1,0:T(8,128)(2,1)S(1)} fusion(f32[128,64]{1,0:T(8,128)S(1)} %add_multiply_fusion, f32[8]{0:T(128)S(1)} %multiply_add_fusion, f32[128,64]{1,0:T(8,128)} %bitcast.297, s32[128,64]{1,0:T(8,128)} %bitcast.296), kind=kOutput, calls=%fused_computation.16 | convolution fusion | flops 15478784 | bytes 319520 | tf_op jit(solution)/shard_map/ask,asc->akc/dot_general | solution.py:170
  17.2 7.9 %collective-permute-start.3 = (bf16[1,1,40,256]{3,2,1,0:T(8,128)(2,1)S(1)}, bf16[1,1,40,256]{3,2,1,0:T(8,128)(2,1)S(1)}, u32[]{:S(2)}, u32[]{:S(2)}) collective-permute-start(bf16[1,1,40,256]{3,2,1,0:T(8,128)(2,1)S(1)} %get-tuple-element.73), channel_id=1, source_target_pairs={{4,0},{8,4},{12,8},{16,12},{20,16},{24,20},{28,24},{32,28},{36,32}... | collective-permute-start | bytes 61448 | tf_op jit(solution)/shard_map/ppermute | solution.py:28
  25.0 1.9 collective-permute-start.2
  27.1 5.2 %collective-permute-done.2 = bf16[1,1,40,256]{3,2,1,0:T(8,128)(2,1)S(1)} collective-permute-done((bf16[1,1,40,256]{3,2,1,0:T(8,128)(2,1)S(1)}, bf16[1,1,40,256]{3,2,1,0:T(8,128)(2,1)S(1)}, u32[]{:S(2)}, u32[]{:S(2)}) %collective-permute-start.2) | collective-permute-done | bytes 20512 | tf_op jit(solution)/shard_map/ppermute | solution.py:26
  32.4 3.2 %collective-permute-start.4 = (bf16[1,6,40,256]{3,2,1,0:T(8,128)(2,1)S(1)}, bf16[1,6,40,256]{3,2,1,0:T(8,128)(2,1)S(1)}, u32[]{:S(2)}, u32[]{:S(2)}) collective-permute-start(bf16[1,6,40,256]{3,2,1,0:T(8,128)(2,1)S(1)} %pad_maximum_fusion.1), channel_id=1, source_target_pairs={{0,64},{64,128},{128,192},{192,256},{256,320},{320,384},{384,448},... | collective-permute-start | bytes 368648 | tf_op jit(solution)/shard_map/ppermute | solution.py:26
  35.6 3.8 %collective-permute-start.5 = (bf16[1,6,40,256]{3,2,1,0:T(8,128)(2,1)S(1)}, bf16[1,6,40,256]{3,2,1,0:T(8,128)(2,1)S(1)}, u32[]{:S(2)}, u32[]{:S(2)}) collective-permute-start(bf16[1,6,40,256]{3,2,1,0:T(8,128)(2,1)S(1)} %pad_maximum_fusion.1), channel_id=1, source_target_pairs={{64,0},{128,64},{192,128},{256,192},{320,256},{384,320},{448,384},... | collective-permute-start | bytes 368648 | tf_op jit(solution)/shard_map/ppermute | solution.py:28
  45.3 1.8 multiply_reduce_fusion.1
  47.3 3.1 %collective-permute-start.6 = (bf16[1,4,4,256]{3,1,2,0:T(4,128)(2,1)S(1)}, bf16[1,4,4,256]{3,1,2,0:T(4,128)(2,1)S(1)}, u32[]{:S(2)}, u32[]{:S(2)}) collective-permute-start(bf16[1,4,4,256]{3,1,2,0:T(4,128)(2,1)S(1)} %get-tuple-element.77), channel_id=1, source_target_pairs={{0,1},{1,2},{2,3},{4,5},{5,6},{6,7},{8,9},{9,10},{10,11},{12,13},{... | collective-permute-start | bytes 24584 | tf_op jit(solution)/shard_map/ppermute | solution.py:26
  51.2 1.3 collective-permute-start.7
  52.6 3.0 %collective-permute-done.7 = bf16[1,4,4,256]{3,1,2,0:T(4,128)(2,1)S(1)} collective-permute-done((bf16[1,4,4,256]{3,1,2,0:T(4,128)(2,1)S(1)}, bf16[1,4,4,256]{3,1,2,0:T(4,128)(2,1)S(1)}, u32[]{:S(2)}, u32[]{:S(2)}) %collective-permute-start.7) | collective-permute-done | bytes 8224 | tf_op jit(solution)/shard_map/ppermute | solution.py:28
  55.7 13.5 %collective-permute-start.9 = (bf16[1,1,40,256]{3,1,2,0:T(2,128)(2,1)S(1)}, bf16[1,1,40,256]{3,1,2,0:T(2,128)(2,1)S(1)}, u32[]{:S(2)}, u32[]{:S(2)}) collective-permute-start(bf16[1,1,40,256]{3,1,2,0:T(2,128)(2,1)S(1)} %get-tuple-element.69), channel_id=1, source_target_pairs={{4,0},{8,4},{12,8},{16,12},{20,16},{24,20},{28,24},{32,28},{36,32}... | collective-permute-start | bytes 61448 | tf_op jit(solution)/shard_map/ppermute | solution.py:28
  69.2 1.9 collective-permute-start.8
  72.4 3.2 %collective-permute-start.10 = (bf16[1,6,40,256]{3,1,2,0:T(8,128)(2,1)S(1)}, bf16[1,6,40,256]{3,1,2,0:T(8,128)(2,1)S(1)}, u32[]{:S(2)}, u32[]{:S(2)}) collective-permute-start(bf16[1,6,40,256]{3,1,2,0:T(8,128)(2,1)S(1)} %pad_maximum_fusion), channel_id=1, source_target_pairs={{0,64},{64,128},{128,192},{192,256},{256,320},{320,384},{384,448},... | collective-permute-start | bytes 368648 | tf_op jit(solution)/shard_map/ppermute | solution.py:26
  75.7 3.6 %collective-permute-start.11 = (bf16[1,6,40,256]{3,1,2,0:T(8,128)(2,1)S(1)}, bf16[1,6,40,256]{3,1,2,0:T(8,128)(2,1)S(1)}, u32[]{:S(2)}, u32[]{:S(2)}) collective-permute-start(bf16[1,6,40,256]{3,1,2,0:T(8,128)(2,1)S(1)} %pad_maximum_fusion), channel_id=1, source_target_pairs={{64,0},{128,64},{192,128},{256,192},{320,256},{384,320},{448,384},... | collective-permute-start | bytes 368648 | tf_op jit(solution)/shard_map/ppermute | solution.py:28
  81.1 1.3 collective-permute-done.11
  85.3 1.8 multiply_reduce_fusion
  87.4 1.3 collective-permute-start.13
  88.7 4.0 %collective-permute-start.12 = (bf16[1,4,4,128]{3,2,1,0:T(4,128)(2,1)S(1)}, bf16[1,4,4,128]{3,2,1,0:T(4,128)(2,1)S(1)}, u32[]{:S(2)}, u32[]{:S(2)}) collective-permute-start(bf16[1,4,4,128]{3,2,1,0:T(4,128)(2,1)S(1)} %get-tuple-element.112), channel_id=1, source_target_pairs={{0,1},{1,2},{2,3},{4,5},{5,6},{6,7},{8,9},{9,10},{10,11},{12,13},{... | collective-permute-start | bytes 12296 | tf_op jit(solution)/shard_map/ppermute | solution.py:26
  93.9 11.9 %collective-permute-start.15 = (bf16[1,1,40,128]{3,2,1,0:T(8,128)(2,1)S(1)}, bf16[1,1,40,128]{3,2,1,0:T(8,128)(2,1)S(1)}, u32[]{:S(2)}, u32[]{:S(2)}) collective-permute-start(bf16[1,1,40,128]{3,2,1,0:T(8,128)(2,1)S(1)} %get-tuple-element.109), channel_id=1, source_target_pairs={{4,0},{8,4},{12,8},{16,12},{20,16},{24,20},{28,24},{32,28},{36,32}... | collective-permute-start | bytes 30728 | tf_op jit(solution)/shard_map/ppermute | solution.py:28
  105.8 1.9 collective-permute-start.14
  108.9 4.8 %collective-permute-start.16 = (bf16[1,6,40,128]{3,2,1,0:T(8,128)(2,1)S(1)}, bf16[1,6,40,128]{3,2,1,0:T(8,128)(2,1)S(1)}, u32[]{:S(2)}, u32[]{:S(2)}) collective-permute-start(bf16[1,6,40,128]{3,2,1,0:T(8,128)(2,1)S(1)} %pad_maximum_fusion.9), channel_id=1, source_target_pairs={{0,64},{64,128},{128,192},{192,256},{256,320},{320,384},{384,448},... | collective-permute-start | bytes 184328 | tf_op jit(solution)/shard_map/ppermute | solution.py:26
  113.8 1.9 collective-permute-start.17
  116.3 2.7 collective-permute-done.17
  122.2 3.2 %copy.104 = bf16[32,8,64,128]{3,2,1,0:T(8,128)(2,1)} copy(bf16[32,8,64,128]{3,1,2,0:T(8,128)(2,1)S(1)} %fusion) | data formatting | bytes 8388608
  125.5 15.7 %all-to-all-start = ((bf16[128,2,64,128]{3,2,1,0:T(8,128)(2,1)}), bf16[128,2,64,128]{3,2,1,0:T(8,128)(2,1)}, u32[]{:S(2)}, u32[]{:S(2)}) async-start(bf16[128,2,64,128]{3,2,1,0:T(8,128)(2,1)} %bitcast.192), calls=%async_computation | async-start | bytes 8388608 | tf_op jit(solution)/shard_map/all_to_all | solution.py:216
  143.4 96.9 %all-to-all-done = bf16[128,2,64,128]{3,2,1,0:T(8,128)(2,1)} async-done(((bf16[128,2,64,128]{3,2,1,0:T(8,128)(2,1)}), bf16[128,2,64,128]{3,2,1,0:T(8,128)(2,1)}, u32[]{:S(2)}, u32[]{:S(2)}) %all-to-all-start) | async-done | bytes 4194336 | tf_op jit(solution)/shard_map/all_to_all | solution.py:216
  240.3 16.6 %shard_map.127 = f32[256,128]{1,0:T(8,128)} custom-call(bf16[16384,128]{1,0:T(8,128)(2,1)} %bitcast.103.env_ref, bf16[128,1024]{1,0:T(8,128)(2,1)} %bitcast.214, bf16[1024,128]{1,0:T(8,128)(2,1)} %scatter.4.head_ref), custom_call_target="tpu_custom_call" | custom-call | tf_op jit(solution)/shard_map/pallas_call | solution.py:134
  256.9 9.6 %all-to-all-start.1 = ((f32[128,2,3]{2,1,0:T(2,128)}), f32[128,2,3]{2,1,0:T(2,128)S(1)}, u32[]{:S(2)}, u32[]{:S(2)}) async-start(f32[128,2,3]{2,1,0:T(2,128)} %bitcast.210), calls=%async_computation.1 | async-start | bytes 262144 | tf_op jit(solution)/shard_map/all_to_all | solution.py:226
  266.8 15.6 %all-to-all-done.1 = f32[128,2,3]{2,1,0:T(2,128)S(1)} async-done(((f32[128,2,3]{2,1,0:T(2,128)}), f32[128,2,3]{2,1,0:T(2,128)S(1)}, u32[]{:S(2)}, u32[]{:S(2)}) %all-to-all-start.1) | async-done | bytes 3104 | tf_op jit(solution)/shard_map/all_to_all | solution.py:226
  (202 shorter events, 25.9 us)
Async XLA Ops:
  0.0 87.1 %copy-start = (bf16[256,128]{1,0:T(8,128)(2,1)S(1)}, bf16[256,128]{1,0:T(8,128)(2,1)}, u32[]{:S(2)}) copy-start(bf16[256,128]{1,0:T(8,128)(2,1)} %param.21) | copy-start | bytes 196612
  0.0 17.0 %copy-start.1 = (bf16[1,4,32,256]{3,2,1,0:T(8,128)(2,1)S(1)}, bf16[1,4,32,256]{3,2,1,0:T(8,128)(2,1)}, u32[]{:S(2)}) copy-start(bf16[1,4,32,256]{3,2,1,0:T(8,128)(2,1)} %param.15) | copy-start | bytes 196612
  0.0 17.0 %copy-start.6 = (s32[1,1,1,32]{3,2,1,0:T(1,128)S(1)}, s32[1,1,1,32]{3,2,1,0:T(1,128)}, u32[]{:S(2)}) copy-start(s32[1,1,1,32]{3,2,1,0:T(1,128)} %param.25) | copy-start | bytes 388
  0.8 16.3 %collective-permute-start.1 = (bf16[1,4,4,256]{3,2,1,0:T(4,128)(2,1)S(1)}, bf16[1,4,4,256]{3,2,1,0:T(4,128)(2,1)S(1)}, u32[]{:S(2)}, u32[]{:S(2)}) collective-permute-start(bf16[1,4,4,256]{3,2,1,0:T(4,128)(2,1)S(1)} %get-tuple-element.81), channel_id=1, source_target_pairs={{1,0},{2,1},{3,2},{5,4},{6,5},{7,6},{9,8},{10,9},{11,10},{13,12},{... | collective-permute-start | bytes 24584 | tf_op jit(solution)/shard_map/ppermute | solution.py:28
  2.1 15.0 %collective-permute-start = (bf16[1,4,4,256]{3,2,1,0:T(4,128)(2,1)S(1)}, bf16[1,4,4,256]{3,2,1,0:T(4,128)(2,1)S(1)}, u32[]{:S(2)}, u32[]{:S(2)}) collective-permute-start(bf16[1,4,4,256]{3,2,1,0:T(4,128)(2,1)S(1)} %get-tuple-element.80), channel_id=1, source_target_pairs={{0,1},{1,2},{2,3},{4,5},{5,6},{6,7},{8,9},{9,10},{10,11},{12,13},{... | collective-permute-start | bytes 24584 | tf_op jit(solution)/shard_map/ppermute | solution.py:26
  17.2 10.0 %collective-permute-start.3 = (bf16[1,1,40,256]{3,2,1,0:T(8,128)(2,1)S(1)}, bf16[1,1,40,256]{3,2,1,0:T(8,128)(2,1)S(1)}, u32[]{:S(2)}, u32[]{:S(2)}) collective-permute-start(bf16[1,1,40,256]{3,2,1,0:T(8,128)(2,1)S(1)} %get-tuple-element.73), channel_id=1, source_target_pairs={{4,0},{8,4},{12,8},{16,12},{20,16},{24,20},{28,24},{32,28},{36,32}... | collective-permute-start | bytes 61448 | tf_op jit(solution)/shard_map/ppermute | solution.py:28
  25.0 7.3 %collective-permute-start.2 = (bf16[1,1,40,256]{3,2,1,0:T(8,128)(2,1)S(1)}, bf16[1,1,40,256]{3,2,1,0:T(8,128)(2,1)S(1)}, u32[]{:S(2)}, u32[]{:S(2)}) collective-permute-start(bf16[1,1,40,256]{3,2,1,0:T(8,128)(2,1)S(1)} %get-tuple-element.72), channel_id=1, source_target_pairs={{0,4},{4,8},{8,12},{12,16},{16,20},{20,24},{24,28},{28,32},{32,36}... | collective-permute-start | bytes 61448 | tf_op jit(solution)/shard_map/ppermute | solution.py:26
  32.4 7.7 %collective-permute-start.4 = (bf16[1,6,40,256]{3,2,1,0:T(8,128)(2,1)S(1)}, bf16[1,6,40,256]{3,2,1,0:T(8,128)(2,1)S(1)}, u32[]{:S(2)}, u32[]{:S(2)}) collective-permute-start(bf16[1,6,40,256]{3,2,1,0:T(8,128)(2,1)S(1)} %pad_maximum_fusion.1), channel_id=1, source_target_pairs={{0,64},{64,128},{128,192},{192,256},{256,320},{320,384},{384,448},... | collective-permute-start | bytes 368648 | tf_op jit(solution)/shard_map/ppermute | solution.py:26
  35.6 5.7 %collective-permute-start.5 = (bf16[1,6,40,256]{3,2,1,0:T(8,128)(2,1)S(1)}, bf16[1,6,40,256]{3,2,1,0:T(8,128)(2,1)S(1)}, u32[]{:S(2)}, u32[]{:S(2)}) collective-permute-start(bf16[1,6,40,256]{3,2,1,0:T(8,128)(2,1)S(1)} %pad_maximum_fusion.1), channel_id=1, source_target_pairs={{64,0},{128,64},{192,128},{256,192},{320,256},{384,320},{448,384},... | collective-permute-start | bytes 368648 | tf_op jit(solution)/shard_map/ppermute | solution.py:28
  44.0 1.3 copy-start.5
  45.3 5.1 %copy-start.3 = (s32[1,1,1,32,1]{3,4,2,1,0:T(1,128)S(1)}, s32[1,1,1,32,1]{3,4,2,1,0:T(1,128)}, u32[]{:S(2)}) copy-start(s32[1,1,1,32,1]{3,4,2,1,0:T(1,128)} %param.26) | copy-start | bytes 388
  47.3 5.3 %collective-permute-start.6 = (bf16[1,4,4,256]{3,1,2,0:T(4,128)(2,1)S(1)}, bf16[1,4,4,256]{3,1,2,0:T(4,128)(2,1)S(1)}, u32[]{:S(2)}, u32[]{:S(2)}) collective-permute-start(bf16[1,4,4,256]{3,1,2,0:T(4,128)(2,1)S(1)} %get-tuple-element.77), channel_id=1, source_target_pairs={{0,1},{1,2},{2,3},{4,5},{5,6},{6,7},{8,9},{9,10},{10,11},{12,13},{... | collective-permute-start | bytes 24584 | tf_op jit(solution)/shard_map/ppermute | solution.py:26
  51.2 4.4 %collective-permute-start.7 = (bf16[1,4,4,256]{3,1,2,0:T(4,128)(2,1)S(1)}, bf16[1,4,4,256]{3,1,2,0:T(4,128)(2,1)S(1)}, u32[]{:S(2)}, u32[]{:S(2)}) collective-permute-start(bf16[1,4,4,256]{3,1,2,0:T(4,128)(2,1)S(1)} %get-tuple-element.76), channel_id=1, source_target_pairs={{1,0},{2,1},{3,2},{5,4},{6,5},{7,6},{9,8},{10,9},{11,10},{13,12},{... | collective-permute-start | bytes 24584 | tf_op jit(solution)/shard_map/ppermute | solution.py:28
  55.7 15.5 %collective-permute-start.9 = (bf16[1,1,40,256]{3,1,2,0:T(2,128)(2,1)S(1)}, bf16[1,1,40,256]{3,1,2,0:T(2,128)(2,1)S(1)}, u32[]{:S(2)}, u32[]{:S(2)}) collective-permute-start(bf16[1,1,40,256]{3,1,2,0:T(2,128)(2,1)S(1)} %get-tuple-element.69), channel_id=1, source_target_pairs={{4,0},{8,4},{12,8},{16,12},{20,16},{24,20},{28,24},{32,28},{36,32}... | collective-permute-start | bytes 61448 | tf_op jit(solution)/shard_map/ppermute | solution.py:28
  69.2 3.1 %collective-permute-start.8 = (bf16[1,1,40,256]{3,1,2,0:T(2,128)(2,1)S(1)}, bf16[1,1,40,256]{3,1,2,0:T(2,128)(2,1)S(1)}, u32[]{:S(2)}, u32[]{:S(2)}) collective-permute-start(bf16[1,1,40,256]{3,1,2,0:T(2,128)(2,1)S(1)} %get-tuple-element.68), channel_id=1, source_target_pairs={{0,4},{4,8},{8,12},{12,16},{16,20},{20,24},{24,28},{28,32},{32,36}... | collective-permute-start | bytes 61448 | tf_op jit(solution)/shard_map/ppermute | solution.py:26
  72.4 7.7 %collective-permute-start.10 = (bf16[1,6,40,256]{3,1,2,0:T(8,128)(2,1)S(1)}, bf16[1,6,40,256]{3,1,2,0:T(8,128)(2,1)S(1)}, u32[]{:S(2)}, u32[]{:S(2)}) collective-permute-start(bf16[1,6,40,256]{3,1,2,0:T(8,128)(2,1)S(1)} %pad_maximum_fusion), channel_id=1, source_target_pairs={{0,64},{64,128},{128,192},{192,256},{256,320},{320,384},{384,448},... | collective-permute-start | bytes 368648 | tf_op jit(solution)/shard_map/ppermute | solution.py:26
  75.7 6.7 %collective-permute-start.11 = (bf16[1,6,40,256]{3,1,2,0:T(8,128)(2,1)S(1)}, bf16[1,6,40,256]{3,1,2,0:T(8,128)(2,1)S(1)}, u32[]{:S(2)}, u32[]{:S(2)}) collective-permute-start(bf16[1,6,40,256]{3,1,2,0:T(8,128)(2,1)S(1)} %pad_maximum_fusion), channel_id=1, source_target_pairs={{64,0},{128,64},{192,128},{256,192},{320,256},{384,320},{448,384},... | collective-permute-start | bytes 368648 | tf_op jit(solution)/shard_map/ppermute | solution.py:28
  87.4 6.5 %collective-permute-start.13 = (bf16[1,4,4,128]{3,2,1,0:T(4,128)(2,1)S(1)}, bf16[1,4,4,128]{3,2,1,0:T(4,128)(2,1)S(1)}, u32[]{:S(2)}, u32[]{:S(2)}) collective-permute-start(bf16[1,4,4,128]{3,2,1,0:T(4,128)(2,1)S(1)} %get-tuple-element.113), channel_id=1, source_target_pairs={{1,0},{2,1},{3,2},{5,4},{6,5},{7,6},{9,8},{10,9},{11,10},{13,12},{... | collective-permute-start | bytes 12296 | tf_op jit(solution)/shard_map/ppermute | solution.py:28
  88.7 5.2 %collective-permute-start.12 = (bf16[1,4,4,128]{3,2,1,0:T(4,128)(2,1)S(1)}, bf16[1,4,4,128]{3,2,1,0:T(4,128)(2,1)S(1)}, u32[]{:S(2)}, u32[]{:S(2)}) collective-permute-start(bf16[1,4,4,128]{3,2,1,0:T(4,128)(2,1)S(1)} %get-tuple-element.112), channel_id=1, source_target_pairs={{0,1},{1,2},{2,3},{4,5},{5,6},{6,7},{8,9},{9,10},{10,11},{12,13},{... | collective-permute-start | bytes 12296 | tf_op jit(solution)/shard_map/ppermute | solution.py:26
  93.9 13.9 %collective-permute-start.15 = (bf16[1,1,40,128]{3,2,1,0:T(8,128)(2,1)S(1)}, bf16[1,1,40,128]{3,2,1,0:T(8,128)(2,1)S(1)}, u32[]{:S(2)}, u32[]{:S(2)}) collective-permute-start(bf16[1,1,40,128]{3,2,1,0:T(8,128)(2,1)S(1)} %get-tuple-element.109), channel_id=1, source_target_pairs={{4,0},{8,4},{12,8},{16,12},{20,16},{24,20},{28,24},{32,28},{36,32}... | collective-permute-start | bytes 30728 | tf_op jit(solution)/shard_map/ppermute | solution.py:28
  105.8 3.1 %collective-permute-start.14 = (bf16[1,1,40,128]{3,2,1,0:T(8,128)(2,1)S(1)}, bf16[1,1,40,128]{3,2,1,0:T(8,128)(2,1)S(1)}, u32[]{:S(2)}, u32[]{:S(2)}) collective-permute-start(bf16[1,1,40,128]{3,2,1,0:T(8,128)(2,1)S(1)} %get-tuple-element.108), channel_id=1, source_target_pairs={{0,4},{4,8},{8,12},{12,16},{16,20},{20,24},{24,28},{28,32},{32,36}... | collective-permute-start | bytes 30728 | tf_op jit(solution)/shard_map/ppermute | solution.py:26
  108.9 6.9 %collective-permute-start.16 = (bf16[1,6,40,128]{3,2,1,0:T(8,128)(2,1)S(1)}, bf16[1,6,40,128]{3,2,1,0:T(8,128)(2,1)S(1)}, u32[]{:S(2)}, u32[]{:S(2)}) collective-permute-start(bf16[1,6,40,128]{3,2,1,0:T(8,128)(2,1)S(1)} %pad_maximum_fusion.9), channel_id=1, source_target_pairs={{0,64},{64,128},{128,192},{192,256},{256,320},{320,384},{384,448},... | collective-permute-start | bytes 184328 | tf_op jit(solution)/shard_map/ppermute | solution.py:26
  113.8 5.2 %collective-permute-start.17 = (bf16[1,6,40,128]{3,2,1,0:T(8,128)(2,1)S(1)}, bf16[1,6,40,128]{3,2,1,0:T(8,128)(2,1)S(1)}, u32[]{:S(2)}, u32[]{:S(2)}) collective-permute-start(bf16[1,6,40,128]{3,2,1,0:T(8,128)(2,1)S(1)} %pad_maximum_fusion.9), channel_id=1, source_target_pairs={{64,0},{128,64},{192,128},{256,192},{320,256},{384,320},{448,384},... | collective-permute-start | bytes 184328 | tf_op jit(solution)/shard_map/ppermute | solution.py:28
  125.5 15.7 %copy-start.2 = (bf16[1,3,1024]{2,1,0:T(4,128)(2,1)S(1)}, bf16[1,3,1024]{2,1,0:T(4,128)(2,1)}, u32[]{:S(2)}) copy-start(bf16[1,3,1024]{2,1,0:T(4,128)(2,1)} %param.24) | copy-start | bytes 18436
  125.5 114.8 %all-to-all-start = ((bf16[128,2,64,128]{3,2,1,0:T(8,128)(2,1)}), bf16[128,2,64,128]{3,2,1,0:T(8,128)(2,1)}, u32[]{:S(2)}, u32[]{:S(2)}) async-start(bf16[128,2,64,128]{3,2,1,0:T(8,128)(2,1)} %bitcast.192), calls=%async_computation | async-start | bytes 8388608 | tf_op jit(solution)/shard_map/all_to_all | solution.py:216
  240.3 26.2 %copy-start.4 = (bf16[3,256]{1,0:T(4,128)(2,1)S(1)}, bf16[3,256]{1,0:T(4,128)(2,1)}, u32[]{:S(2)}) copy-start(bf16[3,256]{1,0:T(4,128)(2,1)} %param.22) | copy-start | bytes 4612
  256.9 25.5 %all-to-all-start.1 = ((f32[128,2,3]{2,1,0:T(2,128)}), f32[128,2,3]{2,1,0:T(2,128)S(1)}, u32[]{:S(2)}, u32[]{:S(2)}) async-start(f32[128,2,3]{2,1,0:T(2,128)} %bitcast.210), calls=%async_computation.1 | async-start | bytes 262144 | tf_op jit(solution)/shard_map/all_to_all | solution.py:226
